TPU v7x, 768 devices: a whole 4x8x12 slice. The times are simulated.
768 devices in a mesh: fsdp: 192 (over y, z, core), ctx: 4 (over x).
Axes of the slice: x: 4, y: 8, z: 12, core: 2. Of those that a mesh axis runs over, the one named last changes fastest.
Arguments:
- queries: bfloat16 [79872, 3072], P(('fsdp', 'ctx')), may hold values from -6 to 6
- keys: bfloat16 [79872, 3072], P(('fsdp', 'ctx')), may hold values from -6 to 6
- values: bfloat16 [79872, 3072], P(('fsdp', 'ctx')), may hold values from -6 to 6
- norm_gain: float32 [3072], replicated, may hold values from 0.1 to 1.9
- out_weight: bfloat16 [3072, 3072], P('fsdp', 'ctx'), may hold values from -0.109375 to 0.109375
Outputs:
- layer_out: bfloat16 [79872, 3072], P('fsdp', 'ctx')
All inputs are finite; a program needn't handle non-finite values.
Results may differ from a plain program's by a relative error of at most 0.0061.
Values may be sent and summed in bfloat16 or wider, within the bound.
No kernel may reach another device: no remote copies, remote signals or barrier semaphores. Data moves between devices by JAX's collectives and lax.ppermute only.
A program may use at most 32 MiB of HBM per device.

v0:
```python
import jax
import jax.numpy as jnp
from jax import lax
from jax.sharding import PartitionSpec as P

HEADS = 32
HEAD_DIM = 96


def on_device(queries, keys, values, norm_gain, out_weight):
    tok_rows = queries.shape[0]
    q_heads = queries.reshape(tok_rows, HEADS, HEAD_DIM)
    k_heads = keys.reshape(tok_rows, HEADS, HEAD_DIM)
    v_heads = values.reshape(tok_rows, HEADS, HEAD_DIM)
    scores = jnp.einsum("thd,shd->hts", q_heads, k_heads, preferred_element_type=jnp.float32)
    causal = jnp.arange(tok_rows)[:, None] >= jnp.arange(tok_rows)[None, :]
    scores = jnp.where(causal, scores, 0.0).astype(jnp.bfloat16)
    intra = jnp.einsum("hts,shd->thd", scores, v_heads, preferred_element_type=jnp.float32)
    local_state = jnp.einsum("shd,she->hde", k_heads, v_heads, preferred_element_type=jnp.float32)
    flat_state = local_state.reshape(HEADS, HEAD_DIM * HEAD_DIM).astype(jnp.bfloat16)
    every_state = lax.all_gather(flat_state[None], "ctx", axis=0, tiled=True)
    position = lax.axis_index("ctx")
    earlier = (jnp.arange(every_state.shape[0]) < position)[:, None, None]
    prefix_flat = jnp.sum(jnp.where(earlier, every_state.astype(jnp.float32), 0.0), axis=0)
    prefix_state = prefix_flat.reshape(HEADS, HEAD_DIM, HEAD_DIM).astype(jnp.bfloat16)
    inter = jnp.einsum("thd,hde->the", q_heads, prefix_state, preferred_element_type=jnp.float32)
    attn = (intra + inter).reshape(tok_rows, HEADS * HEAD_DIM)
    mean_sq = jnp.mean(attn * attn, axis=-1, keepdims=True)
    normed = (attn * lax.rsqrt(mean_sq + 1e-05) * norm_gain).astype(jnp.bfloat16)
    weight_block = lax.all_gather(out_weight, "fsdp", axis=0, tiled=True)
    result = jnp.dot(
        lax.all_gather(normed, "ctx", axis=0, tiled=True),
        weight_block,
        preferred_element_type=jnp.float32,
    )
    return result.astype(jnp.bfloat16)


def solution(mesh):
    placed = (
        P(("fsdp", "ctx"), None),
        P(("fsdp", "ctx"), None),
        P(("fsdp", "ctx"), None),
        P(),
        P("fsdp", "ctx"),
    )
    return jax.shard_map(
        on_device, mesh=mesh, in_specs=placed, out_specs=P("fsdp", "ctx"), check_vma=False
    )
```

profile of v0, /device:TPU:6, one launch (start us, length us, event | category | flops | bytes accessed | tf_op | source)
XLA Modules:
  0.0 252.4 jit_solution(3749592660355717773)
XLA Ops:
  6.5 0.0 copy-start.1
  6.5 0.0 all-gather.4.cloned.1.call-start
  6.5 1.5 copy.25
  8.1 0.0 copy-done.1
  8.1 0.4 copy.26
  8.5 0.0 copy-start.2
  8.5 0.7 convolution_convert_fusion
  9.1 1.9 convert_element_type.33
  11.0 0.0 all-gather.4.cloned.1.call-update
  11.0 0.0 all-gather.6.cloned.1.call-start
  11.1 0.0 copy-done.2
  11.1 0.4 copy.24
  11.5 2.3 fusion
  13.8 0.0 copy-start
  13.8 43.2 %all-gather.4.cloned.1.call-done = bf16[4,32,9216]{2,1,0:T(8,128)(2,1)} async-done(((bf16[1,32,9216]{2,1,0:T(8,128)(2,1)}), bf16[4,32,9216]{2,1,0:T(8,128)(2,1)}) %all-gather.4.cloned.1.call-update) | async-done | bytes 2359312 | tf_op jit(solution)/shard_map/all_gather | solution.py:21
  57.1 3.2 %select_reduce_fusion = bf16[32,9216]{1,0:T(8,128)(2,1)} fusion(bf16[4,32,9216]{2,1,0:T(8,128)(2,1)} %all-gather.4.cloned.1.call-done, pred[4]{0:T(512)(128)(4,1)S(1)} %iota_compare_fusion.1), kind=kLoop, calls=%fused_computation | loop fusion | flops 3244032 | bytes 2949124 | tf_op jit(solution)/shard_map/reduce_sum | solution.py:24
  60.3 1.8 convert_element_type.36
  62.1 0.0 copy-done
  62.1 1.7 multiply_reduce_fusion
  63.9 0.0 copy-start.3
  63.9 1.9 copy.22
  65.8 0.0 copy-done.3
  65.8 1.0 multiply_convert_fusion
  66.8 0.0 all-gather.6.cloned.1.call-update
  66.8 0.0 all-gather.8.cloned.1.call-start
  66.9 0.7 all-gather.8.cloned.1.call-update
  67.6 42.3 %all-gather.6.cloned.1.call-done = bf16[416,3072]{1,0:T(8,128)(2,1)} async-done(((bf16[104,3072]{1,0:T(8,128)(2,1)}), bf16[416,3072]{1,0:T(8,128)(2,1)}) %all-gather.6.cloned.1.call-update) | async-done | bytes 2555920 | tf_op jit(solution)/shard_map/all_gather | solution.py:32
  109.9 130.0 %all-gather.8.cloned.1.call-done = bf16[3072,768]{1,0:T(8,128)(2,1)} async-done(((bf16[16,768]{1,0:T(8,128)(2,1)}), bf16[3072,768]{1,0:T(8,128)(2,1)}) %all-gather.8.cloned.1.call-update) | async-done | bytes 4718608 | tf_op jit(solution)/shard_map/all_gather | solution.py:30
  239.8 6.1 %convolution_convert_fusion.1 = bf16[416,768]{1,0:T(8,128)(2,1)} fusion(bf16[416,3072]{1,0:T(8,128)(2,1)} %all-gather.6.cloned.1.call-done, bf16[3072,768]{1,0:T(8,128)(2,1)} %all-gather.8.cloned.1.call-done), kind=kOutput, calls=%fused_computation.5 | convolution fusion | flops 1963253760 | bytes 7913472 | tf_op jit(solution)/shard_map/dot_general | solution.py:31
  (3 shorter events, 0.0 us)
Async XLA Ops:
  6.5 1.5 copy-start.1
  6.5 50.5 %all-gather.4.cloned.1.call-start = ((), (), s32[]{:S(2)}) async-start(), calls=%async_computation | async-start | bytes 2949120 | tf_op jit(solution)/shard_map/all_gather | solution.py:21
  8.5 2.6 %copy-start.2 = (bf16[104,3072]{1,0:T(8,128)(2,1)S(1)}, bf16[104,3072]{1,0:T(8,128)(2,1)}, u32[]{:S(2)}) copy-start(bf16[104,3072]{1,0:T(8,128)(2,1)} %param.5) | copy-start | bytes 1916932
  11.0 98.8 %all-gather.6.cloned.1.call-start = ((), (), s32[]{:S(2)}) async-start(), calls=%async_computation.1 | async-start | bytes 3194880 | tf_op jit(solution)/shard_map/all_gather | solution.py:32
  13.8 48.3 %copy-start = (f32[32,104,96]{1,2,0:T(8,128)S(1)}, f32[32,104,96]{1,2,0:T(8,128)}, u32[]{:S(2)}) copy-start(f32[32,104,96]{1,2,0:T(8,128)} %fusion) | copy-start | bytes 3833860
  63.9 1.9 copy-start.3
  66.8 173.0 %all-gather.8.cloned.1.call-start = ((), (), s32[]{:S(2)}) async-start(), calls=%async_computation.2 | async-start | bytes 4743168 | tf_op jit(solution)/shard_map/all_gather | solution.py:30
Sparse Core Ops, SparseCore 0:
  11.1 45.8 all-gather.3
  67.0 42.8 all-gather.5
  113.6 126.1 all-gather.7
where the time goes:
time: 254 us; the launch traced here: 252 us
  waiting for transfers between devices  216 us (85%)
  between operations  13.2 us (5%)
  matrix products  10.8 us (4%)
  local copies, waits for them, and re-layouts  7.85 us (3%)
  other arithmetic  4.27 us (2%)
    all_gather x1, waiting for transfers between devices, on_device(): weight_block = lax.all_gather(out_weight, 'fsdp', axis=0, tiled=True)  130 us
    all_gather x1, waiting for transfers between devices, on_device(): every_state = lax.all_gather(flat_state[None], 'ctx', axis=0, tiled=True)  43.2 us
    all_gather x1, waiting for transfers between devices, on_device(): lax.all_gather(normed, 'ctx', axis=0, tiled=True)  42.3 us
    dot_general x1, matrix products, on_device(): jnp.dot(lax.all_gather(normed, 'ctx', axis=0, tiled=True), weight_block,...  6.09 us
  transfers between devices with their start and end apart: 3, of which 3 were waited for; matrix products, arithmetic and copies ran while one was open for 1% of the time, Pallas kernels for 0%

commit v1 on v0

v1 whole, which is shorter than its diff:
```python
import jax
import jax.numpy as jnp
import numpy as np
from jax import lax
from jax.sharding import Mesh
from jax.sharding import PartitionSpec as P

HEADS = 32
HEAD_DIM = 96


def make_on_device(n_ctx, n_core):
    def on_device(queries, keys, values, norm_gain, out_weight):
        w_half = lax.all_gather(out_weight, "chips", axis=0, tiled=True)
        w_both = lax.all_gather(w_half, "core", axis=0, tiled=False)
        rows, cols = out_weight.shape
        weight_block = (
            w_both.reshape(n_core, -1, rows, cols).transpose(1, 0, 2, 3).reshape(-1, cols)
        )

        tok_rows = queries.shape[0]
        q_heads = queries.reshape(tok_rows, HEADS, HEAD_DIM)
        k_heads = keys.reshape(tok_rows, HEADS, HEAD_DIM)
        v_heads = values.reshape(tok_rows, HEADS, HEAD_DIM)
        local_state = jnp.einsum("shd,she->hde", k_heads, v_heads, preferred_element_type=jnp.float32)
        state_bf = local_state.astype(jnp.bfloat16)
        prefix_f32 = jnp.zeros(local_state.shape, jnp.float32)
        for shift in range(1, n_ctx):
            pairs = [(i, i + shift) for i in range(n_ctx - shift)]
            prefix_f32 = prefix_f32 + lax.ppermute(state_bf, "ctx", pairs).astype(jnp.float32)
        prefix_state = prefix_f32.astype(jnp.bfloat16)

        scores = jnp.einsum("thd,shd->hts", q_heads, k_heads, preferred_element_type=jnp.float32)
        causal = jnp.arange(tok_rows)[:, None] >= jnp.arange(tok_rows)[None, :]
        scores = jnp.where(causal, scores, 0.0).astype(jnp.bfloat16)
        intra = jnp.einsum("hts,shd->thd", scores, v_heads, preferred_element_type=jnp.float32)
        inter = jnp.einsum("thd,hde->the", q_heads, prefix_state, preferred_element_type=jnp.float32)
        attn = (intra + inter).reshape(tok_rows, HEADS * HEAD_DIM)
        mean_sq = jnp.mean(attn * attn, axis=-1, keepdims=True)
        normed = (attn * lax.rsqrt(mean_sq + 1e-05) * norm_gain).astype(jnp.bfloat16)

        outs = [jnp.dot(normed, weight_block, preferred_element_type=jnp.float32)]
        for shift in range(1, n_ctx):
            pairs = [(i, (i - shift) % n_ctx) for i in range(n_ctx)]
            got = lax.ppermute(normed, "ctx", pairs)
            outs.append(jnp.dot(got, weight_block, preferred_element_type=jnp.float32))
        stacked = jnp.concatenate(outs + outs, axis=0).astype(jnp.bfloat16)
        position = lax.axis_index("ctx")
        return lax.dynamic_slice_in_dim(stacked, (n_ctx - position) * tok_rows, n_ctx * tok_rows, axis=0)

    return on_device


def solution(mesh):
    n_fsdp, n_ctx = mesh.devices.shape
    n_core = 2
    split = Mesh(mesh.devices.reshape(n_fsdp // n_core, n_core, n_ctx), ("chips", "core", "ctx"))
    rows = ("chips", "core", "ctx")
    placed = (
        P(rows, None),
        P(rows, None),
        P(rows, None),
        P(),
        P(("chips", "core"), "ctx"),
    )
    return jax.shard_map(
        make_on_device(n_ctx, n_core),
        mesh=split,
        in_specs=placed,
        out_specs=P(("chips", "core"), "ctx"),
        check_vma=False,
    )
```

time: 254 us -> 233 us (0.917)
  waiting for transfers between devices: 216 us -> 181 us
  starting transfers between devices: 0.09 us -> 14 us
  other arithmetic: 4.27 us -> 0.68 us
    all_gather x3 -> x2, waiting for transfers between devices: 215 us -> 134 us  [the longest x1 134 us: on_device(): w_half = lax.all_gather(out_weight, 'chips', axis=0, tiled=True)]
    ppermute x0 -> x6, waiting for transfers between devices: none -> 46.4 us  [the longest x3 25 us: on_device(): lax.ppermute(state_bf, 'ctx', pairs).astype(jnp.float32)]
    ppermute x0 -> x6, starting transfers between devices: none -> 14 us  [the longest x3 10.1 us: on_device(): got = lax.ppermute(normed, 'ctx', pairs)]
    convert_element_type x2 -> x0, local copies, waits for them, and re-layouts: 3.68 us -> none  [the longest x1 1.87 us: on_device(): local_state.reshape(HEADS, HEAD_DIM * HEAD_DIM).astype(jnp.bfloat16)]
    reduce_sum x1 -> x0, other arithmetic: 3.22 us -> none  [on_device(): jnp.sum(jnp.where(earlier, every_state.astype(jnp.float32), 0.0), axis=0)]
    transpose x0 -> x1, local copies, waits for them, and re-layouts: none -> 2.91 us  [on_device(): w_both.reshape(n_core, -1, rows, cols).transpose(1, 0, 2, 3)]
    dot_general x1 -> x4, matrix products: 6.09 us -> 6.68 us  [the longest x3 5.85 us: on_device(): outs.append(jnp.dot(got, weight_block, preferred_element_type=jnp.float32))]
  transfers between devices with their start and end apart: 3 -> 8, of which waited for: 3 -> 3; matrix products, arithmetic and copies ran while one was open for 1% -> 8% of each run, Pallas kernels for 0% -> 0%
where the time goes in v1:
time: 233 us; the launch traced here: 230 us
  waiting for transfers between devices  181 us (78%)
  starting transfers between devices  14 us (6%)
  between operations  13.6 us (6%)
  matrix products  13.2 us (6%)
  local copies, waits for them, and re-layouts  7.25 us (3%)
    all_gather x1, waiting for transfers between devices, on_device(): w_half = lax.all_gather(out_weight, 'chips', axis=0, tiled=True)  134 us
    ppermute x3, waiting for transfers between devices, on_device(): lax.ppermute(state_bf, 'ctx', pairs).astype(jnp.float32)  25 us
    ppermute x3, waiting for transfers between devices, on_device(): got = lax.ppermute(normed, 'ctx', pairs)  21.5 us
    ppermute x3, starting transfers between devices, on_device(): got = lax.ppermute(normed, 'ctx', pairs)  10.1 us
    dot_general x3, matrix products, on_device(): outs.append(jnp.dot(got, weight_block, preferred_element_type=jnp.float32))  5.85 us
  transfers between devices with their start and end apart: 8, of which 3 were waited for; matrix products, arithmetic and copies ran while one was open for 8% of the time, Pallas kernels for 0%

profile of v1, /device:TPU:6, one launch (start us, length us, event | category | flops | bytes accessed | tf_op | source)
XLA Modules:
  0.0 230.1 jit_solution(8674924715262267722)
XLA Ops:
  6.5 0.7 all-gather.4.cloned.1.call-update
  7.3 0.0 all-gather.6.cloned.1.call-start
  7.3 134.1 %all-gather.4.cloned.1.call-done = bf16[1536,768]{1,0:T(8,128)(2,1)} async-done(((bf16[16,768]{1,0:T(8,128)(2,1)}), bf16[1536,768]{1,0:T(8,128)(2,1)}) %all-gather.4.cloned.1.call-update) | async-done | bytes 2359312 | tf_op jit(solution)/shard_map/all_gather | solution.py:14
  141.4 0.0 all-gather.6.cloned.1.call-update
  141.5 0.4 copy.35
  141.8 0.7 copy-done.1
  142.5 0.4 copy.36
  142.9 1.6 convolution_convert_fusion
  144.5 1.3 collective-permute-start.2
  145.8 1.3 collective-permute-start.1
  147.1 1.3 collective-permute-start
  148.4 0.1 mul.38
  148.5 1.5 copy.34
  149.9 2.4 %fusion = f32[32,104,96]{1,2,0:T(8,128)} fusion(bf16[104,32,96]{0,2,1:T(8,128)(2,1)S(1)} %bitcast.37, bf16[104,32,96]{0,2,1:T(8,128)(2,1)S(1)} %bitcast.32, bf16[104,32,96]{0,2,1:T(8,128)(2,1)S(1)} %bitcast.35, pred[104,104]{1,0:T(8,128)(4,1)S(1)} %iota_compare_fusion), kind=kOutput, calls=%fused_computation.6 | convolution fusion | flops 133599232 | bytes 3205696 | tf_op jit(solution)/shard_map/hts,shd->thd/dot_general | solution.py:36
  152.4 24.9 %collective-permute-done.2 = bf16[32,96,96]{2,1,0:T(8,128)(2,1)S(1)} collective-permute-done((bf16[32,96,96]{2,1,0:T(8,128)(2,1)}, bf16[32,96,96]{2,1,0:T(8,128)(2,1)S(1)}, u32[]{:S(2)}, u32[]{:S(2)}) %collective-permute-start.2) | collective-permute-done | bytes 589856 | tf_op jit(solution)/shard_map/ppermute | solution.py:30
  177.3 0.0 collective-permute-done.1
  177.3 2.5 %multiply_reduce_fusion = (f32[104]{0:T(128)S(1)}, f32[104,32,96]{0,2,1:T(8,128)S(1)}) fusion(bf16[104,32,96]{0,2,1:T(8,128)(2,1)S(1)} %bitcast.33, bf16[32,96,96]{2,1,0:T(8,128)(2,1)S(1)} %collective-permute-done.2, bf16[32,96,96]{2,1,0:T(8,128)(2,1)} %collective-permute-done.1, bf16[32,96,96]{2,1,0:T(8,128)(2,1)} %collective-permute-done, ...), kind=kOutput, calls=%fused_computation.3 | convolution fusion | flops 64069528 | bytes 4964768 | tf_op jit(solution)/shard_map/thd,hde->the/dot_general | solution.py:37
  179.8 0.5 copy.32
  180.3 0.2 multiply_convert_fusion.1
  180.5 2.9 %collective-permute-start.5 = (bf16[104,3072]{1,0:T(8,128)(2,1)S(1)}, bf16[104,3072]{1,0:T(8,128)(2,1)}, u32[]{:S(2)}, u32[]{:S(2)}) collective-permute-start(bf16[104,3072]{1,0:T(8,128)(2,1)S(1)} %multiply_convert_fusion.1), channel_id=1, source_target_pairs={{0,1},{1,2},{2,3},{3,0},{4,5},{5,6},{6,7},{7,4},{8,9},{9,10},{10,1... | collective-permute-start | bytes 1916936 | tf_op jit(solution)/shard_map/ppermute | solution.py:45
  183.5 5.2 %collective-permute-start.4 = (bf16[104,3072]{1,0:T(8,128)(2,1)S(1)}, bf16[104,3072]{1,0:T(8,128)(2,1)}, u32[]{:S(2)}, u32[]{:S(2)}) collective-permute-start(bf16[104,3072]{1,0:T(8,128)(2,1)S(1)} %multiply_convert_fusion.1), channel_id=1, source_target_pairs={{0,2},{1,3},{2,0},{3,1},{4,6},{5,7},{6,4},{7,5},{8,10},{9,11},{10,... | collective-permute-start | bytes 1916936 | tf_op jit(solution)/shard_map/ppermute | solution.py:45
  188.7 1.9 collective-permute-start.3
  190.6 0.5 multiply_convert_fusion
  191.1 0.0 all-gather.6.cloned.1.call-done
  191.2 2.9 %copy.31 = bf16[96,2,16,768]{3,2,1,0:T(8,128)(2,1)S(1)} copy(bf16[96,2,16,768]{3,2,0,1:T(8,128)(2,1)} %bitcast.38) | data formatting | bytes 9437184 | tf_op jit(solution)/shard_map/transpose | solution.py:18
  194.1 0.8 constant_dynamic-update-slice_fusion.7
  194.9 21.5 %collective-permute-done.3 = bf16[104,3072]{1,0:T(8,128)(2,1)} collective-permute-done((bf16[104,3072]{1,0:T(8,128)(2,1)S(1)}, bf16[104,3072]{1,0:T(8,128)(2,1)}, u32[]{:S(2)}, u32[]{:S(2)}) %collective-permute-start.3) | collective-permute-done | bytes 639008 | tf_op jit(solution)/shard_map/ppermute | solution.py:45
  216.4 1.9 constant_dynamic-update-slice_fusion.6
  218.3 1.9 constant_dynamic-update-slice_fusion.5
  220.3 0.0 collective-permute-done.5
  220.3 1.9 constant_dynamic-update-slice_fusion.4
  222.4 0.9 constant_dynamic-slice_fusion
  (14 shorter events, 0.1 us)
Async XLA Ops:
  6.5 134.9 %copy-start = (bf16[104,3072]{1,0:T(8,128)(2,1)S(1)}, bf16[104,3072]{1,0:T(8,128)(2,1)}, u32[]{:S(2)}) copy-start(bf16[104,3072]{1,0:T(8,128)(2,1)} %param.6) | copy-start | bytes 1916932
  6.5 134.9 %all-gather.4.cloned.1.call-start = ((), (), s32[]{:S(2)}) async-start(), calls=%async_computation | async-start | bytes 2383872 | tf_op jit(solution)/shard_map/all_gather | solution.py:14
  7.3 183.9 %all-gather.6.cloned.1.call-start = ((), (), s32[]{:S(2)}) async-start(), calls=%async_computation.1 | async-start | bytes 7077888 | tf_op jit(solution)/shard_map/all_gather | solution.py:15
  141.4 1.1 copy-start.1
  142.5 5.9 %copy-start.2 = (f32[3072]{0:T(1024)S(1)}, f32[3072]{0:T(1024)}, u32[]{:S(2)}) copy-start(f32[3072]{0:T(1024)} %param.8) | copy-start | bytes 36868
  144.5 32.8 %collective-permute-start.2 = (bf16[32,96,96]{2,1,0:T(8,128)(2,1)}, bf16[32,96,96]{2,1,0:T(8,128)(2,1)S(1)}, u32[]{:S(2)}, u32[]{:S(2)}) collective-permute-start(bf16[32,96,96]{2,1,0:T(8,128)(2,1)} %convolution_convert_fusion), channel_id=1, source_target_pairs={{0,3},{4,7},{8,11},{12,15},{16,19},{20,23},{24,27},{28,31},{32,35}... | collective-permute-start | bytes 1769480 | tf_op jit(solution)/shard_map/ppermute | solution.py:30
  145.8 31.5 %collective-permute-start.1 = (bf16[32,96,96]{2,1,0:T(8,128)(2,1)}, bf16[32,96,96]{2,1,0:T(8,128)(2,1)}, u32[]{:S(2)}, u32[]{:S(2)}) collective-permute-start(bf16[32,96,96]{2,1,0:T(8,128)(2,1)} %convolution_convert_fusion), channel_id=1, source_target_pairs={{0,2},{1,3},{4,6},{5,7},{8,10},{9,11},{12,14},{13,15},{16,18},{17,... | collective-permute-start | bytes 1769480 | tf_op jit(solution)/shard_map/ppermute | solution.py:30
  147.1 30.2 %collective-permute-start = (bf16[32,96,96]{2,1,0:T(8,128)(2,1)}, bf16[32,96,96]{2,1,0:T(8,128)(2,1)}, u32[]{:S(2)}, u32[]{:S(2)}) collective-permute-start(bf16[32,96,96]{2,1,0:T(8,128)(2,1)} %convolution_convert_fusion), channel_id=1, source_target_pairs={{0,1},{1,2},{2,3},{4,5},{5,6},{6,7},{8,9},{9,10},{10,11},{12,13},{... | collective-permute-start | bytes 1769480 | tf_op jit(solution)/shard_map/ppermute | solution.py:30
  180.5 39.8 %collective-permute-start.5 = (bf16[104,3072]{1,0:T(8,128)(2,1)S(1)}, bf16[104,3072]{1,0:T(8,128)(2,1)}, u32[]{:S(2)}, u32[]{:S(2)}) collective-permute-start(bf16[104,3072]{1,0:T(8,128)(2,1)S(1)} %multiply_convert_fusion.1), channel_id=1, source_target_pairs={{0,1},{1,2},{2,3},{3,0},{4,5},{5,6},{6,7},{7,4},{8,9},{9,10},{10,1... | collective-permute-start | bytes 1916936 | tf_op jit(solution)/shard_map/ppermute | solution.py:45
  183.5 34.9 %collective-permute-start.4 = (bf16[104,3072]{1,0:T(8,128)(2,1)S(1)}, bf16[104,3072]{1,0:T(8,128)(2,1)}, u32[]{:S(2)}, u32[]{:S(2)}) collective-permute-start(bf16[104,3072]{1,0:T(8,128)(2,1)S(1)} %multiply_convert_fusion.1), channel_id=1, source_target_pairs={{0,2},{1,3},{2,0},{3,1},{4,6},{5,7},{6,4},{7,5},{8,10},{9,11},{10,... | collective-permute-start | bytes 1916936 | tf_op jit(solution)/shard_map/ppermute | solution.py:45
  188.7 27.7 %collective-permute-start.3 = (bf16[104,3072]{1,0:T(8,128)(2,1)S(1)}, bf16[104,3072]{1,0:T(8,128)(2,1)}, u32[]{:S(2)}, u32[]{:S(2)}) collective-permute-start(bf16[104,3072]{1,0:T(8,128)(2,1)S(1)} %multiply_convert_fusion.1), channel_id=1, source_target_pairs={{0,3},{1,0},{2,1},{3,2},{4,7},{5,4},{6,5},{7,6},{8,11},{9,8},{10,9... | collective-permute-start | bytes 1916936 | tf_op jit(solution)/shard_map/ppermute | solution.py:45
Sparse Core Ops, SparseCore 0:
  11.1 130.2 all-gather.3
  143.8 22.0 all-gather.5

commit v2 on v1

--- a/solution.py
+++ b/solution.py
@@ -11,12 +11,9 @@
 
 def make_on_device(n_ctx, n_core):
     def on_device(queries, keys, values, norm_gain, out_weight):
-        w_half = lax.all_gather(out_weight, "chips", axis=0, tiled=True)
-        w_both = lax.all_gather(w_half, "core", axis=0, tiled=False)
-        rows, cols = out_weight.shape
-        weight_block = (
-            w_both.reshape(n_core, -1, rows, cols).transpose(1, 0, 2, 3).reshape(-1, cols)
-        )
+        weight_block = out_weight
+        for axis in ("core", "z", "y"):
+            weight_block = lax.all_gather(weight_block, axis, axis=0, tiled=True)
 
         tok_rows = queries.shape[0]
         q_heads = queries.reshape(tok_rows, HEADS, HEAD_DIM)
@@ -54,19 +51,21 @@
 def solution(mesh):
     n_fsdp, n_ctx = mesh.devices.shape
     n_core = 2
-    split = Mesh(mesh.devices.reshape(n_fsdp // n_core, n_core, n_ctx), ("chips", "core", "ctx"))
-    rows = ("chips", "core", "ctx")
+    n_y = len({d.coords[1] for d in mesh.devices.flat})
+    n_z = n_fsdp // (n_core * n_y)
+    split = Mesh(mesh.devices.reshape(n_y, n_z, n_core, n_ctx), ("y", "z", "core", "ctx"))
+    rows = ("y", "z", "core", "ctx")
     placed = (
         P(rows, None),
         P(rows, None),
         P(rows, None),
         P(),
-        P(("chips", "core"), "ctx"),
+        P(("y", "z", "core"), "ctx"),
     )
     return jax.shard_map(
         make_on_device(n_ctx, n_core),
         mesh=split,
         in_specs=placed,
-        out_specs=P(("chips", "core"), "ctx"),
+        out_specs=P(("y", "z", "core"), "ctx"),
         check_vma=False,
     )

time: 233 us -> 136 us (0.58)
  the two profiles are of different devices: /device:TPU:6 before, /device:TPU:1 now
where the time goes in v2:
time: 136 us
  waiting for transfers between devices  49.8 us (37%)
  blocking collectives  35.8 us (26%)
  starting transfers between devices  20.3 us (15%)
  between operations  13.6 us (10%)
  matrix products  12.4 us (9%)
  local copies, waits for them, and re-layouts  3.83 us (3%)
    all_gather x2, blocking collectives, on_device(): weight_block = lax.all_gather(weight_block, axis, axis=0, tiled=True)  35.8 us
    ppermute x3, waiting for transfers between devices, on_device(): lax.ppermute(state_bf, 'ctx', pairs).astype(jnp.float32)  25.9 us
    ppermute x3, waiting for transfers between devices, on_device(): got = lax.ppermute(normed, 'ctx', pairs)  15.6 us
    ppermute x3, starting transfers between devices, on_device(): lax.ppermute(state_bf, 'ctx', pairs).astype(jnp.float32)  10.6 us
    ppermute x3, starting transfers between devices, on_device(): got = lax.ppermute(normed, 'ctx', pairs)  9.74 us
    all_gather x1, waiting for transfers between devices, on_device(): weight_block = lax.all_gather(weight_block, axis, axis=0, tiled=True)  8.23 us
    dot_general x1, matrix products, on_device(): outs = [jnp.dot(normed, weight_block, preferred_element_type=jnp.float32)]  3.32 us
  transfers between devices with their start and end apart: 7, of which 6 were waited for; matrix products, arithmetic and copies ran while one was open for 11% of the time, Pallas kernels for 0%

profile of v2, /device:TPU:1, one launch (start us, length us, event | category | flops | bytes accessed | tf_op | source)
XLA Modules:
  0.0 136.0 jit_solution(13027062971472647657)
XLA Ops:
  6.5 0.0 all-gather.2.cloned.1.call-start
  6.5 12.3 %all_gather.9 = bf16[32,768]{1,0:T(8,128)(2,1)S(1)} all-gather(bf16[16,768]{1,0:T(8,128)(2,1)} %param.9), channel_id=1, replica_groups=mesh['y'=8,'z'=12,'core'=2,'ctx'=4] {'core'}, dimensions={0}, use_global_device_ids=true | all-gather | bytes 73728 | tf_op jit(solution)/shard_map/all_gather | solution.py:16
  18.9 23.4 %all_gather.10 = bf16[384,768]{1,0:T(8,128)(2,1)} all-gather(bf16[32,768]{1,0:T(8,128)(2,1)S(1)} %all_gather.9), channel_id=1, replica_groups=mesh['y'=8,'z'=12,'core'=2,'ctx'=4] {'z'}, dimensions={0}, use_global_device_ids=true | all-gather | bytes 638976 | tf_op jit(solution)/shard_map/all_gather | solution.py:16
  42.3 0.0 all-gather.2.cloned.1.call-update
  42.4 0.4 copy.26
  42.8 0.4 copy.27
  43.1 1.6 %convolution_convert_fusion = bf16[32,96,96]{2,1,0:T(8,128)(2,1)} fusion(bf16[104,32,96]{0,2,1:T(8,128)(2,1)S(1)} %bitcast.24, bf16[104,32,96]{0,2,1:T(8,128)(2,1)S(1)} %bitcast.26), kind=kOutput, calls=%fused_computation.4 | convolution fusion | flops 61636608 | bytes 1867776 | tf_op jit(solution)/shard_map/shd,she->hde/dot_general | solution.py:22
  44.7 3.2 %collective-permute-start = (bf16[32,96,96]{2,1,0:T(8,128)(2,1)}, bf16[32,96,96]{2,1,0:T(8,128)(2,1)S(1)}, u32[]{:S(2)}, u32[]{:S(2)}) collective-permute-start(bf16[32,96,96]{2,1,0:T(8,128)(2,1)} %convolution_convert_fusion), channel_id=1, source_target_pairs={{0,1},{1,2},{2,3},{4,5},{5,6},{6,7},{8,9},{9,10},{10,11},{12,13},{... | collective-permute-start | bytes 1769480 | tf_op jit(solution)/shard_map/ppermute | solution.py:27
  47.9 5.3 %collective-permute-start.1 = (bf16[32,96,96]{2,1,0:T(8,128)(2,1)}, bf16[32,96,96]{2,1,0:T(8,128)(2,1)}, u32[]{:S(2)}, u32[]{:S(2)}) collective-permute-start(bf16[32,96,96]{2,1,0:T(8,128)(2,1)} %convolution_convert_fusion), channel_id=1, source_target_pairs={{0,2},{1,3},{4,6},{5,7},{8,10},{9,11},{12,14},{13,15},{16,18},{17,... | collective-permute-start | bytes 1769480 | tf_op jit(solution)/shard_map/ppermute | solution.py:27
  53.1 2.2 %collective-permute-start.2 = (bf16[32,96,96]{2,1,0:T(8,128)(2,1)}, bf16[32,96,96]{2,1,0:T(8,128)(2,1)}, u32[]{:S(2)}, u32[]{:S(2)}) collective-permute-start(bf16[32,96,96]{2,1,0:T(8,128)(2,1)} %convolution_convert_fusion), channel_id=1, source_target_pairs={{0,3},{4,7},{8,11},{12,15},{16,19},{20,23},{24,27},{28,31},{32,35}... | collective-permute-start | bytes 1769480 | tf_op jit(solution)/shard_map/ppermute | solution.py:27
  55.3 1.5 %copy.25 = bf16[104,3072]{0,1:T(8,128)(2,1)S(1)} copy(bf16[104,3072]{1,0:T(8,128)(2,1)} %param.5) | data formatting | bytes 1277952 | tf_op jit(solution)/shard_map/reshape | solution.py:19
  56.8 2.4 %fusion = f32[32,104,96]{1,2,0:T(8,128)} fusion(bf16[104,32,96]{0,2,1:T(8,128)(2,1)S(1)} %bitcast.27, bf16[104,32,96]{0,2,1:T(8,128)(2,1)S(1)} %bitcast.22, bf16[104,32,96]{0,2,1:T(8,128)(2,1)S(1)} %bitcast.25, pred[104,104]{1,0:T(8,128)(4,1)S(1)} %iota_compare_fusion), kind=kOutput, calls=%fused_computation.5 | convolution fusion | flops 133599232 | bytes 3205696 | tf_op jit(solution)/shard_map/hts,shd->thd/dot_general | solution.py:33
  59.2 0.5 collective-permute-done
  59.6 16.9 %collective-permute-done.1 = bf16[32,96,96]{2,1,0:T(8,128)(2,1)} collective-permute-done((bf16[32,96,96]{2,1,0:T(8,128)(2,1)}, bf16[32,96,96]{2,1,0:T(8,128)(2,1)}, u32[]{:S(2)}, u32[]{:S(2)}) %collective-permute-start.1) | collective-permute-done | bytes 589856 | tf_op jit(solution)/shard_map/ppermute | solution.py:27
  76.5 8.6 %collective-permute-done.2 = bf16[32,96,96]{2,1,0:T(8,128)(2,1)} collective-permute-done((bf16[32,96,96]{2,1,0:T(8,128)(2,1)}, bf16[32,96,96]{2,1,0:T(8,128)(2,1)}, u32[]{:S(2)}, u32[]{:S(2)}) %collective-permute-start.2) | collective-permute-done | bytes 589856 | tf_op jit(solution)/shard_map/ppermute | solution.py:27
  85.1 2.5 %multiply_reduce_fusion = (f32[104]{0:T(128)S(1)}, f32[104,32,96]{0,2,1:T(8,128)S(1)}) fusion(bf16[104,32,96]{0,2,1:T(8,128)(2,1)S(1)} %bitcast.23, bf16[32,96,96]{2,1,0:T(8,128)(2,1)} %collective-permute-done.2, bf16[32,96,96]{2,1,0:T(8,128)(2,1)} %collective-permute-done.1, bf16[32,96,96]{2,1,0:T(8,128)(2,1)S(1)} %collective-permute-done, ...), kind=kOutput, calls=%fused_computation.2 | convolution fusion | flops 64069528 | bytes 4964768 | tf_op jit(solution)/shard_map/thd,hde->the/dot_general | solution.py:34
  87.6 0.5 copy.23
  88.1 0.2 copy-done.3
  88.3 0.2 multiply_convert_fusion
  88.5 5.3 %collective-permute-start.3 = (bf16[104,3072]{1,0:T(8,128)(2,1)S(1)}, bf16[104,3072]{1,0:T(8,128)(2,1)S(1)}, u32[]{:S(2)}, u32[]{:S(2)}) collective-permute-start(bf16[104,3072]{1,0:T(8,128)(2,1)S(1)} %multiply_convert_fusion), channel_id=1, source_target_pairs={{0,3},{1,0},{2,1},{3,2},{4,7},{5,4},{6,5},{7,6},{8,11},{9,8},{10,9... | collective-permute-start | bytes 1916936 | tf_op jit(solution)/shard_map/ppermute | solution.py:42
  93.9 1.9 %collective-permute-start.4 = (bf16[104,3072]{1,0:T(8,128)(2,1)S(1)}, bf16[104,3072]{1,0:T(8,128)(2,1)S(1)}, u32[]{:S(2)}, u32[]{:S(2)}) collective-permute-start(bf16[104,3072]{1,0:T(8,128)(2,1)S(1)} %multiply_convert_fusion), channel_id=1, source_target_pairs={{0,2},{1,3},{2,0},{3,1},{4,6},{5,7},{6,4},{7,5},{8,10},{9,11},{10,... | collective-permute-start | bytes 1916936 | tf_op jit(solution)/shard_map/ppermute | solution.py:42
  95.8 2.5 %collective-permute-start.5 = (bf16[104,3072]{1,0:T(8,128)(2,1)S(1)}, bf16[104,3072]{1,0:T(8,128)(2,1)S(1)}, u32[]{:S(2)}, u32[]{:S(2)}) collective-permute-start(bf16[104,3072]{1,0:T(8,128)(2,1)S(1)} %multiply_convert_fusion), channel_id=1, source_target_pairs={{0,1},{1,2},{2,3},{3,0},{4,5},{5,6},{6,7},{7,4},{8,9},{9,10},{10,1... | collective-permute-start | bytes 1916936 | tf_op jit(solution)/shard_map/ppermute | solution.py:42
  98.3 8.2 %all-gather.2.cloned.1.call-done = bf16[3072,768]{1,0:T(8,128)(2,1)} async-done(((bf16[384,768]{1,0:T(8,128)(2,1)}), bf16[3072,768]{1,0:T(8,128)(2,1)}) %all-gather.2.cloned.1.call-update) | async-done | bytes 4718608 | tf_op jit(solution)/shard_map/all_gather | solution.py:16
  106.5 3.3 %constant_dynamic-update-slice_fusion.7 = (bf16[832,768]{1,0:T(8,128)(2,1)S(1)}, bf16[104,768]{1,0:T(8,128)(2,1)S(1)}) fusion(bf16[104,3072]{1,0:T(8,128)(2,1)S(1)} %multiply_convert_fusion, bf16[3072,768]{1,0:T(8,128)(2,1)} %all-gather.2.cloned.1.call-done), kind=kOutput, calls=%fused_computation.21 | convolution fusion | flops 490813440 | bytes 5677056 | tf_op jit(solution)/shard_map/dot_general | solution.py:39
  109.9 10.8 %collective-permute-done.3 = bf16[104,3072]{1,0:T(8,128)(2,1)S(1)} collective-permute-done((bf16[104,3072]{1,0:T(8,128)(2,1)S(1)}, bf16[104,3072]{1,0:T(8,128)(2,1)S(1)}, u32[]{:S(2)}, u32[]{:S(2)}) %collective-permute-start.3) | collective-permute-done | bytes 639008 | tf_op jit(solution)/shard_map/ppermute | solution.py:42
  120.6 0.0 copy-done
  120.6 0.9 constant_dynamic-update-slice_fusion.6
  121.5 0.0 collective-permute-done.4
  121.5 0.9 constant_dynamic-update-slice_fusion.5
  122.4 4.9 %collective-permute-done.5 = bf16[104,3072]{1,0:T(8,128)(2,1)S(1)} collective-permute-done((bf16[104,3072]{1,0:T(8,128)(2,1)S(1)}, bf16[104,3072]{1,0:T(8,128)(2,1)S(1)}, u32[]{:S(2)}, u32[]{:S(2)}) %collective-permute-start.5) | collective-permute-done | bytes 639008 | tf_op jit(solution)/shard_map/ppermute | solution.py:42
  127.3 0.9 constant_dynamic-update-slice_fusion.4
  128.2 0.9 constant_dynamic-slice_fusion
  (12 shorter events, 0.1 us)
Async XLA Ops:
  6.5 35.8 %copy-start.1 = (bf16[104,3072]{1,0:T(8,128)(2,1)S(1)}, bf16[104,3072]{1,0:T(8,128)(2,1)}, u32[]{:S(2)}) copy-start(bf16[104,3072]{1,0:T(8,128)(2,1)} %param.6) | copy-start | bytes 1916932
  6.5 100.0 %all-gather.2.cloned.1.call-start = ((), (), s32[]{:S(2)}) async-start(), calls=%async_computation | async-start | bytes 5308416 | tf_op jit(solution)/shard_map/all_gather | solution.py:16
  18.9 23.9 %copy-start.2 = (bf16[104,3072]{1,0:T(8,128)(2,1)S(1)}, bf16[104,3072]{1,0:T(8,128)(2,1)}, u32[]{:S(2)}) copy-start(bf16[104,3072]{1,0:T(8,128)(2,1)} %param.7) | copy-start | bytes 1916932
  44.7 14.9 %collective-permute-start = (bf16[32,96,96]{2,1,0:T(8,128)(2,1)}, bf16[32,96,96]{2,1,0:T(8,128)(2,1)S(1)}, u32[]{:S(2)}, u32[]{:S(2)}) collective-permute-start(bf16[32,96,96]{2,1,0:T(8,128)(2,1)} %convolution_convert_fusion), channel_id=1, source_target_pairs={{0,1},{1,2},{2,3},{4,5},{5,6},{6,7},{8,9},{9,10},{10,11},{12,13},{... | collective-permute-start | bytes 1769480 | tf_op jit(solution)/shard_map/ppermute | solution.py:27
  47.9 28.6 %collective-permute-start.1 = (bf16[32,96,96]{2,1,0:T(8,128)(2,1)}, bf16[32,96,96]{2,1,0:T(8,128)(2,1)}, u32[]{:S(2)}, u32[]{:S(2)}) collective-permute-start(bf16[32,96,96]{2,1,0:T(8,128)(2,1)} %convolution_convert_fusion), channel_id=1, source_target_pairs={{0,2},{1,3},{4,6},{5,7},{8,10},{9,11},{12,14},{13,15},{16,18},{17,... | collective-permute-start | bytes 1769480 | tf_op jit(solution)/shard_map/ppermute | solution.py:27
  53.1 32.0 %collective-permute-start.2 = (bf16[32,96,96]{2,1,0:T(8,128)(2,1)}, bf16[32,96,96]{2,1,0:T(8,128)(2,1)}, u32[]{:S(2)}, u32[]{:S(2)}) collective-permute-start(bf16[32,96,96]{2,1,0:T(8,128)(2,1)} %convolution_convert_fusion), channel_id=1, source_target_pairs={{0,3},{4,7},{8,11},{12,15},{16,19},{20,23},{24,27},{28,31},{32,35}... | collective-permute-start | bytes 1769480 | tf_op jit(solution)/shard_map/ppermute | solution.py:27
  87.6 0.7 copy-start.3
  88.5 32.1 %collective-permute-start.3 = (bf16[104,3072]{1,0:T(8,128)(2,1)S(1)}, bf16[104,3072]{1,0:T(8,128)(2,1)S(1)}, u32[]{:S(2)}, u32[]{:S(2)}) collective-permute-start(bf16[104,3072]{1,0:T(8,128)(2,1)S(1)} %multiply_convert_fusion), channel_id=1, source_target_pairs={{0,3},{1,0},{2,1},{3,2},{4,7},{5,4},{6,5},{7,6},{8,11},{9,8},{10,9... | collective-permute-start | bytes 1916936 | tf_op jit(solution)/shard_map/ppermute | solution.py:42
  93.9 27.6 %collective-permute-start.4 = (bf16[104,3072]{1,0:T(8,128)(2,1)S(1)}, bf16[104,3072]{1,0:T(8,128)(2,1)S(1)}, u32[]{:S(2)}, u32[]{:S(2)}) collective-permute-start(bf16[104,3072]{1,0:T(8,128)(2,1)S(1)} %multiply_convert_fusion), channel_id=1, source_target_pairs={{0,2},{1,3},{2,0},{3,1},{4,6},{5,7},{6,4},{7,5},{8,10},{9,11},{10,... | collective-permute-start | bytes 1916936 | tf_op jit(solution)/shard_map/ppermute | solution.py:42
  95.8 31.5 %collective-permute-start.5 = (bf16[104,3072]{1,0:T(8,128)(2,1)S(1)}, bf16[104,3072]{1,0:T(8,128)(2,1)S(1)}, u32[]{:S(2)}, u32[]{:S(2)}) collective-permute-start(bf16[104,3072]{1,0:T(8,128)(2,1)S(1)} %multiply_convert_fusion), channel_id=1, source_target_pairs={{0,1},{1,2},{2,3},{3,0},{4,5},{5,6},{6,7},{7,4},{8,9},{9,10},{10,1... | collective-permute-start | bytes 1916936 | tf_op jit(solution)/shard_map/ppermute | solution.py:42
  106.5 14.1 %copy-start = (bf16[3072,768]{1,0:T(8,128)(2,1)S(1)}, bf16[3072,768]{1,0:T(8,128)(2,1)}, u32[]{:S(2)}) copy-start(bf16[3072,768]{1,0:T(8,128)(2,1)} %all-gather.2.cloned.1.call-done) | copy-start | bytes 14155780
Sparse Core Ops, SparseCore 0:
  42.5 64.0 all-gather.1

commit v3 on v2

--- a/solution.py
+++ b/solution.py
@@ -22,9 +22,16 @@
         local_state = jnp.einsum("shd,she->hde", k_heads, v_heads, preferred_element_type=jnp.float32)
         state_bf = local_state.astype(jnp.bfloat16)
         prefix_f32 = jnp.zeros(local_state.shape, jnp.float32)
-        for shift in range(1, n_ctx):
-            pairs = [(i, i + shift) for i in range(n_ctx - shift)]
-            prefix_f32 = prefix_f32 + lax.ppermute(state_bf, "ctx", pairs).astype(jnp.float32)
+        if n_ctx == 4:
+            from_prev = lax.ppermute(state_bf, "ctx", [(0, 1), (1, 2), (2, 3)])
+            from_first = lax.ppermute(state_bf, "ctx", [(0, 3)])
+            forwarded = lax.ppermute(from_prev, "ctx", [(1, 2), (2, 3)])
+            for got in (from_prev, from_first, forwarded):
+                prefix_f32 = prefix_f32 + got.astype(jnp.float32)
+        else:
+            for shift in range(1, n_ctx):
+                pairs = [(i, i + shift) for i in range(n_ctx - shift)]
+                prefix_f32 = prefix_f32 + lax.ppermute(state_bf, "ctx", pairs).astype(jnp.float32)
         prefix_state = prefix_f32.astype(jnp.bfloat16)
 
         scores = jnp.einsum("thd,shd->hts", q_heads, k_heads, preferred_element_type=jnp.float32)
@@ -36,11 +43,25 @@
         mean_sq = jnp.mean(attn * attn, axis=-1, keepdims=True)
         normed = (attn * lax.rsqrt(mean_sq + 1e-05) * norm_gain).astype(jnp.bfloat16)
 
-        outs = [jnp.dot(normed, weight_block, preferred_element_type=jnp.float32)]
-        for shift in range(1, n_ctx):
-            pairs = [(i, (i - shift) % n_ctx) for i in range(n_ctx)]
-            got = lax.ppermute(normed, "ctx", pairs)
-            outs.append(jnp.dot(got, weight_block, preferred_element_type=jnp.float32))
+        def shift_by(x, s):
+            return lax.ppermute(x, "ctx", [(i, (i - s) % n_ctx) for i in range(n_ctx)])
+
+        half = HEADS * HEAD_DIM // 2
+        outs = [None] * n_ctx
+        outs[0] = jnp.dot(normed, weight_block, preferred_element_type=jnp.float32)
+        ahead, behind = normed, normed
+        for s in range(1, n_ctx // 2 + 1):
+            if 2 * s < n_ctx:
+                ahead = shift_by(ahead, 1)
+                behind = shift_by(behind, -1)
+                outs[s] = jnp.dot(ahead, weight_block, preferred_element_type=jnp.float32)
+                outs[n_ctx - s] = jnp.dot(behind, weight_block, preferred_element_type=jnp.float32)
+            else:
+                left = shift_by(ahead[:, :half], 1)
+                right = shift_by(behind[:, half:], -1)
+                outs[s] = jnp.dot(left, weight_block[:half], preferred_element_type=jnp.float32) + jnp.dot(
+                    right, weight_block[half:], preferred_element_type=jnp.float32
+                )
         stacked = jnp.concatenate(outs + outs, axis=0).astype(jnp.bfloat16)
         position = lax.axis_index("ctx")
         return lax.dynamic_slice_in_dim(stacked, (n_ctx - position) * tok_rows, n_ctx * tok_rows, axis=0)

time: 136 us -> 123 us (0.904)
  the two profiles are of different devices: /device:TPU:1 before, /device:TPU:6 now
where the time goes in v3:
time: 123 us; the launch traced here: 122 us
  blocking collectives  39.5 us (32%)
  waiting for transfers between devices  35.9 us (29%)
  starting transfers between devices  15.7 us (13%)
  between operations  13.6 us (11%)
  matrix products  12.6 us (10%)
  local copies, waits for them, and re-layouts  4.3 us (3%)
    all_gather x2, blocking collectives, on_device(): weight_block = lax.all_gather(weight_block, axis, axis=0, tiled=True)  39.5 us
    ppermute x1, waiting for transfers between devices, on_device(): from_prev = lax.ppermute(state_bf, 'ctx', [(0, 1), (1, 2), (2, 3)])  15.2 us
    ppermute x4, starting transfers between devices, shift_by(): return lax.ppermute(x, 'ctx', [(i, (i - s) % n_ctx) for i in range(n_ctx)])  11.9 us
    ppermute x1, waiting for transfers between devices, on_device(): forwarded = lax.ppermute(from_prev, 'ctx', [(1, 2), (2, 3)])  10.7 us
    ppermute x4, waiting for transfers between devices, shift_by(): return lax.ppermute(x, 'ctx', [(i, (i - s) % n_ctx) for i in range(n_ctx)])  9.89 us
    dot_general x1, matrix products, on_device(): outs[0] = jnp.dot(normed, weight_block, preferred_element_type=jnp.float32)  3.33 us
    dot_general x1, matrix products, on_device(): jnp.einsum('thd,hde->the', q_heads, prefix_state, preferred_element_type=...  2.54 us
  transfers between devices with their start and end apart: 8, of which 4 were waited for; matrix products, arithmetic and copies ran while one was open for 12% of the time, Pallas kernels for 0%

profile of v3, /device:TPU:6, one launch (start us, length us, event | category | flops | bytes accessed | tf_op | source)
XLA Modules:
  0.0 121.8 jit_solution(4951348361775518493)
XLA Ops:
  6.5 2.2 %all_gather.9 = bf16[32,768]{1,0:T(8,128)(2,1)S(1)} all-gather(bf16[16,768]{1,0:T(8,128)(2,1)} %param.9), channel_id=1, replica_groups=mesh['y'=8,'z'=12,'core'=2,'ctx'=4] {'core'}, dimensions={0}, use_global_device_ids=true | all-gather | bytes 73728 | tf_op jit(solution)/shard_map/all_gather | solution.py:16
  8.7 37.3 %all_gather.10 = bf16[384,768]{1,0:T(8,128)(2,1)} all-gather(bf16[32,768]{1,0:T(8,128)(2,1)S(1)} %all_gather.9), channel_id=1, replica_groups=mesh['y'=8,'z'=12,'core'=2,'ctx'=4] {'z'}, dimensions={0}, use_global_device_ids=true | all-gather | bytes 638976 | tf_op jit(solution)/shard_map/all_gather | solution.py:16
  46.0 0.0 all-gather.2.cloned.1.call-update
  46.1 0.4 copy.26
  46.4 0.4 copy.27
  46.8 1.6 %convolution_convert_fusion = bf16[32,96,96]{2,1,0:T(8,128)(2,1)} fusion(bf16[104,32,96]{0,2,1:T(8,128)(2,1)S(1)} %bitcast.24, bf16[104,32,96]{0,2,1:T(8,128)(2,1)S(1)} %bitcast.26), kind=kOutput, calls=%fused_computation.8 | convolution fusion | flops 61636608 | bytes 1867776 | tf_op jit(solution)/shard_map/shd,she->hde/dot_general | solution.py:22
  48.4 1.3 %collective-permute-start = (bf16[32,96,96]{2,1,0:T(8,128)(2,1)}, bf16[32,96,96]{2,1,0:T(8,128)(2,1)S(1)}, u32[]{:S(2)}, u32[]{:S(2)}) collective-permute-start(bf16[32,96,96]{2,1,0:T(8,128)(2,1)} %convolution_convert_fusion), channel_id=1, source_target_pairs={{0,1},{1,2},{2,3},{4,5},{5,6},{6,7},{8,9},{9,10},{10,11},{12,13},{... | collective-permute-start | bytes 1769480 | tf_op jit(solution)/shard_map/ppermute | solution.py:26
  49.7 1.3 %collective-permute-start.1 = (bf16[32,96,96]{2,1,0:T(8,128)(2,1)}, bf16[32,96,96]{2,1,0:T(8,128)(2,1)}, u32[]{:S(2)}, u32[]{:S(2)}) collective-permute-start(bf16[32,96,96]{2,1,0:T(8,128)(2,1)} %convolution_convert_fusion), channel_id=1, source_target_pairs={{0,3},{4,7},{8,11},{12,15},{16,19},{20,23},{24,27},{28,31},{32,35}... | collective-permute-start | bytes 1769480 | tf_op jit(solution)/shard_map/ppermute | solution.py:27
  51.0 15.2 %collective-permute-done = bf16[32,96,96]{2,1,0:T(8,128)(2,1)S(1)} collective-permute-done((bf16[32,96,96]{2,1,0:T(8,128)(2,1)}, bf16[32,96,96]{2,1,0:T(8,128)(2,1)S(1)}, u32[]{:S(2)}, u32[]{:S(2)}) %collective-permute-start) | collective-permute-done | bytes 589856 | tf_op jit(solution)/shard_map/ppermute | solution.py:26
  66.2 1.3 %collective-permute-start.2 = (bf16[32,96,96]{2,1,0:T(8,128)(2,1)S(1)}, bf16[32,96,96]{2,1,0:T(8,128)(2,1)}, u32[]{:S(2)}, u32[]{:S(2)}) collective-permute-start(bf16[32,96,96]{2,1,0:T(8,128)(2,1)S(1)} %collective-permute-done), channel_id=1, source_target_pairs={{1,2},{2,3},{5,6},{6,7},{9,10},{10,11},{13,14},{14,15},{17,18},{18... | collective-permute-start | bytes 1769480 | tf_op jit(solution)/shard_map/ppermute | solution.py:28
  67.5 1.5 %copy.25 = bf16[104,3072]{0,1:T(8,128)(2,1)S(1)} copy(bf16[104,3072]{1,0:T(8,128)(2,1)} %param.5) | data formatting | bytes 1277952 | tf_op jit(solution)/shard_map/reshape | solution.py:19
  69.0 2.4 %fusion.4 = f32[32,104,96]{1,2,0:T(8,128)} fusion(bf16[104,32,96]{0,2,1:T(8,128)(2,1)S(1)} %bitcast.27, bf16[104,32,96]{0,2,1:T(8,128)(2,1)S(1)} %bitcast.22, bf16[104,32,96]{0,2,1:T(8,128)(2,1)S(1)} %bitcast.25, pred[104,104]{1,0:T(8,128)(4,1)S(1)} %iota_compare_fusion), kind=kOutput, calls=%fused_computation.9 | convolution fusion | flops 133599232 | bytes 3205696 | tf_op jit(solution)/shard_map/hts,shd->thd/dot_general | solution.py:40
  71.4 0.0 collective-permute-done.1
  71.4 10.7 %collective-permute-done.2 = bf16[32,96,96]{2,1,0:T(8,128)(2,1)} collective-permute-done((bf16[32,96,96]{2,1,0:T(8,128)(2,1)S(1)}, bf16[32,96,96]{2,1,0:T(8,128)(2,1)}, u32[]{:S(2)}, u32[]{:S(2)}) %collective-permute-start.2) | collective-permute-done | bytes 589856 | tf_op jit(solution)/shard_map/ppermute | solution.py:28
  82.1 2.5 %multiply_reduce_fusion = (f32[104]{0:T(128)S(1)}, f32[104,32,96]{0,2,1:T(8,128)S(1)}) fusion(bf16[104,32,96]{0,2,1:T(8,128)(2,1)S(1)} %bitcast.23, bf16[32,96,96]{2,1,0:T(8,128)(2,1)} %collective-permute-done.2, bf16[32,96,96]{2,1,0:T(8,128)(2,1)} %collective-permute-done.1, bf16[32,96,96]{2,1,0:T(8,128)(2,1)S(1)} %collective-permute-done, ...), kind=kOutput, calls=%fused_computation.6 | convolution fusion | flops 64069528 | bytes 4964768 | tf_op jit(solution)/shard_map/thd,hde->the/dot_general | solution.py:41
  84.6 0.5 copy.23
  85.1 0.2 copy-done.3
  85.3 0.2 multiply_convert_fusion
  85.5 1.9 %collective-permute-start.5 = (bf16[104,3072]{1,0:T(8,128)(2,1)S(1)}, bf16[104,3072]{1,0:T(8,128)(2,1)S(1)}, u32[]{:S(2)}, u32[]{:S(2)}) collective-permute-start(bf16[104,3072]{1,0:T(8,128)(2,1)S(1)} %multiply_convert_fusion), channel_id=1, source_target_pairs={{0,1},{1,2},{2,3},{3,0},{4,5},{5,6},{6,7},{7,4},{8,9},{9,10},{10,1... | collective-permute-start | bytes 1916936 | tf_op jit(solution)/shard_map/ppermute | solution.py:47
  87.5 3.9 %collective-permute-start.3 = (bf16[104,3072]{1,0:T(8,128)(2,1)S(1)}, bf16[104,3072]{1,0:T(8,128)(2,1)S(1)}, u32[]{:S(2)}, u32[]{:S(2)}) collective-permute-start(bf16[104,3072]{1,0:T(8,128)(2,1)S(1)} %multiply_convert_fusion), channel_id=1, source_target_pairs={{0,3},{1,0},{2,1},{3,2},{4,7},{5,4},{6,5},{7,6},{8,11},{9,8},{10,9... | collective-permute-start | bytes 1916936 | tf_op jit(solution)/shard_map/ppermute | solution.py:47
  91.4 9.1 %collective-permute-done.5 = bf16[104,3072]{1,0:T(8,128)(2,1)S(1)} collective-permute-done((bf16[104,3072]{1,0:T(8,128)(2,1)S(1)}, bf16[104,3072]{1,0:T(8,128)(2,1)S(1)}, u32[]{:S(2)}, u32[]{:S(2)}) %collective-permute-start.5) | collective-permute-done | bytes 639008 | tf_op jit(solution)/shard_map/ppermute | solution.py:47
  100.5 1.9 %collective-permute-start.6 = (bf16[104,1536]{1,0:T(8,128)(2,1)S(1)}, bf16[104,1536]{1,0:T(8,128)(2,1)S(1)}, u32[]{:S(2)}, u32[]{:S(2)}) collective-permute-start(bf16[104,1536]{1,0:T(8,128)(2,1)S(1)} %slice.18), channel_id=1, source_target_pairs={{0,1},{1,2},{2,3},{3,0},{4,5},{5,6},{6,7},{7,4},{8,9},{9,10},{10,1... | collective-permute-start | bytes 958472 | tf_op jit(solution)/shard_map/ppermute | solution.py:47
  102.5 4.1 %collective-permute-start.4 = (bf16[104,1536]{1,0:T(8,128)(2,1)S(1)}, bf16[104,1536]{1,0:T(8,128)(2,1)S(1)}, u32[]{:S(2)}, u32[]{:S(2)}) collective-permute-start(bf16[104,1536]{1,0:T(8,128)(2,1)S(1)} %slice.16), channel_id=1, source_target_pairs={{0,3},{1,0},{2,1},{3,2},{4,7},{5,4},{6,5},{7,6},{8,11},{9,8},{10,9... | collective-permute-start | bytes 958472 | tf_op jit(solution)/shard_map/ppermute | solution.py:47
  106.6 0.0 all-gather.2.cloned.1.call-done
  106.7 3.3 %constant_dynamic-update-slice_fusion.7 = (bf16[832,768]{1,0:T(8,128)(2,1)S(1)}, bf16[104,768]{1,0:T(8,128)(2,1)S(1)}) fusion(bf16[104,3072]{1,0:T(8,128)(2,1)S(1)} %multiply_convert_fusion, bf16[3072,768]{1,0:T(8,128)(2,1)} %all-gather.2.cloned.1.call-done), kind=kOutput, calls=%fused_computation.26 | convolution fusion | flops 490813440 | bytes 5677056 | tf_op jit(solution)/shard_map/dot_general | solution.py:51
  110.0 0.4 copy-done
  110.4 0.9 constant_dynamic-update-slice_fusion.6
  111.3 0.5 fusion
  111.8 0.8 collective-permute-done.4
  112.6 0.5 constant_dynamic-update-slice_fusion.5
  113.1 0.9 constant_dynamic-update-slice_fusion.4
  114.1 0.9 constant_dynamic-slice_fusion
  (17 shorter events, 0.1 us)
Async XLA Ops:
  6.5 39.5 %copy-start.1 = (bf16[104,3072]{1,0:T(8,128)(2,1)S(1)}, bf16[104,3072]{1,0:T(8,128)(2,1)}, u32[]{:S(2)}) copy-start(bf16[104,3072]{1,0:T(8,128)(2,1)} %param.6) | copy-start | bytes 1916932
  6.5 39.9 %copy-start.2 = (bf16[104,3072]{1,0:T(8,128)(2,1)S(1)}, bf16[104,3072]{1,0:T(8,128)(2,1)}, u32[]{:S(2)}) copy-start(bf16[104,3072]{1,0:T(8,128)(2,1)} %param.7) | copy-start | bytes 1916932
  6.5 100.1 %all-gather.2.cloned.1.call-start = ((), (), s32[]{:S(2)}) async-start(), calls=%async_computation | async-start | bytes 5308416 | tf_op jit(solution)/shard_map/all_gather | solution.py:16
  48.4 17.8 %collective-permute-start = (bf16[32,96,96]{2,1,0:T(8,128)(2,1)}, bf16[32,96,96]{2,1,0:T(8,128)(2,1)S(1)}, u32[]{:S(2)}, u32[]{:S(2)}) collective-permute-start(bf16[32,96,96]{2,1,0:T(8,128)(2,1)} %convolution_convert_fusion), channel_id=1, source_target_pairs={{0,1},{1,2},{2,3},{4,5},{5,6},{6,7},{8,9},{9,10},{10,11},{12,13},{... | collective-permute-start | bytes 1769480 | tf_op jit(solution)/shard_map/ppermute | solution.py:26
  49.7 21.7 %collective-permute-start.1 = (bf16[32,96,96]{2,1,0:T(8,128)(2,1)}, bf16[32,96,96]{2,1,0:T(8,128)(2,1)}, u32[]{:S(2)}, u32[]{:S(2)}) collective-permute-start(bf16[32,96,96]{2,1,0:T(8,128)(2,1)} %convolution_convert_fusion), channel_id=1, source_target_pairs={{0,3},{4,7},{8,11},{12,15},{16,19},{20,23},{24,27},{28,31},{32,35}... | collective-permute-start | bytes 1769480 | tf_op jit(solution)/shard_map/ppermute | solution.py:27
  66.2 15.9 %collective-permute-start.2 = (bf16[32,96,96]{2,1,0:T(8,128)(2,1)S(1)}, bf16[32,96,96]{2,1,0:T(8,128)(2,1)}, u32[]{:S(2)}, u32[]{:S(2)}) collective-permute-start(bf16[32,96,96]{2,1,0:T(8,128)(2,1)S(1)} %collective-permute-done), channel_id=1, source_target_pairs={{1,2},{2,3},{5,6},{6,7},{9,10},{10,11},{13,14},{14,15},{17,18},{18... | collective-permute-start | bytes 1769480 | tf_op jit(solution)/shard_map/ppermute | solution.py:28
  84.6 0.7 copy-start.3
  85.5 15.0 %collective-permute-start.5 = (bf16[104,3072]{1,0:T(8,128)(2,1)S(1)}, bf16[104,3072]{1,0:T(8,128)(2,1)S(1)}, u32[]{:S(2)}, u32[]{:S(2)}) collective-permute-start(bf16[104,3072]{1,0:T(8,128)(2,1)S(1)} %multiply_convert_fusion), channel_id=1, source_target_pairs={{0,1},{1,2},{2,3},{3,0},{4,5},{5,6},{6,7},{7,4},{8,9},{9,10},{10,1... | collective-permute-start | bytes 1916936 | tf_op jit(solution)/shard_map/ppermute | solution.py:47
  87.5 15.0 %collective-permute-start.3 = (bf16[104,3072]{1,0:T(8,128)(2,1)S(1)}, bf16[104,3072]{1,0:T(8,128)(2,1)S(1)}, u32[]{:S(2)}, u32[]{:S(2)}) collective-permute-start(bf16[104,3072]{1,0:T(8,128)(2,1)S(1)} %multiply_convert_fusion), channel_id=1, source_target_pairs={{0,3},{1,0},{2,1},{3,2},{4,7},{5,4},{6,5},{7,6},{8,11},{9,8},{10,9... | collective-permute-start | bytes 1916936 | tf_op jit(solution)/shard_map/ppermute | solution.py:47
  100.5 10.8 %collective-permute-start.6 = (bf16[104,1536]{1,0:T(8,128)(2,1)S(1)}, bf16[104,1536]{1,0:T(8,128)(2,1)S(1)}, u32[]{:S(2)}, u32[]{:S(2)}) collective-permute-start(bf16[104,1536]{1,0:T(8,128)(2,1)S(1)} %slice.18), channel_id=1, source_target_pairs={{0,1},{1,2},{2,3},{3,0},{4,5},{5,6},{6,7},{7,4},{8,9},{9,10},{10,1... | collective-permute-start | bytes 958472 | tf_op jit(solution)/shard_map/ppermute | solution.py:47
  102.5 10.1 %collective-permute-start.4 = (bf16[104,1536]{1,0:T(8,128)(2,1)S(1)}, bf16[104,1536]{1,0:T(8,128)(2,1)S(1)}, u32[]{:S(2)}, u32[]{:S(2)}) collective-permute-start(bf16[104,1536]{1,0:T(8,128)(2,1)S(1)} %slice.16), channel_id=1, source_target_pairs={{0,3},{1,0},{2,1},{3,2},{4,7},{5,4},{6,5},{7,6},{8,11},{9,8},{10,9... | collective-permute-start | bytes 958472 | tf_op jit(solution)/shard_map/ppermute | solution.py:47
  106.6 3.8 %copy-start = (bf16[3072,768]{1,0:T(8,128)(2,1)S(1)}, bf16[3072,768]{1,0:T(8,128)(2,1)}, u32[]{:S(2)}) copy-start(bf16[3072,768]{1,0:T(8,128)(2,1)} %all-gather.2.cloned.1.call-done) | copy-start | bytes 14155780
Sparse Core Ops, SparseCore 0:
  46.2 59.2 all-gather.1

commit v4 on v3

--- a/solution.py
+++ b/solution.py
@@ -9,11 +9,12 @@
 HEAD_DIM = 96
 
 
-def make_on_device(n_ctx, n_core):
+def make_on_device(n_ctx, n_core, n_y, n_z):
     def on_device(queries, keys, values, norm_gain, out_weight):
-        weight_block = out_weight
-        for axis in ("core", "z", "y"):
-            weight_block = lax.all_gather(weight_block, axis, axis=0, tiled=True)
+        rows, cols = out_weight.shape
+        half = out_weight
+        for axis in ("z", "y"):
+            half = lax.all_gather(half, axis, axis=0, tiled=True)
 
         tok_rows = queries.shape[0]
         q_heads = queries.reshape(tok_rows, HEADS, HEAD_DIM)
@@ -33,6 +34,15 @@
                 pairs = [(i, i + shift) for i in range(n_ctx - shift)]
                 prefix_f32 = prefix_f32 + lax.ppermute(state_bf, "ctx", pairs).astype(jnp.float32)
         prefix_state = prefix_f32.astype(jnp.bfloat16)
+
+        half, _ = lax.optimization_barrier((half, prefix_f32))
+        other = lax.ppermute(half, "core", [(0, 1), (1, 0)])
+        mine_first = lax.axis_index("core") == 0
+        half = half.reshape(-1, 1, rows, cols)
+        other = other.reshape(-1, 1, rows, cols)
+        weight_block = jnp.concatenate(
+            [jnp.where(mine_first, half, other), jnp.where(mine_first, other, half)], axis=1
+        ).reshape(-1, cols)
 
         scores = jnp.einsum("thd,shd->hts", q_heads, k_heads, preferred_element_type=jnp.float32)
         causal = jnp.arange(tok_rows)[:, None] >= jnp.arange(tok_rows)[None, :]
@@ -84,7 +94,7 @@
         P(("y", "z", "core"), "ctx"),
     )
     return jax.shard_map(
-        make_on_device(n_ctx, n_core),
+        make_on_device(n_ctx, n_core, n_y, n_z),
         mesh=split,
         in_specs=placed,
         out_specs=P(("y", "z", "core"), "ctx"),

time: 123 us -> 136 us (1.11)
  waiting for transfers between devices: 35.9 us -> 48.1 us
  other arithmetic: 0.21 us -> 5.48 us
  blocking collectives: 39.5 us -> 35.9 us
  matrix products: 12.6 us -> 9.54 us
  starting transfers between devices: 15.7 us -> 17.4 us
    ppermute x4, waiting for transfers between devices: 9.89 us -> 17 us  [shift_by(): return lax.ppermute(x, 'ctx', [(i, (i - s) % n_ctx) for i in range(n_ctx)])]
    all_gather x2 -> x1, blocking collectives: 39.5 us -> 35.9 us  [on_device(): half = lax.all_gather(half, axis, axis=0, tiled=True)]
    all_gather x1, waiting for transfers between devices: 0.02 us -> 3.55 us  [on_device(): half = lax.all_gather(half, axis, axis=0, tiled=True)]
    dot_general x1, matrix products: 3.33 us -> 0.81 us  [on_device(): outs[0] = jnp.dot(normed, weight_block, preferred_element_type=jnp.float32)]
    select_n x0 -> x1, other arithmetic: none -> 1.98 us  [on_device(): jnp.where(mine_first, half, other)]
    add x0 -> x1, other arithmetic: none -> 1.94 us  [on_device(): prefix_f32 = prefix_f32 + got.astype(jnp.float32)]
    ppermute x0 -> x1, starting transfers between devices: none -> 1.91 us  [on_device(): other = lax.ppermute(half, 'core', [(0, 1), (1, 0)])]
    ppermute x1, waiting for transfers between devices: 10.7 us -> 12.3 us  [on_device(): forwarded = lax.ppermute(from_prev, 'ctx', [(1, 2), (2, 3)])]
  transfers between devices with their start and end apart: 8 -> 9, of which waited for: 4 -> 6; matrix products, arithmetic and copies ran while one was open for 12% -> 13% of each run, Pallas kernels for 0% -> 0%
where the time goes in v4:
time: 136 us; the launch traced here: 135 us
  waiting for transfers between devices  48.1 us (35%)
  blocking collectives  35.9 us (26%)
  starting transfers between devices  17.4 us (13%)
  between operations  13.7 us (10%)
  matrix products  9.54 us (7%)
  other arithmetic  5.48 us (4%)
  local copies, waits for them, and re-layouts  5.05 us (4%)
    all_gather x1, blocking collectives, on_device(): half = lax.all_gather(half, axis, axis=0, tiled=True)  35.9 us
    ppermute x4, waiting for transfers between devices, shift_by(): return lax.ppermute(x, 'ctx', [(i, (i - s) % n_ctx) for i in range(n_ctx)])  17 us
    ppermute x1, waiting for transfers between devices, on_device(): from_prev = lax.ppermute(state_bf, 'ctx', [(0, 1), (1, 2), (2, 3)])  15.2 us
    ppermute x1, waiting for transfers between devices, on_device(): forwarded = lax.ppermute(from_prev, 'ctx', [(1, 2), (2, 3)])  12.3 us
    ppermute x4, starting transfers between devices, shift_by(): return lax.ppermute(x, 'ctx', [(i, (i - s) % n_ctx) for i in range(n_ctx)])  11.7 us
    all_gather x1, waiting for transfers between devices, on_device(): half = lax.all_gather(half, axis, axis=0, tiled=True)  3.55 us
  transfers between devices with their start and end apart: 9, of which 6 were waited for; matrix products, arithmetic and copies ran while one was open for 13% of the time, Pallas kernels for 0%

profile of v4, /device:TPU:6, one launch (start us, length us, event | category | flops | bytes accessed | tf_op | source)
XLA Modules:
  0.0 135.2 jit_solution(12601546179558884340)
XLA Ops:
  6.5 35.9 %all_gather.6 = bf16[192,768]{1,0:T(8,128)(2,1)} all-gather(bf16[16,768]{1,0:T(8,128)(2,1)} %param.9), channel_id=1, replica_groups=mesh['y'=8,'z'=12,'core'=2,'ctx'=4] {'z'}, dimensions={0}, use_global_device_ids=true | all-gather | bytes 319488 | tf_op jit(solution)/shard_map/all_gather | solution.py:17
  42.5 1.5 %copy.26 = bf16[104,3072]{0,1:T(8,128)(2,1)S(1)} copy(bf16[104,3072]{1,0:T(8,128)(2,1)} %param.6) | data formatting | bytes 1277952 | tf_op jit(solution)/shard_map/reshape | solution.py:21
  44.3 1.6 %convolution_convert_fusion = bf16[32,96,96]{2,1,0:T(8,128)(2,1)} fusion(bf16[104,32,96]{0,2,1:T(8,128)(2,1)S(1)} %bitcast.43, bf16[104,32,96]{0,2,1:T(8,128)(2,1)S(1)} %bitcast.45), kind=kOutput, calls=%fused_computation.14 | convolution fusion | flops 61636608 | bytes 1867776 | tf_op jit(solution)/shard_map/shd,she->hde/dot_general | solution.py:23
  45.9 1.3 collective-permute-start
  47.2 1.3 collective-permute-start.1
  48.5 15.2 %collective-permute-done = bf16[32,96,96]{2,1,0:T(8,128)(2,1)S(1)} collective-permute-done((bf16[32,96,96]{2,1,0:T(8,128)(2,1)}, bf16[32,96,96]{2,1,0:T(8,128)(2,1)S(1)}, u32[]{:S(2)}, u32[]{:S(2)}) %collective-permute-start) | collective-permute-done | bytes 589856 | tf_op jit(solution)/shard_map/ppermute | solution.py:27
  63.7 1.3 collective-permute-start.2
  65.0 1.5 %copy.25 = bf16[104,3072]{0,1:T(8,128)(2,1)S(1)} copy(bf16[104,3072]{1,0:T(8,128)(2,1)} %param.5) | data formatting | bytes 1277952 | tf_op jit(solution)/shard_map/reshape | solution.py:20
  66.5 12.3 %collective-permute-done.2 = bf16[32,96,96]{2,1,0:T(8,128)(2,1)} collective-permute-done((bf16[32,96,96]{2,1,0:T(8,128)(2,1)S(1)}, bf16[32,96,96]{2,1,0:T(8,128)(2,1)}, u32[]{:S(2)}, u32[]{:S(2)}) %collective-permute-start.2) | collective-permute-done | bytes 589856 | tf_op jit(solution)/shard_map/ppermute | solution.py:29
  78.8 1.9 %convert_add_fusion = bf16[32,96,96]{2,1,0:T(8,128)(2,1)S(1)} fusion(bf16[32,96,96]{2,1,0:T(8,128)(2,1)} %collective-permute-done.2, bf16[32,96,96]{2,1,0:T(8,128)(2,1)} %collective-permute-done.1, bf16[32,96,96]{2,1,0:T(8,128)(2,1)} %copy-done.1), kind=kLoop, calls=%fused_computation.13 | loop fusion | flops 1769472 | bytes 2359296 | tf_op jit(solution)/shard_map/add | solution.py:31
  80.7 3.5 %all-gather.2.cloned.1.call-done = bf16[1536,768]{1,0:T(8,128)(2,1)} async-done(((bf16[192,768]{1,0:T(8,128)(2,1)}), bf16[1536,768]{1,0:T(8,128)(2,1)}) %all-gather.2.cloned.1.call-update) | async-done | bytes 2359312 | tf_op jit(solution)/shard_map/all_gather | solution.py:17
  84.3 1.9 %collective-permute-start.3 = (bf16[1536,768]{1,0:T(8,128)(2,1)}, bf16[1536,768]{1,0:T(8,128)(2,1)}, u32[]{:S(2)}, u32[]{:S(2)}) collective-permute-start(bf16[1536,768]{1,0:T(8,128)(2,1)} %all-gather.2.cloned.1.call-done), channel_id=1, source_target_pairs={{0,4},{4,0},{1,5},{5,1},{2,6},{6,2},{3,7},{7,3},{8,12},{12,8},{9,1... | collective-permute-start | bytes 7077896 | tf_op jit(solution)/shard_map/ppermute | solution.py:39
  86.2 2.4 %fusion.2 = f32[32,104,96]{1,2,0:T(8,128)} fusion(bf16[104,32,96]{0,2,1:T(8,128)(2,1)S(1)} %bitcast.46, bf16[104,32,96]{0,2,1:T(8,128)(2,1)S(1)} %bitcast.41, bf16[104,32,96]{0,2,1:T(8,128)(2,1)S(1)} %bitcast.44, pred[104,104]{1,0:T(8,128)(4,1)S(1)} %iota_compare_fusion), kind=kOutput, calls=%fused_computation.15 | convolution fusion | flops 133599232 | bytes 3205696 | tf_op jit(solution)/shard_map/hts,shd->thd/dot_general | solution.py:50
  88.6 2.0 %multiply_reduce_fusion = (f32[104]{0:T(128)S(1)}, f32[104,32,96]{0,2,1:T(8,128)S(1)}) fusion(bf16[32,96,96]{2,1,0:T(8,128)(2,1)S(1)} %convert_add_fusion, bf16[104,32,96]{0,2,1:T(8,128)(2,1)S(1)} %bitcast.42, f32[32,104,96]{1,2,0:T(8,128)} %fusion.2), kind=kOutput, calls=%fused_computation.12 | convolution fusion | flops 62300056 | bytes 3785120 | tf_op jit(solution)/shard_map/thd,hde->the/dot_general | solution.py:51
  90.6 0.5 copy.23
  91.5 2.5 %collective-permute-start.6 = (bf16[104,3072]{1,0:T(8,128)(2,1)S(1)}, bf16[104,3072]{1,0:T(8,128)(2,1)S(1)}, u32[]{:S(2)}, u32[]{:S(2)}) collective-permute-start(bf16[104,3072]{1,0:T(8,128)(2,1)S(1)} %multiply_convert_fusion.1), channel_id=1, source_target_pairs={{0,1},{1,2},{2,3},{3,0},{4,5},{5,6},{6,7},{7,4},{8,9},{9,10},{10,1... | collective-permute-start | bytes 1916936 | tf_op jit(solution)/shard_map/ppermute | solution.py:57
  94.0 3.4 %collective-permute-start.4 = (bf16[104,3072]{1,0:T(8,128)(2,1)S(1)}, bf16[104,3072]{1,0:T(8,128)(2,1)S(1)}, u32[]{:S(2)}, u32[]{:S(2)}) collective-permute-start(bf16[104,3072]{1,0:T(8,128)(2,1)S(1)} %multiply_convert_fusion.1), channel_id=1, source_target_pairs={{0,3},{1,0},{2,1},{3,2},{4,7},{5,4},{6,5},{7,6},{8,11},{9,8},{10,9... | collective-permute-start | bytes 1916936 | tf_op jit(solution)/shard_map/ppermute | solution.py:57
  97.5 0.5 multiply_convert_fusion
  98.0 12.3 %collective-permute-done.6 = bf16[104,3072]{1,0:T(8,128)(2,1)S(1)} collective-permute-done((bf16[104,3072]{1,0:T(8,128)(2,1)S(1)}, bf16[104,3072]{1,0:T(8,128)(2,1)S(1)}, u32[]{:S(2)}, u32[]{:S(2)}) %collective-permute-start.6) | collective-permute-done | bytes 639008 | tf_op jit(solution)/shard_map/ppermute | solution.py:57
  110.2 3.7 %collective-permute-start.7 = (bf16[104,1536]{1,0:T(8,128)(2,1)S(1)}, bf16[104,1536]{1,0:T(8,128)(2,1)S(1)}, u32[]{:S(2)}, u32[]{:S(2)}) collective-permute-start(bf16[104,1536]{1,0:T(8,128)(2,1)S(1)} %slice.27), channel_id=1, source_target_pairs={{0,1},{1,2},{2,3},{3,0},{4,5},{5,6},{6,7},{7,4},{8,9},{9,10},{10,1... | collective-permute-start | bytes 958472 | tf_op jit(solution)/shard_map/ppermute | solution.py:57
  114.0 2.2 %collective-permute-start.5 = (bf16[104,1536]{1,0:T(8,128)(2,1)S(1)}, bf16[104,1536]{1,0:T(8,128)(2,1)S(1)}, u32[]{:S(2)}, u32[]{:S(2)}) collective-permute-start(bf16[104,1536]{1,0:T(8,128)(2,1)S(1)} %slice.24), channel_id=1, source_target_pairs={{0,3},{1,0},{2,1},{3,2},{4,7},{5,4},{6,5},{7,6},{8,11},{9,8},{10,9... | collective-permute-start | bytes 958472 | tf_op jit(solution)/shard_map/ppermute | solution.py:57
  116.2 2.0 %broadcast_select_fusion.1 = (bf16[1536,768]{1,0:T(8,128)(2,1)S(1)}, bf16[1536,768]{1,0:T(8,128)(2,1)S(1)}) fusion(bf16[1536,768]{1,0:T(8,128)(2,1)S(1)} %copy-done, bf16[1536,768]{1,0:T(8,128)(2,1)} %collective-permute-done.3, pred[]{:T(512)S(6)} %eq.3), kind=kLoop, calls=%fused_computation.8 | loop fusion | flops 2359296 | bytes 9437185 | tf_op jit(solution)/shard_map/jit(_where)/select_n | solution.py:44
  118.1 0.4 pad_maximum_fusion
  118.6 0.8 constant_dynamic-update-slice_fusion.7
  119.4 0.9 constant_dynamic-update-slice_fusion.6
  120.3 0.5 fusion
  120.7 0.6 collective-permute-done.7
  121.3 0.5 fusion.8
  121.8 4.1 %collective-permute-done.5 = bf16[104,1536]{1,0:T(8,128)(2,1)S(1)} collective-permute-done((bf16[104,1536]{1,0:T(8,128)(2,1)S(1)}, bf16[104,1536]{1,0:T(8,128)(2,1)S(1)}, u32[]{:S(2)}, u32[]{:S(2)}) %collective-permute-start.5) | collective-permute-done | bytes 319520 | tf_op jit(solution)/shard_map/ppermute | solution.py:57
  125.9 0.5 constant_dynamic-update-slice_fusion.5
  126.5 0.9 constant_dynamic-update-slice_fusion.4
  127.4 0.9 constant_dynamic-slice_fusion
  (24 shorter events, 1.0 us)
Async XLA Ops:
  6.5 37.4 %copy-start.2 = (bf16[104,3072]{1,0:T(8,128)(2,1)S(1)}, bf16[104,3072]{1,0:T(8,128)(2,1)}, u32[]{:S(2)}) copy-start(bf16[104,3072]{1,0:T(8,128)(2,1)} %param.7) | copy-start | bytes 1916932
  6.5 77.8 %all-gather.2.cloned.1.call-start = ((), (), s32[]{:S(2)}) async-start(), calls=%async_computation | async-start | bytes 2654208 | tf_op jit(solution)/shard_map/all_gather | solution.py:17
  45.9 17.8 %collective-permute-start = (bf16[32,96,96]{2,1,0:T(8,128)(2,1)}, bf16[32,96,96]{2,1,0:T(8,128)(2,1)S(1)}, u32[]{:S(2)}, u32[]{:S(2)}) collective-permute-start(bf16[32,96,96]{2,1,0:T(8,128)(2,1)} %convolution_convert_fusion), channel_id=1, source_target_pairs={{0,1},{1,2},{2,3},{4,5},{5,6},{6,7},{8,9},{9,10},{10,11},{12,13},{... | collective-permute-start | bytes 1769480 | tf_op jit(solution)/shard_map/ppermute | solution.py:27
  47.2 19.3 %collective-permute-start.1 = (bf16[32,96,96]{2,1,0:T(8,128)(2,1)}, bf16[32,96,96]{2,1,0:T(8,128)(2,1)}, u32[]{:S(2)}, u32[]{:S(2)}) collective-permute-start(bf16[32,96,96]{2,1,0:T(8,128)(2,1)} %convolution_convert_fusion), channel_id=1, source_target_pairs={{0,3},{4,7},{8,11},{12,15},{16,19},{20,23},{24,27},{28,31},{32,35}... | collective-permute-start | bytes 1769480 | tf_op jit(solution)/shard_map/ppermute | solution.py:28
  63.7 2.8 %copy-start.1 = (bf16[32,96,96]{2,1,0:T(8,128)(2,1)}, bf16[32,96,96]{2,1,0:T(8,128)(2,1)S(1)}, u32[]{:S(2)}) copy-start(bf16[32,96,96]{2,1,0:T(8,128)(2,1)S(1)} %collective-permute-done) | copy-start | bytes 1769476
  63.7 15.1 %collective-permute-start.2 = (bf16[32,96,96]{2,1,0:T(8,128)(2,1)S(1)}, bf16[32,96,96]{2,1,0:T(8,128)(2,1)}, u32[]{:S(2)}, u32[]{:S(2)}) collective-permute-start(bf16[32,96,96]{2,1,0:T(8,128)(2,1)S(1)} %collective-permute-done), channel_id=1, source_target_pairs={{1,2},{2,3},{5,6},{6,7},{9,10},{10,11},{13,14},{14,15},{17,18},{18... | collective-permute-start | bytes 1769480 | tf_op jit(solution)/shard_map/ppermute | solution.py:29
  84.3 31.9 %collective-permute-start.3 = (bf16[1536,768]{1,0:T(8,128)(2,1)}, bf16[1536,768]{1,0:T(8,128)(2,1)}, u32[]{:S(2)}, u32[]{:S(2)}) collective-permute-start(bf16[1536,768]{1,0:T(8,128)(2,1)} %all-gather.2.cloned.1.call-done), channel_id=1, source_target_pairs={{0,4},{4,0},{1,5},{5,1},{2,6},{6,2},{3,7},{7,3},{8,12},{12,8},{9,1... | collective-permute-start | bytes 7077896 | tf_op jit(solution)/shard_map/ppermute | solution.py:39
  90.6 0.7 copy-start.3
  91.5 18.7 %collective-permute-start.6 = (bf16[104,3072]{1,0:T(8,128)(2,1)S(1)}, bf16[104,3072]{1,0:T(8,128)(2,1)S(1)}, u32[]{:S(2)}, u32[]{:S(2)}) collective-permute-start(bf16[104,3072]{1,0:T(8,128)(2,1)S(1)} %multiply_convert_fusion.1), channel_id=1, source_target_pairs={{0,1},{1,2},{2,3},{3,0},{4,5},{5,6},{6,7},{7,4},{8,9},{9,10},{10,1... | collective-permute-start | bytes 1916936 | tf_op jit(solution)/shard_map/ppermute | solution.py:57
  94.0 19.9 %collective-permute-start.4 = (bf16[104,3072]{1,0:T(8,128)(2,1)S(1)}, bf16[104,3072]{1,0:T(8,128)(2,1)S(1)}, u32[]{:S(2)}, u32[]{:S(2)}) collective-permute-start(bf16[104,3072]{1,0:T(8,128)(2,1)S(1)} %multiply_convert_fusion.1), channel_id=1, source_target_pairs={{0,3},{1,0},{2,1},{3,2},{4,7},{5,4},{6,5},{7,6},{8,11},{9,8},{10,9... | collective-permute-start | bytes 1916936 | tf_op jit(solution)/shard_map/ppermute | solution.py:57
  97.5 18.7 %copy-start = (bf16[1536,768]{1,0:T(8,128)(2,1)S(1)}, bf16[1536,768]{1,0:T(8,128)(2,1)}, u32[]{:S(2)}) copy-start(bf16[1536,768]{1,0:T(8,128)(2,1)} %all-gather.2.cloned.1.call-done) | copy-start | bytes 7077892
  110.2 11.1 %collective-permute-start.7 = (bf16[104,1536]{1,0:T(8,128)(2,1)S(1)}, bf16[104,1536]{1,0:T(8,128)(2,1)S(1)}, u32[]{:S(2)}, u32[]{:S(2)}) collective-permute-start(bf16[104,1536]{1,0:T(8,128)(2,1)S(1)} %slice.27), channel_id=1, source_target_pairs={{0,1},{1,2},{2,3},{3,0},{4,5},{5,6},{6,7},{7,4},{8,9},{9,10},{10,1... | collective-permute-start | bytes 958472 | tf_op jit(solution)/shard_map/ppermute | solution.py:57
  114.0 12.0 %collective-permute-start.5 = (bf16[104,1536]{1,0:T(8,128)(2,1)S(1)}, bf16[104,1536]{1,0:T(8,128)(2,1)S(1)}, u32[]{:S(2)}, u32[]{:S(2)}) collective-permute-start(bf16[104,1536]{1,0:T(8,128)(2,1)S(1)} %slice.24), channel_id=1, source_target_pairs={{0,3},{1,0},{2,1},{3,2},{4,7},{5,4},{6,5},{7,6},{8,11},{9,8},{10,9... | collective-permute-start | bytes 958472 | tf_op jit(solution)/shard_map/ppermute | solution.py:57
Sparse Core Ops, SparseCore 0:
  42.6 41.6 all-gather.1

commit v5 on v4

--- a/solution.py
+++ b/solution.py
@@ -13,7 +13,7 @@
     def on_device(queries, keys, values, norm_gain, out_weight):
         rows, cols = out_weight.shape
         half = out_weight
-        for axis in ("z", "y"):
+        for axis in ("y", "z"):
             half = lax.all_gather(half, axis, axis=0, tiled=True)
 
         tok_rows = queries.shape[0]
@@ -35,14 +35,6 @@
                 prefix_f32 = prefix_f32 + lax.ppermute(state_bf, "ctx", pairs).astype(jnp.float32)
         prefix_state = prefix_f32.astype(jnp.bfloat16)
 
-        half, _ = lax.optimization_barrier((half, prefix_f32))
-        other = lax.ppermute(half, "core", [(0, 1), (1, 0)])
-        mine_first = lax.axis_index("core") == 0
-        half = half.reshape(-1, 1, rows, cols)
-        other = other.reshape(-1, 1, rows, cols)
-        weight_block = jnp.concatenate(
-            [jnp.where(mine_first, half, other), jnp.where(mine_first, other, half)], axis=1
-        ).reshape(-1, cols)
 
         scores = jnp.einsum("thd,shd->hts", q_heads, k_heads, preferred_element_type=jnp.float32)
         causal = jnp.arange(tok_rows)[:, None] >= jnp.arange(tok_rows)[None, :]
@@ -52,6 +44,18 @@
         attn = (intra + inter).reshape(tok_rows, HEADS * HEAD_DIM)
         mean_sq = jnp.mean(attn * attn, axis=-1, keepdims=True)
         normed = (attn * lax.rsqrt(mean_sq + 1e-05) * norm_gain).astype(jnp.bfloat16)
+
+        half, _ = lax.optimization_barrier((half, normed))
+        other = lax.ppermute(half, "core", [(0, 1), (1, 0)])
+        mine_first = lax.axis_index("core") == 0
+
+        def fsdp_order(h):
+            return h.reshape(n_z, n_y, 1, rows, cols).transpose(1, 0, 2, 3, 4)
+
+        half, other = fsdp_order(half), fsdp_order(other)
+        weight_block = jnp.concatenate(
+            [jnp.where(mine_first, half, other), jnp.where(mine_first, other, half)], axis=2
+        ).reshape(-1, cols)
 
         def shift_by(x, s):
             return lax.ppermute(x, "ctx", [(i, (i - s) % n_ctx) for i in range(n_ctx)])

time: 136 us -> 149 us (1.096)
  waiting for transfers between devices: 48.1 us -> 69.1 us
  blocking collectives: 35.9 us -> 28.7 us
  other arithmetic: 5.48 us -> 3.55 us
    all_gather x1, waiting for transfers between devices: 3.55 us -> 29.3 us  [on_device(): half = lax.all_gather(half, axis, axis=0, tiled=True)]
    all_gather x1, blocking collectives: 35.9 us -> 28.7 us  [on_device(): half = lax.all_gather(half, axis, axis=0, tiled=True)]
    ppermute x1, waiting for transfers between devices: 12.3 us -> 8.88 us  [on_device(): forwarded = lax.ppermute(from_prev, 'ctx', [(1, 2), (2, 3)])]
    add x1 -> x0, other arithmetic: 1.94 us -> none  [on_device(): prefix_f32 = prefix_f32 + got.astype(jnp.float32)]
  transfers between devices with their start and end apart: 9 -> 9, of which waited for: 6 -> 5; matrix products, arithmetic and copies ran while one was open for 13% -> 12% of each run, Pallas kernels for 0% -> 0%
where the time goes in v5:
time: 149 us
  waiting for transfers between devices  69.1 us (46%)
  blocking collectives  28.7 us (19%)
  starting transfers between devices  17.4 us (12%)
  between operations  13.7 us (9%)
  matrix products  9.99 us (7%)
  local copies, waits for them, and re-layouts  6.4 us (4%)
  other arithmetic  3.55 us (2%)
    all_gather x1, waiting for transfers between devices, on_device(): half = lax.all_gather(half, axis, axis=0, tiled=True)  29.3 us
    all_gather x1, blocking collectives, on_device(): half = lax.all_gather(half, axis, axis=0, tiled=True)  28.7 us
    ppermute x4, waiting for transfers between devices, shift_by(): return lax.ppermute(x, 'ctx', [(i, (i - s) % n_ctx) for i in range(n_ctx)])  15.5 us
    ppermute x1, waiting for transfers between devices, on_device(): from_prev = lax.ppermute(state_bf, 'ctx', [(0, 1), (1, 2), (2, 3)])  15.3 us
    ppermute x4, starting transfers between devices, shift_by(): return lax.ppermute(x, 'ctx', [(i, (i - s) % n_ctx) for i in range(n_ctx)])  11.7 us
    ppermute x1, waiting for transfers between devices, on_device(): forwarded = lax.ppermute(from_prev, 'ctx', [(1, 2), (2, 3)])  8.88 us
  transfers between devices with their start and end apart: 9, of which 5 were waited for; matrix products, arithmetic and copies ran while one was open for 12% of the time, Pallas kernels for 0%

profile of v5, /device:TPU:6, one launch (start us, length us, event | category | flops | bytes accessed | tf_op | source)
XLA Modules:
  0.0 148.9 jit_solution(2031730720855647792)
XLA Ops:
  6.5 28.7 %all_gather.6 = bf16[128,768]{1,0:T(8,128)(2,1)} all-gather(bf16[16,768]{1,0:T(8,128)(2,1)} %param.9), channel_id=1, replica_groups=mesh['y'=8,'z'=12,'core'=2,'ctx'=4] {'y'}, dimensions={0}, use_global_device_ids=true | all-gather | bytes 221184 | tf_op jit(solution)/shard_map/all_gather | solution.py:17
  35.3 1.5 copy.39
  36.7 0.4 copy.40
  37.1 1.6 %convolution_convert_fusion = bf16[32,96,96]{2,1,0:T(8,128)(2,1)} fusion(bf16[104,32,96]{0,2,1:T(8,128)(2,1)S(1)} %bitcast.46, bf16[104,32,96]{0,2,1:T(8,128)(2,1)S(1)} %bitcast.48), kind=kOutput, calls=%fused_computation.14 | convolution fusion | flops 61636608 | bytes 1867776 | tf_op jit(solution)/shard_map/shd,she->hde/dot_general | solution.py:23
  38.7 1.3 collective-permute-start
  40.0 1.3 collective-permute-start.1
  41.3 15.3 %collective-permute-done = bf16[32,96,96]{2,1,0:T(8,128)(2,1)S(1)} collective-permute-done((bf16[32,96,96]{2,1,0:T(8,128)(2,1)}, bf16[32,96,96]{2,1,0:T(8,128)(2,1)S(1)}, u32[]{:S(2)}, u32[]{:S(2)}) %collective-permute-start) | collective-permute-done | bytes 589856 | tf_op jit(solution)/shard_map/ppermute | solution.py:27
  56.6 1.3 collective-permute-start.2
  57.9 1.5 copy.38
  59.4 2.3 %fusion.2 = f32[32,104,96]{1,2,0:T(8,128)} fusion(bf16[104,32,96]{0,2,1:T(8,128)(2,1)S(1)} %bitcast.49, bf16[104,32,96]{0,2,1:T(8,128)(2,1)S(1)} %bitcast.44, bf16[104,32,96]{0,2,1:T(8,128)(2,1)S(1)} %bitcast.47, pred[104,104]{1,0:T(8,128)(4,1)S(1)} %iota_compare_fusion), kind=kOutput, calls=%fused_computation.15 | convolution fusion | flops 133599232 | bytes 3205696 | tf_op jit(solution)/shard_map/hts,shd->thd/dot_general | solution.py:42
  61.7 8.9 %collective-permute-done.2 = bf16[32,96,96]{2,1,0:T(8,128)(2,1)} collective-permute-done((bf16[32,96,96]{2,1,0:T(8,128)(2,1)S(1)}, bf16[32,96,96]{2,1,0:T(8,128)(2,1)}, u32[]{:S(2)}, u32[]{:S(2)}) %collective-permute-start.2) | collective-permute-done | bytes 589856 | tf_op jit(solution)/shard_map/ppermute | solution.py:29
  70.6 2.5 %multiply_reduce_fusion = (f32[104]{0:T(128)S(1)}, f32[104,32,96]{0,2,1:T(8,128)S(1)}) fusion(bf16[104,32,96]{0,2,1:T(8,128)(2,1)S(1)} %bitcast.45, bf16[32,96,96]{2,1,0:T(8,128)(2,1)} %collective-permute-done.2, bf16[32,96,96]{2,1,0:T(8,128)(2,1)} %collective-permute-done.1, bf16[32,96,96]{2,1,0:T(8,128)(2,1)S(1)} %collective-permute-done, ...), kind=kOutput, calls=%fused_computation.12 | convolution fusion | flops 64069528 | bytes 4964768 | tf_op jit(solution)/shard_map/thd,hde->the/dot_general | solution.py:43
  73.1 0.5 copy.33
  74.0 29.3 %all-gather.2.cloned.1.call-done = bf16[1536,768]{1,0:T(8,128)(2,1)} async-done(((bf16[128,768]{1,0:T(8,128)(2,1)}), bf16[1536,768]{1,0:T(8,128)(2,1)}) %all-gather.2.cloned.1.call-update) | async-done | bytes 2359312 | tf_op jit(solution)/shard_map/all_gather | solution.py:17
  103.3 1.9 %collective-permute-start.3 = (bf16[1536,768]{1,0:T(8,128)(2,1)}, bf16[1536,768]{1,0:T(8,128)(2,1)}, u32[]{:S(2)}, u32[]{:S(2)}) collective-permute-start(bf16[1536,768]{1,0:T(8,128)(2,1)} %all-gather.2.cloned.1.call-done), channel_id=1, source_target_pairs={{0,4},{4,0},{1,5},{5,1},{2,6},{6,2},{3,7},{7,3},{8,12},{12,8},{9,1... | collective-permute-start | bytes 7077896 | tf_op jit(solution)/shard_map/ppermute | solution.py:49
  105.3 2.5 %collective-permute-start.6 = (bf16[104,3072]{1,0:T(8,128)(2,1)S(1)}, bf16[104,3072]{1,0:T(8,128)(2,1)S(1)}, u32[]{:S(2)}, u32[]{:S(2)}) collective-permute-start(bf16[104,3072]{1,0:T(8,128)(2,1)S(1)} %multiply_convert_fusion.1), channel_id=1, source_target_pairs={{0,1},{1,2},{2,3},{3,0},{4,5},{5,6},{6,7},{7,4},{8,9},{9,10},{10,1... | collective-permute-start | bytes 1916936 | tf_op jit(solution)/shard_map/ppermute | solution.py:61
  107.7 3.4 %collective-permute-start.4 = (bf16[104,3072]{1,0:T(8,128)(2,1)S(1)}, bf16[104,3072]{1,0:T(8,128)(2,1)S(1)}, u32[]{:S(2)}, u32[]{:S(2)}) collective-permute-start(bf16[104,3072]{1,0:T(8,128)(2,1)S(1)} %multiply_convert_fusion.1), channel_id=1, source_target_pairs={{0,3},{1,0},{2,1},{3,2},{4,7},{5,4},{6,5},{7,6},{8,11},{9,8},{10,9... | collective-permute-start | bytes 1916936 | tf_op jit(solution)/shard_map/ppermute | solution.py:61
  111.2 0.5 multiply_convert_fusion
  111.7 12.3 %collective-permute-done.6 = bf16[104,3072]{1,0:T(8,128)(2,1)S(1)} collective-permute-done((bf16[104,3072]{1,0:T(8,128)(2,1)S(1)}, bf16[104,3072]{1,0:T(8,128)(2,1)S(1)}, u32[]{:S(2)}, u32[]{:S(2)}) %collective-permute-start.6) | collective-permute-done | bytes 639008 | tf_op jit(solution)/shard_map/ppermute | solution.py:61
  124.0 3.7 %collective-permute-start.7 = (bf16[104,1536]{1,0:T(8,128)(2,1)S(1)}, bf16[104,1536]{1,0:T(8,128)(2,1)S(1)}, u32[]{:S(2)}, u32[]{:S(2)}) collective-permute-start(bf16[104,1536]{1,0:T(8,128)(2,1)S(1)} %slice.27), channel_id=1, source_target_pairs={{0,1},{1,2},{2,3},{3,0},{4,5},{5,6},{6,7},{7,4},{8,9},{9,10},{10,1... | collective-permute-start | bytes 958472 | tf_op jit(solution)/shard_map/ppermute | solution.py:61
  127.7 2.2 %collective-permute-start.5 = (bf16[104,1536]{1,0:T(8,128)(2,1)S(1)}, bf16[104,1536]{1,0:T(8,128)(2,1)S(1)}, u32[]{:S(2)}, u32[]{:S(2)}) collective-permute-start(bf16[104,1536]{1,0:T(8,128)(2,1)S(1)} %slice.24), channel_id=1, source_target_pairs={{0,3},{1,0},{2,1},{3,2},{4,7},{5,4},{6,5},{7,6},{8,11},{9,8},{10,9... | collective-permute-start | bytes 958472 | tf_op jit(solution)/shard_map/ppermute | solution.py:61
  129.9 2.0 %broadcast_select_fusion.1 = (bf16[1536,768]{1,0:T(8,128)(2,1)S(1)}, bf16[1536,768]{1,0:T(8,128)(2,1)S(1)}) fusion(bf16[1536,768]{1,0:T(8,128)(2,1)S(1)} %copy-done, bf16[1536,768]{1,0:T(8,128)(2,1)} %collective-permute-done.3, pred[]{:T(512)S(6)} %eq.3), kind=kLoop, calls=%fused_computation.8 | loop fusion | flops 2359296 | bytes 9437185 | tf_op jit(solution)/shard_map/jit(_where)/select_n | solution.py:57
  131.9 0.4 pad_maximum_fusion
  132.3 0.7 copy.34
  133.0 0.8 constant_dynamic-update-slice_fusion.7
  133.9 0.9 constant_dynamic-update-slice_fusion.6
  134.7 0.5 fusion
  135.9 0.5 fusion.7
  136.4 3.3 %collective-permute-done.5 = bf16[104,1536]{1,0:T(8,128)(2,1)S(1)} collective-permute-done((bf16[104,1536]{1,0:T(8,128)(2,1)S(1)}, bf16[104,1536]{1,0:T(8,128)(2,1)S(1)}, u32[]{:S(2)}, u32[]{:S(2)}) %collective-permute-start.5) | collective-permute-done | bytes 319520 | tf_op jit(solution)/shard_map/ppermute | solution.py:61
  139.7 0.5 constant_dynamic-update-slice_fusion.5
  140.2 0.9 constant_dynamic-update-slice_fusion.4
  141.1 0.9 constant_dynamic-slice_fusion
  (24 shorter events, 1.3 us)
Async XLA Ops:
  6.5 30.2 %copy-start.1 = (bf16[104,3072]{1,0:T(8,128)(2,1)S(1)}, bf16[104,3072]{1,0:T(8,128)(2,1)}, u32[]{:S(2)}) copy-start(bf16[104,3072]{1,0:T(8,128)(2,1)} %param.7) | copy-start | bytes 1916932
  6.5 96.8 %all-gather.2.cloned.1.call-start = ((), (), s32[]{:S(2)}) async-start(), calls=%async_computation | async-start | bytes 2555904 | tf_op jit(solution)/shard_map/all_gather | solution.py:17
  38.7 17.9 %collective-permute-start = (bf16[32,96,96]{2,1,0:T(8,128)(2,1)}, bf16[32,96,96]{2,1,0:T(8,128)(2,1)S(1)}, u32[]{:S(2)}, u32[]{:S(2)}) collective-permute-start(bf16[32,96,96]{2,1,0:T(8,128)(2,1)} %convolution_convert_fusion), channel_id=1, source_target_pairs={{0,1},{1,2},{2,3},{4,5},{5,6},{6,7},{8,9},{9,10},{10,11},{12,13},{... | collective-permute-start | bytes 1769480 | tf_op jit(solution)/shard_map/ppermute | solution.py:27
  40.0 21.7 %collective-permute-start.1 = (bf16[32,96,96]{2,1,0:T(8,128)(2,1)}, bf16[32,96,96]{2,1,0:T(8,128)(2,1)}, u32[]{:S(2)}, u32[]{:S(2)}) collective-permute-start(bf16[32,96,96]{2,1,0:T(8,128)(2,1)} %convolution_convert_fusion), channel_id=1, source_target_pairs={{0,3},{4,7},{8,11},{12,15},{16,19},{20,23},{24,27},{28,31},{32,35}... | collective-permute-start | bytes 1769480 | tf_op jit(solution)/shard_map/ppermute | solution.py:28
  56.6 14.0 %collective-permute-start.2 = (bf16[32,96,96]{2,1,0:T(8,128)(2,1)S(1)}, bf16[32,96,96]{2,1,0:T(8,128)(2,1)}, u32[]{:S(2)}, u32[]{:S(2)}) collective-permute-start(bf16[32,96,96]{2,1,0:T(8,128)(2,1)S(1)} %collective-permute-done), channel_id=1, source_target_pairs={{1,2},{2,3},{5,6},{6,7},{9,10},{10,11},{13,14},{14,15},{17,18},{18... | collective-permute-start | bytes 1769480 | tf_op jit(solution)/shard_map/ppermute | solution.py:29
  73.1 0.7 copy-start.2
  103.3 26.5 %collective-permute-start.3 = (bf16[1536,768]{1,0:T(8,128)(2,1)}, bf16[1536,768]{1,0:T(8,128)(2,1)}, u32[]{:S(2)}, u32[]{:S(2)}) collective-permute-start(bf16[1536,768]{1,0:T(8,128)(2,1)} %all-gather.2.cloned.1.call-done), channel_id=1, source_target_pairs={{0,4},{4,0},{1,5},{5,1},{2,6},{6,2},{3,7},{7,3},{8,12},{12,8},{9,1... | collective-permute-start | bytes 7077896 | tf_op jit(solution)/shard_map/ppermute | solution.py:49
  105.3 18.7 %collective-permute-start.6 = (bf16[104,3072]{1,0:T(8,128)(2,1)S(1)}, bf16[104,3072]{1,0:T(8,128)(2,1)S(1)}, u32[]{:S(2)}, u32[]{:S(2)}) collective-permute-start(bf16[104,3072]{1,0:T(8,128)(2,1)S(1)} %multiply_convert_fusion.1), channel_id=1, source_target_pairs={{0,1},{1,2},{2,3},{3,0},{4,5},{5,6},{6,7},{7,4},{8,9},{9,10},{10,1... | collective-permute-start | bytes 1916936 | tf_op jit(solution)/shard_map/ppermute | solution.py:61
  107.7 19.9 %collective-permute-start.4 = (bf16[104,3072]{1,0:T(8,128)(2,1)S(1)}, bf16[104,3072]{1,0:T(8,128)(2,1)S(1)}, u32[]{:S(2)}, u32[]{:S(2)}) collective-permute-start(bf16[104,3072]{1,0:T(8,128)(2,1)S(1)} %multiply_convert_fusion.1), channel_id=1, source_target_pairs={{0,3},{1,0},{2,1},{3,2},{4,7},{5,4},{6,5},{7,6},{8,11},{9,8},{10,9... | collective-permute-start | bytes 1916936 | tf_op jit(solution)/shard_map/ppermute | solution.py:61
  111.2 18.7 %copy-start = (bf16[1536,768]{1,0:T(8,128)(2,1)S(1)}, bf16[1536,768]{1,0:T(8,128)(2,1)}, u32[]{:S(2)}) copy-start(bf16[1536,768]{1,0:T(8,128)(2,1)} %all-gather.2.cloned.1.call-done) | copy-start | bytes 7077892
  124.0 11.9 %collective-permute-start.7 = (bf16[104,1536]{1,0:T(8,128)(2,1)S(1)}, bf16[104,1536]{1,0:T(8,128)(2,1)S(1)}, u32[]{:S(2)}, u32[]{:S(2)}) collective-permute-start(bf16[104,1536]{1,0:T(8,128)(2,1)S(1)} %slice.27), channel_id=1, source_target_pairs={{0,1},{1,2},{2,3},{3,0},{4,5},{5,6},{6,7},{7,4},{8,9},{9,10},{10,1... | collective-permute-start | bytes 958472 | tf_op jit(solution)/shard_map/ppermute | solution.py:61
  127.7 12.0 %collective-permute-start.5 = (bf16[104,1536]{1,0:T(8,128)(2,1)S(1)}, bf16[104,1536]{1,0:T(8,128)(2,1)S(1)}, u32[]{:S(2)}, u32[]{:S(2)}) collective-permute-start(bf16[104,1536]{1,0:T(8,128)(2,1)S(1)} %slice.24), channel_id=1, source_target_pairs={{0,3},{1,0},{2,1},{3,2},{4,7},{5,4},{6,5},{7,6},{8,11},{9,8},{10,9... | collective-permute-start | bytes 958472 | tf_op jit(solution)/shard_map/ppermute | solution.py:61
Sparse Core Ops, SparseCore 0:
  35.4 67.9 all-gather.1

commit v6 on v3

--- a/solution.py
+++ b/solution.py
@@ -46,25 +46,24 @@
         def shift_by(x, s):
             return lax.ppermute(x, "ctx", [(i, (i - s) % n_ctx) for i in range(n_ctx)])
 
+        position = lax.axis_index("ctx")
+
+        def place(seq, block, s, col=0):
+            row = ((position + s) % n_ctx) * tok_rows
+            return lax.dynamic_update_slice(seq, block, (row, col))
+
         half = HEADS * HEAD_DIM // 2
-        outs = [None] * n_ctx
-        outs[0] = jnp.dot(normed, weight_block, preferred_element_type=jnp.float32)
+        seq = place(jnp.zeros((n_ctx * tok_rows, HEADS * HEAD_DIM), jnp.bfloat16), normed, 0)
         ahead, behind = normed, normed
         for s in range(1, n_ctx // 2 + 1):
             if 2 * s < n_ctx:
                 ahead = shift_by(ahead, 1)
                 behind = shift_by(behind, -1)
-                outs[s] = jnp.dot(ahead, weight_block, preferred_element_type=jnp.float32)
-                outs[n_ctx - s] = jnp.dot(behind, weight_block, preferred_element_type=jnp.float32)
+                seq = place(place(seq, ahead, s), behind, n_ctx - s)
             else:
-                left = shift_by(ahead[:, :half], 1)
-                right = shift_by(behind[:, half:], -1)
-                outs[s] = jnp.dot(left, weight_block[:half], preferred_element_type=jnp.float32) + jnp.dot(
-                    right, weight_block[half:], preferred_element_type=jnp.float32
-                )
-        stacked = jnp.concatenate(outs + outs, axis=0).astype(jnp.bfloat16)
-        position = lax.axis_index("ctx")
-        return lax.dynamic_slice_in_dim(stacked, (n_ctx - position) * tok_rows, n_ctx * tok_rows, axis=0)
+                seq = place(seq, shift_by(ahead[:, :half], 1), s)
+                seq = place(seq, shift_by(behind[:, half:], -1), s, half)
+        return jnp.dot(seq, weight_block, preferred_element_type=jnp.float32).astype(jnp.bfloat16)
 
     return on_device
 

time: 123 us -> 134 us (1.089)
  the two profiles are of different devices: /device:TPU:6 before, /device:TPU:40 now
where the time goes in v6:
time: 134 us; the launch traced here: 133 us
  blocking collectives  39.5 us (29%)
  starting transfers between devices  35 us (26%)
  waiting for transfers between devices  22.5 us (17%)
  between operations  13.6 us (10%)
  matrix products  12.6 us (9%)
  local copies, waits for them, and re-layouts  8.94 us (7%)
    all_gather x2, blocking collectives, on_device(): weight_block = lax.all_gather(weight_block, axis, axis=0, tiled=True)  39.5 us
    ppermute x4, starting transfers between devices, shift_by(): return lax.ppermute(x, 'ctx', [(i, (i - s) % n_ctx) for i in range(n_ctx)])  26.6 us
    ppermute x4, waiting for transfers between devices, shift_by(): return lax.ppermute(x, 'ctx', [(i, (i - s) % n_ctx) for i in range(n_ctx)])  13.6 us
    ppermute x1, waiting for transfers between devices, on_device(): from_prev = lax.ppermute(state_bf, 'ctx', [(0, 1), (1, 2), (2, 3)])  8.89 us
    dot_general x1, matrix products, on_device(): jnp.dot(seq, weight_block, preferred_element_type=jnp.float32)  6.09 us
    ppermute x1, starting transfers between devices, on_device(): from_first = lax.ppermute(state_bf, 'ctx', [(0, 3)])  3.49 us
    ppermute x1, starting transfers between devices, on_device(): from_prev = lax.ppermute(state_bf, 'ctx', [(0, 1), (1, 2), (2, 3)])  3.43 us
    dynamic_update_slice x4, local copies, waits for them, and re-layouts, place(): return lax.dynamic_update_slice(seq, block, (row, col))  3.34 us
  transfers between devices with their start and end apart: 8, of which 5 were waited for; matrix products, arithmetic and copies ran while one was open for 12% of the time, Pallas kernels for 0%

profile of v6, /device:TPU:40, one launch (start us, length us, event | category | flops | bytes accessed | tf_op | source)
XLA Modules:
  0.0 133.2 jit_solution(9204611344466383694)
XLA Ops:
  6.5 0.0 all-gather.2.cloned.1.call-start
  6.5 2.2 %all_gather.9 = bf16[32,768]{1,0:T(8,128)(2,1)S(1)} all-gather(bf16[16,768]{1,0:T(8,128)(2,1)} %param.9), channel_id=1, replica_groups=mesh['y'=8,'z'=12,'core'=2,'ctx'=4] {'core'}, dimensions={0}, use_global_device_ids=true | all-gather | bytes 73728 | tf_op jit(solution)/shard_map/all_gather | solution.py:16
  8.7 37.3 %all_gather.10 = bf16[384,768]{1,0:T(8,128)(2,1)} all-gather(bf16[32,768]{1,0:T(8,128)(2,1)S(1)} %all_gather.9), channel_id=1, replica_groups=mesh['y'=8,'z'=12,'core'=2,'ctx'=4] {'z'}, dimensions={0}, use_global_device_ids=true | all-gather | bytes 638976 | tf_op jit(solution)/shard_map/all_gather | solution.py:16
  46.0 0.0 all-gather.2.cloned.1.call-update
  46.0 1.5 %copy.26 = bf16[104,3072]{0,1:T(8,128)(2,1)S(1)} copy(bf16[104,3072]{1,0:T(8,128)(2,1)} %param.6) | data formatting | bytes 1277952 | tf_op jit(solution)/shard_map/reshape | solution.py:20
  47.5 0.4 copy.27
  47.9 1.6 %convolution_convert_fusion = bf16[32,96,96]{2,1,0:T(8,128)(2,1)} fusion(bf16[104,32,96]{0,2,1:T(8,128)(2,1)S(1)} %bitcast.18, bf16[104,32,96]{0,2,1:T(8,128)(2,1)S(1)} %bitcast.20), kind=kOutput, calls=%fused_computation.4 | convolution fusion | flops 61636608 | bytes 1867776 | tf_op jit(solution)/shard_map/shd,she->hde/dot_general | solution.py:22
  49.5 3.4 %collective-permute-start = (bf16[32,96,96]{2,1,0:T(8,128)(2,1)}, bf16[32,96,96]{2,1,0:T(8,128)(2,1)S(1)}, u32[]{:S(2)}, u32[]{:S(2)}) collective-permute-start(bf16[32,96,96]{2,1,0:T(8,128)(2,1)} %convolution_convert_fusion), channel_id=1, source_target_pairs={{0,1},{1,2},{2,3},{4,5},{5,6},{6,7},{8,9},{9,10},{10,11},{12,13},{... | collective-permute-start | bytes 1769480 | tf_op jit(solution)/shard_map/ppermute | solution.py:26
  52.9 3.5 %collective-permute-start.1 = (bf16[32,96,96]{2,1,0:T(8,128)(2,1)}, bf16[32,96,96]{2,1,0:T(8,128)(2,1)}, u32[]{:S(2)}, u32[]{:S(2)}) collective-permute-start(bf16[32,96,96]{2,1,0:T(8,128)(2,1)} %convolution_convert_fusion), channel_id=1, source_target_pairs={{0,3},{4,7},{8,11},{12,15},{16,19},{20,23},{24,27},{28,31},{32,35}... | collective-permute-start | bytes 1769480 | tf_op jit(solution)/shard_map/ppermute | solution.py:27
  56.4 8.9 %collective-permute-done = bf16[32,96,96]{2,1,0:T(8,128)(2,1)S(1)} collective-permute-done((bf16[32,96,96]{2,1,0:T(8,128)(2,1)}, bf16[32,96,96]{2,1,0:T(8,128)(2,1)S(1)}, u32[]{:S(2)}, u32[]{:S(2)}) %collective-permute-start) | collective-permute-done | bytes 589856 | tf_op jit(solution)/shard_map/ppermute | solution.py:26
  65.3 1.5 %collective-permute-start.2 = (bf16[32,96,96]{2,1,0:T(8,128)(2,1)S(1)}, bf16[32,96,96]{2,1,0:T(8,128)(2,1)}, u32[]{:S(2)}, u32[]{:S(2)}) collective-permute-start(bf16[32,96,96]{2,1,0:T(8,128)(2,1)S(1)} %collective-permute-done), channel_id=1, source_target_pairs={{1,2},{2,3},{5,6},{6,7},{9,10},{10,11},{13,14},{14,15},{17,18},{18... | collective-permute-start | bytes 1769480 | tf_op jit(solution)/shard_map/ppermute | solution.py:28
  66.8 1.5 %copy.25 = bf16[104,3072]{0,1:T(8,128)(2,1)S(1)} copy(bf16[104,3072]{1,0:T(8,128)(2,1)} %param.5) | data formatting | bytes 1277952 | tf_op jit(solution)/shard_map/reshape | solution.py:19
  68.3 2.3 %fusion = f32[32,104,96]{1,2,0:T(8,128)} fusion(bf16[104,32,96]{0,2,1:T(8,128)(2,1)S(1)} %bitcast.21, bf16[104,32,96]{0,2,1:T(8,128)(2,1)S(1)} %bitcast.16, bf16[104,32,96]{0,2,1:T(8,128)(2,1)S(1)} %bitcast.19, pred[104,104]{1,0:T(8,128)(4,1)S(1)} %iota_compare_fusion), kind=kOutput, calls=%fused_computation.6 | convolution fusion | flops 133599232 | bytes 3205696 | tf_op jit(solution)/shard_map/hts,shd->thd/dot_general | solution.py:40
  70.7 0.0 collective-permute-done.1
  70.7 0.0 collective-permute-done.2
  70.7 2.6 %multiply_reduce_fusion = (f32[104]{0:T(128)S(1)}, f32[104,32,96]{0,2,1:T(8,128)S(1)}) fusion(bf16[104,32,96]{0,2,1:T(8,128)(2,1)S(1)} %bitcast.17, bf16[32,96,96]{2,1,0:T(8,128)(2,1)} %collective-permute-done.2, bf16[32,96,96]{2,1,0:T(8,128)(2,1)} %collective-permute-done.1, bf16[32,96,96]{2,1,0:T(8,128)(2,1)S(1)} %collective-permute-done, ...), kind=kOutput, calls=%fused_computation.2 | convolution fusion | flops 64069528 | bytes 4964768 | tf_op jit(solution)/shard_map/thd,hde->the/dot_general | solution.py:41
  73.2 0.5 copy.23
  73.7 1.8 %broadcast_in_dim.15 = bf16[416,3072]{1,0:T(8,128)(2,1)} broadcast(bf16[]{:T(256)} %constant.39.clone.1), dimensions={} | broadcast | bytes 2555906 | tf_op jit(solution)/shard_map/broadcast_in_dim | solution.py:56
  75.5 1.1 constant_dynamic-update-slice_fusion.3
  76.6 17.1 %collective-permute-start.3 = (bf16[104,3072]{1,0:T(8,128)(2,1)S(1)}, bf16[104,3072]{1,0:T(8,128)(2,1)S(1)}, u32[]{:S(2)}, u32[]{:S(2)}) collective-permute-start(bf16[104,3072]{1,0:T(8,128)(2,1)S(1)} %get-tuple-element.6), channel_id=1, source_target_pairs={{0,3},{1,0},{2,1},{3,2},{4,7},{5,4},{6,5},{7,6},{8,11},{9,8},{10,9... | collective-permute-start | bytes 1916936 | tf_op jit(solution)/shard_map/ppermute | solution.py:47
  93.8 1.9 %collective-permute-start.4 = (bf16[104,3072]{1,0:T(8,128)(2,1)S(1)}, bf16[104,3072]{1,0:T(8,128)(2,1)S(1)}, u32[]{:S(2)}, u32[]{:S(2)}) collective-permute-start(bf16[104,3072]{1,0:T(8,128)(2,1)S(1)} %get-tuple-element.6), channel_id=1, source_target_pairs={{0,1},{1,2},{2,3},{3,0},{4,5},{5,6},{6,7},{7,4},{8,9},{9,10},{10,1... | collective-permute-start | bytes 1916936 | tf_op jit(solution)/shard_map/ppermute | solution.py:47
  95.7 7.8 %collective-permute-done.3 = bf16[104,3072]{1,0:T(8,128)(2,1)S(1)} collective-permute-done((bf16[104,3072]{1,0:T(8,128)(2,1)S(1)}, bf16[104,3072]{1,0:T(8,128)(2,1)S(1)}, u32[]{:S(2)}, u32[]{:S(2)}) %collective-permute-start.3) | collective-permute-done | bytes 639008 | tf_op jit(solution)/shard_map/ppermute | solution.py:47
  103.6 5.6 %collective-permute-start.5 = (bf16[104,1536]{1,0:T(8,128)(2,1)S(1)}, bf16[104,1536]{1,0:T(8,128)(2,1)S(1)}, u32[]{:S(2)}, u32[]{:S(2)}) collective-permute-start(bf16[104,1536]{1,0:T(8,128)(2,1)S(1)} %slice.8), channel_id=1, source_target_pairs={{0,3},{1,0},{2,1},{3,2},{4,7},{5,4},{6,5},{7,6},{8,11},{9,8},{10,9... | collective-permute-start | bytes 958472 | tf_op jit(solution)/shard_map/ppermute | solution.py:47
  109.2 0.2 collective-permute-done.4
  109.4 1.9 %collective-permute-start.6 = (bf16[104,1536]{1,0:T(8,128)(2,1)S(1)}, bf16[104,1536]{1,0:T(8,128)(2,1)S(1)}, u32[]{:S(2)}, u32[]{:S(2)}) collective-permute-start(bf16[104,1536]{1,0:T(8,128)(2,1)S(1)} %slice.9), channel_id=1, source_target_pairs={{0,1},{1,2},{2,3},{3,0},{4,5},{5,6},{6,7},{7,4},{8,9},{9,10},{10,1... | collective-permute-start | bytes 958472 | tf_op jit(solution)/shard_map/ppermute | solution.py:47
  111.3 0.9 constant_dynamic-update-slice_fusion.2
  112.2 0.9 constant_dynamic-update-slice_fusion.1
  113.1 0.5 collective-permute-done.5
  113.6 0.8 constant_dynamic-update-slice_fusion
  114.4 5.1 %collective-permute-done.6 = bf16[104,1536]{1,0:T(8,128)(2,1)S(1)} collective-permute-done((bf16[104,1536]{1,0:T(8,128)(2,1)S(1)}, bf16[104,1536]{1,0:T(8,128)(2,1)S(1)}, u32[]{:S(2)}, u32[]{:S(2)}) %collective-permute-start.6) | collective-permute-done | bytes 319520 | tf_op jit(solution)/shard_map/ppermute | solution.py:47
  119.5 0.8 constant_dynamic-update-slice_fusion.4
  120.3 6.1 %convolution_convert_fusion.1 = bf16[416,768]{1,0:T(8,128)(2,1)} fusion(bf16[416,3072]{1,0:T(8,128)(2,1)} %constant_dynamic-update-slice_fusion.4, bf16[3072,768]{1,0:T(8,128)(2,1)} %all-gather.2.cloned.1.call-done), kind=kOutput, calls=%fused_computation.5 | convolution fusion | flops 1963253760 | bytes 7913472 | tf_op jit(solution)/shard_map/dot_general | solution.py:66
  (9 shorter events, 0.1 us)
Async XLA Ops:
  6.5 41.0 %copy-start = (bf16[104,3072]{1,0:T(8,128)(2,1)S(1)}, bf16[104,3072]{1,0:T(8,128)(2,1)}, u32[]{:S(2)}) copy-start(bf16[104,3072]{1,0:T(8,128)(2,1)} %param.7) | copy-start | bytes 1916932
  6.5 113.7 %all-gather.2.cloned.1.call-start = ((), (), s32[]{:S(2)}) async-start(), calls=%async_computation | async-start | bytes 5308416 | tf_op jit(solution)/shard_map/all_gather | solution.py:16
  49.5 15.8 %collective-permute-start = (bf16[32,96,96]{2,1,0:T(8,128)(2,1)}, bf16[32,96,96]{2,1,0:T(8,128)(2,1)S(1)}, u32[]{:S(2)}, u32[]{:S(2)}) collective-permute-start(bf16[32,96,96]{2,1,0:T(8,128)(2,1)} %convolution_convert_fusion), channel_id=1, source_target_pairs={{0,1},{1,2},{2,3},{4,5},{5,6},{6,7},{8,9},{9,10},{10,11},{12,13},{... | collective-permute-start | bytes 1769480 | tf_op jit(solution)/shard_map/ppermute | solution.py:26
  52.9 17.8 %collective-permute-start.1 = (bf16[32,96,96]{2,1,0:T(8,128)(2,1)}, bf16[32,96,96]{2,1,0:T(8,128)(2,1)}, u32[]{:S(2)}, u32[]{:S(2)}) collective-permute-start(bf16[32,96,96]{2,1,0:T(8,128)(2,1)} %convolution_convert_fusion), channel_id=1, source_target_pairs={{0,3},{4,7},{8,11},{12,15},{16,19},{20,23},{24,27},{28,31},{32,35}... | collective-permute-start | bytes 1769480 | tf_op jit(solution)/shard_map/ppermute | solution.py:27
  65.3 5.4 %collective-permute-start.2 = (bf16[32,96,96]{2,1,0:T(8,128)(2,1)S(1)}, bf16[32,96,96]{2,1,0:T(8,128)(2,1)}, u32[]{:S(2)}, u32[]{:S(2)}) collective-permute-start(bf16[32,96,96]{2,1,0:T(8,128)(2,1)S(1)} %collective-permute-done), channel_id=1, source_target_pairs={{1,2},{2,3},{5,6},{6,7},{9,10},{10,11},{13,14},{14,15},{17,18},{18... | collective-permute-start | bytes 1769480 | tf_op jit(solution)/shard_map/ppermute | solution.py:28
  73.2 2.3 %copy-start.1 = (f32[3072]{0:T(1024)S(1)}, f32[3072]{0:T(1024)}, u32[]{:S(2)}) copy-start(f32[3072]{0:T(1024)} %param.8) | copy-start | bytes 36868
  76.6 26.9 %collective-permute-start.3 = (bf16[104,3072]{1,0:T(8,128)(2,1)S(1)}, bf16[104,3072]{1,0:T(8,128)(2,1)S(1)}, u32[]{:S(2)}, u32[]{:S(2)}) collective-permute-start(bf16[104,3072]{1,0:T(8,128)(2,1)S(1)} %get-tuple-element.6), channel_id=1, source_target_pairs={{0,3},{1,0},{2,1},{3,2},{4,7},{5,4},{6,5},{7,6},{8,11},{9,8},{10,9... | collective-permute-start | bytes 1916936 | tf_op jit(solution)/shard_map/ppermute | solution.py:47
  93.8 15.6 %collective-permute-start.4 = (bf16[104,3072]{1,0:T(8,128)(2,1)S(1)}, bf16[104,3072]{1,0:T(8,128)(2,1)S(1)}, u32[]{:S(2)}, u32[]{:S(2)}) collective-permute-start(bf16[104,3072]{1,0:T(8,128)(2,1)S(1)} %get-tuple-element.6), channel_id=1, source_target_pairs={{0,1},{1,2},{2,3},{3,0},{4,5},{5,6},{6,7},{7,4},{8,9},{9,10},{10,1... | collective-permute-start | bytes 1916936 | tf_op jit(solution)/shard_map/ppermute | solution.py:47
  103.6 10.1 %collective-permute-start.5 = (bf16[104,1536]{1,0:T(8,128)(2,1)S(1)}, bf16[104,1536]{1,0:T(8,128)(2,1)S(1)}, u32[]{:S(2)}, u32[]{:S(2)}) collective-permute-start(bf16[104,1536]{1,0:T(8,128)(2,1)S(1)} %slice.8), channel_id=1, source_target_pairs={{0,3},{1,0},{2,1},{3,2},{4,7},{5,4},{6,5},{7,6},{8,11},{9,8},{10,9... | collective-permute-start | bytes 958472 | tf_op jit(solution)/shard_map/ppermute | solution.py:47
  109.4 10.1 %collective-permute-start.6 = (bf16[104,1536]{1,0:T(8,128)(2,1)S(1)}, bf16[104,1536]{1,0:T(8,128)(2,1)S(1)}, u32[]{:S(2)}, u32[]{:S(2)}) collective-permute-start(bf16[104,1536]{1,0:T(8,128)(2,1)S(1)} %slice.9), channel_id=1, source_target_pairs={{0,1},{1,2},{2,3},{3,0},{4,5},{5,6},{6,7},{7,4},{8,9},{9,10},{10,1... | collective-permute-start | bytes 958472 | tf_op jit(solution)/shard_map/ppermute | solution.py:47
Sparse Core Ops, SparseCore 0:
  46.2 57.5 all-gather.1

commit v7 on v3

--- a/solution.py
+++ b/solution.py
@@ -9,11 +9,12 @@
 HEAD_DIM = 96
 
 
-def make_on_device(n_ctx, n_core):
+def make_on_device(n_ctx, n_core, n_y, n_z):
     def on_device(queries, keys, values, norm_gain, out_weight):
-        weight_block = out_weight
-        for axis in ("core", "z", "y"):
-            weight_block = lax.all_gather(weight_block, axis, axis=0, tiled=True)
+        rows, cols = out_weight.shape
+        w_mine = out_weight
+        for axis in ("z", "y"):
+            w_mine = lax.all_gather(w_mine, axis, axis=0, tiled=True)
 
         tok_rows = queries.shape[0]
         q_heads = queries.reshape(tok_rows, HEADS, HEAD_DIM)
@@ -48,20 +49,32 @@
 
         half = HEADS * HEAD_DIM // 2
         outs = [None] * n_ctx
-        outs[0] = jnp.dot(normed, weight_block, preferred_element_type=jnp.float32)
         ahead, behind = normed, normed
+        received = [normed] + [None] * (n_ctx - 1)
         for s in range(1, n_ctx // 2 + 1):
             if 2 * s < n_ctx:
                 ahead = shift_by(ahead, 1)
                 behind = shift_by(behind, -1)
-                outs[s] = jnp.dot(ahead, weight_block, preferred_element_type=jnp.float32)
-                outs[n_ctx - s] = jnp.dot(behind, weight_block, preferred_element_type=jnp.float32)
+                received[s], received[n_ctx - s] = ahead, behind
             else:
-                left = shift_by(ahead[:, :half], 1)
-                right = shift_by(behind[:, half:], -1)
+                received[s] = (shift_by(ahead[:, :half], 1), shift_by(behind[:, half:], -1))
+            if s == 1:
+                w_mine, _, _ = lax.optimization_barrier((w_mine, ahead, behind))
+                w_other = lax.ppermute(w_mine, "core", [(0, 1), (1, 0)])
+                mine_first = lax.axis_index("core") == 0
+                w_mine = w_mine.reshape(-1, 1, rows, cols)
+                w_other = w_other.reshape(-1, 1, rows, cols)
+                weight_block = jnp.concatenate(
+                    [jnp.where(mine_first, w_mine, w_other), jnp.where(mine_first, w_other, w_mine)], axis=1
+                ).reshape(-1, cols)
+        for s in range(n_ctx):
+            if isinstance(received[s], tuple):
+                left, right = received[s]
                 outs[s] = jnp.dot(left, weight_block[:half], preferred_element_type=jnp.float32) + jnp.dot(
                     right, weight_block[half:], preferred_element_type=jnp.float32
                 )
+            else:
+                outs[s] = jnp.dot(received[s], weight_block, preferred_element_type=jnp.float32)
         stacked = jnp.concatenate(outs + outs, axis=0).astype(jnp.bfloat16)
         position = lax.axis_index("ctx")
         return lax.dynamic_slice_in_dim(stacked, (n_ctx - position) * tok_rows, n_ctx * tok_rows, axis=0)
@@ -84,7 +97,7 @@
         P(("y", "z", "core"), "ctx"),
     )
     return jax.shard_map(
-        make_on_device(n_ctx, n_core),
+        make_on_device(n_ctx, n_core, n_y, n_z),
         mesh=split,
         in_specs=placed,
         out_specs=P(("y", "z", "core"), "ctx"),

time: 123 us -> 128 us (1.041)
  starting transfers between devices: 15.7 us -> 20.4 us
  blocking collectives: 39.5 us -> 35.9 us
  other arithmetic: 0.21 us -> 3.54 us
  waiting for transfers between devices: 35.9 us -> 38.9 us
  matrix products: 12.6 us -> 10 us
    ppermute x4, waiting for transfers between devices: 9.89 us -> 13.7 us  [shift_by(): return lax.ppermute(x, 'ctx', [(i, (i - s) % n_ctx) for i in range(n_ctx)])]
    all_gather x2 -> x1, blocking collectives: 39.5 us -> 35.9 us  [on_device(): w_mine = lax.all_gather(w_mine, axis, axis=0, tiled=True)]
    ppermute x4, starting transfers between devices: 11.9 us -> 14.6 us  [shift_by(): return lax.ppermute(x, 'ctx', [(i, (i - s) % n_ctx) for i in range(n_ctx)])]
    dot_general x3, matrix products: 5.07 us -> 2.55 us  [on_device(): jnp.dot(received[s], weight_block, preferred_element_type=jnp.float32)]
    select_n x0 -> x1, other arithmetic: none -> 1.98 us  [on_device(): jnp.where(mine_first, w_mine, w_other)]
    ppermute x0 -> x1, starting transfers between devices: none -> 1.91 us  [on_device(): w_other = lax.ppermute(w_mine, 'core', [(0, 1), (1, 0)])]
  transfers between devices with their start and end apart: 8 -> 9, of which waited for: 4 -> 6; matrix products, arithmetic and copies ran while one was open for 12% -> 13% of each run, Pallas kernels for 0% -> 0%
where the time goes in v7:
time: 128 us; the launch traced here: 127 us
  waiting for transfers between devices  38.9 us (30%)
  blocking collectives  35.9 us (28%)
  starting transfers between devices  20.4 us (16%)
  between operations  13.6 us (11%)
  matrix products  10 us (8%)
  local copies, waits for them, and re-layouts  5.04 us (4%)
  other arithmetic  3.54 us (3%)
    all_gather x1, blocking collectives, on_device(): w_mine = lax.all_gather(w_mine, axis, axis=0, tiled=True)  35.9 us
    ppermute x1, waiting for transfers between devices, on_device(): from_prev = lax.ppermute(state_bf, 'ctx', [(0, 1), (1, 2), (2, 3)])  15.2 us
    ppermute x4, starting transfers between devices, shift_by(): return lax.ppermute(x, 'ctx', [(i, (i - s) % n_ctx) for i in range(n_ctx)])  14.6 us
    ppermute x4, waiting for transfers between devices, shift_by(): return lax.ppermute(x, 'ctx', [(i, (i - s) % n_ctx) for i in range(n_ctx)])  13.7 us
    ppermute x1, waiting for transfers between devices, on_device(): forwarded = lax.ppermute(from_prev, 'ctx', [(1, 2), (2, 3)])  9.99 us
  transfers between devices with their start and end apart: 9, of which 6 were waited for; matrix products, arithmetic and copies ran while one was open for 13% of the time, Pallas kernels for 0%

profile of v7, /device:TPU:6, one launch (start us, length us, event | category | flops | bytes accessed | tf_op | source)
XLA Modules:
  0.0 127.5 jit_solution(12646281820399167906)
XLA Ops:
  6.5 35.9 %all_gather.6 = bf16[192,768]{1,0:T(8,128)(2,1)} all-gather(bf16[16,768]{1,0:T(8,128)(2,1)} %param.9), channel_id=1, replica_groups=mesh['y'=8,'z'=12,'core'=2,'ctx'=4] {'z'}, dimensions={0}, use_global_device_ids=true | all-gather | bytes 319488 | tf_op jit(solution)/shard_map/all_gather | solution.py:17
  42.5 1.5 %copy.26 = bf16[104,3072]{0,1:T(8,128)(2,1)S(1)} copy(bf16[104,3072]{1,0:T(8,128)(2,1)} %param.6) | data formatting | bytes 1277952 | tf_op jit(solution)/shard_map/reshape | solution.py:21
  43.9 0.4 copy.27
  44.3 1.6 %convolution_convert_fusion = bf16[32,96,96]{2,1,0:T(8,128)(2,1)} fusion(bf16[104,32,96]{0,2,1:T(8,128)(2,1)S(1)} %bitcast.42, bf16[104,32,96]{0,2,1:T(8,128)(2,1)S(1)} %bitcast.44), kind=kOutput, calls=%fused_computation.14 | convolution fusion | flops 61636608 | bytes 1867776 | tf_op jit(solution)/shard_map/shd,she->hde/dot_general | solution.py:23
  45.9 1.3 %collective-permute-start = (bf16[32,96,96]{2,1,0:T(8,128)(2,1)}, bf16[32,96,96]{2,1,0:T(8,128)(2,1)S(1)}, u32[]{:S(2)}, u32[]{:S(2)}) collective-permute-start(bf16[32,96,96]{2,1,0:T(8,128)(2,1)} %convolution_convert_fusion), channel_id=1, source_target_pairs={{0,1},{1,2},{2,3},{4,5},{5,6},{6,7},{8,9},{9,10},{10,11},{12,13},{... | collective-permute-start | bytes 1769480 | tf_op jit(solution)/shard_map/ppermute | solution.py:27
  47.2 1.3 %collective-permute-start.1 = (bf16[32,96,96]{2,1,0:T(8,128)(2,1)}, bf16[32,96,96]{2,1,0:T(8,128)(2,1)}, u32[]{:S(2)}, u32[]{:S(2)}) collective-permute-start(bf16[32,96,96]{2,1,0:T(8,128)(2,1)} %convolution_convert_fusion), channel_id=1, source_target_pairs={{0,3},{4,7},{8,11},{12,15},{16,19},{20,23},{24,27},{28,31},{32,35}... | collective-permute-start | bytes 1769480 | tf_op jit(solution)/shard_map/ppermute | solution.py:28
  48.5 15.2 %collective-permute-done = bf16[32,96,96]{2,1,0:T(8,128)(2,1)S(1)} collective-permute-done((bf16[32,96,96]{2,1,0:T(8,128)(2,1)}, bf16[32,96,96]{2,1,0:T(8,128)(2,1)S(1)}, u32[]{:S(2)}, u32[]{:S(2)}) %collective-permute-start) | collective-permute-done | bytes 589856 | tf_op jit(solution)/shard_map/ppermute | solution.py:27
  63.7 1.3 %collective-permute-start.2 = (bf16[32,96,96]{2,1,0:T(8,128)(2,1)S(1)}, bf16[32,96,96]{2,1,0:T(8,128)(2,1)}, u32[]{:S(2)}, u32[]{:S(2)}) collective-permute-start(bf16[32,96,96]{2,1,0:T(8,128)(2,1)S(1)} %collective-permute-done), channel_id=1, source_target_pairs={{1,2},{2,3},{5,6},{6,7},{9,10},{10,11},{13,14},{14,15},{17,18},{18... | collective-permute-start | bytes 1769480 | tf_op jit(solution)/shard_map/ppermute | solution.py:29
  65.0 1.5 %copy.25 = bf16[104,3072]{0,1:T(8,128)(2,1)S(1)} copy(bf16[104,3072]{1,0:T(8,128)(2,1)} %param.5) | data formatting | bytes 1277952 | tf_op jit(solution)/shard_map/reshape | solution.py:20
  66.5 2.3 %fusion.2 = f32[32,104,96]{1,2,0:T(8,128)} fusion(bf16[104,32,96]{0,2,1:T(8,128)(2,1)S(1)} %bitcast.45, bf16[104,32,96]{0,2,1:T(8,128)(2,1)S(1)} %bitcast.40, bf16[104,32,96]{0,2,1:T(8,128)(2,1)S(1)} %bitcast.43, pred[104,104]{1,0:T(8,128)(4,1)S(1)} %iota_compare_fusion), kind=kOutput, calls=%fused_computation.15 | convolution fusion | flops 133599232 | bytes 3205696 | tf_op jit(solution)/shard_map/hts,shd->thd/dot_general | solution.py:41
  68.8 10.0 %collective-permute-done.2 = bf16[32,96,96]{2,1,0:T(8,128)(2,1)} collective-permute-done((bf16[32,96,96]{2,1,0:T(8,128)(2,1)S(1)}, bf16[32,96,96]{2,1,0:T(8,128)(2,1)}, u32[]{:S(2)}, u32[]{:S(2)}) %collective-permute-start.2) | collective-permute-done | bytes 589856 | tf_op jit(solution)/shard_map/ppermute | solution.py:29
  78.8 2.6 %multiply_reduce_fusion = (f32[104]{0:T(128)S(1)}, f32[104,32,96]{0,2,1:T(8,128)S(1)}) fusion(bf16[104,32,96]{0,2,1:T(8,128)(2,1)S(1)} %bitcast.41, bf16[32,96,96]{2,1,0:T(8,128)(2,1)} %collective-permute-done.2, bf16[32,96,96]{2,1,0:T(8,128)(2,1)} %collective-permute-done.1, bf16[32,96,96]{2,1,0:T(8,128)(2,1)S(1)} %collective-permute-done, ...), kind=kOutput, calls=%fused_computation.12 | convolution fusion | flops 64069528 | bytes 4964768 | tf_op jit(solution)/shard_map/thd,hde->the/dot_general | solution.py:42
  81.4 0.5 copy.23
  82.3 2.7 %collective-permute-start.3 = (bf16[104,3072]{1,0:T(8,128)(2,1)S(1)}, bf16[104,3072]{1,0:T(8,128)(2,1)S(1)}, u32[]{:S(2)}, u32[]{:S(2)}) collective-permute-start(bf16[104,3072]{1,0:T(8,128)(2,1)S(1)} %multiply_convert_fusion.1), channel_id=1, source_target_pairs={{0,3},{1,0},{2,1},{3,2},{4,7},{5,4},{6,5},{7,6},{8,11},{9,8},{10,9... | collective-permute-start | bytes 1916936 | tf_op jit(solution)/shard_map/ppermute | solution.py:48
  85.0 4.3 %collective-permute-start.4 = (bf16[104,3072]{1,0:T(8,128)(2,1)S(1)}, bf16[104,3072]{1,0:T(8,128)(2,1)S(1)}, u32[]{:S(2)}, u32[]{:S(2)}) collective-permute-start(bf16[104,3072]{1,0:T(8,128)(2,1)S(1)} %multiply_convert_fusion.1), channel_id=1, source_target_pairs={{0,1},{1,2},{2,3},{3,0},{4,5},{5,6},{6,7},{7,4},{8,9},{9,10},{10,1... | collective-permute-start | bytes 1916936 | tf_op jit(solution)/shard_map/ppermute | solution.py:48
  89.3 6.4 %collective-permute-done.3 = bf16[104,3072]{1,0:T(8,128)(2,1)S(1)} collective-permute-done((bf16[104,3072]{1,0:T(8,128)(2,1)S(1)}, bf16[104,3072]{1,0:T(8,128)(2,1)S(1)}, u32[]{:S(2)}, u32[]{:S(2)}) %collective-permute-start.3) | collective-permute-done | bytes 639008 | tf_op jit(solution)/shard_map/ppermute | solution.py:48
  95.8 1.5 %collective-permute-done.4 = bf16[104,3072]{1,0:T(8,128)(2,1)S(1)} collective-permute-done((bf16[104,3072]{1,0:T(8,128)(2,1)S(1)}, bf16[104,3072]{1,0:T(8,128)(2,1)S(1)}, u32[]{:S(2)}, u32[]{:S(2)}) %collective-permute-start.4) | collective-permute-done | bytes 639008 | tf_op jit(solution)/shard_map/ppermute | solution.py:48
  97.3 1.9 %collective-permute-start.5 = (bf16[1536,768]{1,0:T(8,128)(2,1)}, bf16[1536,768]{1,0:T(8,128)(2,1)}, u32[]{:S(2)}, u32[]{:S(2)}) collective-permute-start(bf16[1536,768]{1,0:T(8,128)(2,1)} %all-gather.2.cloned.1.call-done), channel_id=1, source_target_pairs={{0,4},{4,0},{1,5},{5,1},{2,6},{6,2},{3,7},{7,3},{8,12},{12,8},{9,1... | collective-permute-start | bytes 7077896 | tf_op jit(solution)/shard_map/ppermute | solution.py:63
  99.3 0.5 multiply_convert_fusion
  99.8 5.7 %collective-permute-start.7 = (bf16[104,1536]{1,0:T(8,128)(2,1)S(1)}, bf16[104,1536]{1,0:T(8,128)(2,1)S(1)}, u32[]{:S(2)}, u32[]{:S(2)}) collective-permute-start(bf16[104,1536]{1,0:T(8,128)(2,1)S(1)} %slice.27), channel_id=1, source_target_pairs={{0,1},{1,2},{2,3},{3,0},{4,5},{5,6},{6,7},{7,4},{8,9},{9,10},{10,1... | collective-permute-start | bytes 958472 | tf_op jit(solution)/shard_map/ppermute | solution.py:48
  105.5 1.9 %collective-permute-start.6 = (bf16[104,1536]{1,0:T(8,128)(2,1)S(1)}, bf16[104,1536]{1,0:T(8,128)(2,1)S(1)}, u32[]{:S(2)}, u32[]{:S(2)}) collective-permute-start(bf16[104,1536]{1,0:T(8,128)(2,1)S(1)} %slice.24), channel_id=1, source_target_pairs={{0,3},{1,0},{2,1},{3,2},{4,7},{5,4},{6,5},{7,6},{8,11},{9,8},{10,9... | collective-permute-start | bytes 958472 | tf_op jit(solution)/shard_map/ppermute | solution.py:48
  107.5 2.0 %broadcast_select_fusion.1 = (bf16[1536,768]{1,0:T(8,128)(2,1)S(1)}, bf16[1536,768]{1,0:T(8,128)(2,1)S(1)}) fusion(bf16[1536,768]{1,0:T(8,128)(2,1)S(1)} %copy-done, bf16[1536,768]{1,0:T(8,128)(2,1)} %collective-permute-done.5, pred[]{:T(512)S(6)} %eq.3), kind=kLoop, calls=%fused_computation.8 | loop fusion | flops 2359296 | bytes 9437185 | tf_op jit(solution)/shard_map/jit(_where)/select_n | solution.py:68
  109.4 0.4 pad_maximum_fusion
  109.9 0.8 constant_dynamic-update-slice_fusion.7
  110.7 0.9 constant_dynamic-update-slice_fusion.6
  111.6 0.5 fusion
  112.0 0.9 collective-permute-done.7
  112.9 0.5 fusion.7
  113.4 4.8 %collective-permute-done.6 = bf16[104,1536]{1,0:T(8,128)(2,1)S(1)} collective-permute-done((bf16[104,1536]{1,0:T(8,128)(2,1)S(1)}, bf16[104,1536]{1,0:T(8,128)(2,1)S(1)}, u32[]{:S(2)}, u32[]{:S(2)}) %collective-permute-start.6) | collective-permute-done | bytes 319520 | tf_op jit(solution)/shard_map/ppermute | solution.py:48
  118.3 0.5 constant_dynamic-update-slice_fusion.5
  118.8 0.9 constant_dynamic-update-slice_fusion.4
  119.8 0.9 constant_dynamic-slice_fusion
  (21 shorter events, 0.6 us)
Async XLA Ops:
  6.5 37.4 %copy-start.1 = (bf16[104,3072]{1,0:T(8,128)(2,1)S(1)}, bf16[104,3072]{1,0:T(8,128)(2,1)}, u32[]{:S(2)}) copy-start(bf16[104,3072]{1,0:T(8,128)(2,1)} %param.7) | copy-start | bytes 1916932
  6.5 90.8 %all-gather.2.cloned.1.call-start = ((), (), s32[]{:S(2)}) async-start(), calls=%async_computation | async-start | bytes 2654208 | tf_op jit(solution)/shard_map/all_gather | solution.py:17
  45.9 17.8 %collective-permute-start = (bf16[32,96,96]{2,1,0:T(8,128)(2,1)}, bf16[32,96,96]{2,1,0:T(8,128)(2,1)S(1)}, u32[]{:S(2)}, u32[]{:S(2)}) collective-permute-start(bf16[32,96,96]{2,1,0:T(8,128)(2,1)} %convolution_convert_fusion), channel_id=1, source_target_pairs={{0,1},{1,2},{2,3},{4,5},{5,6},{6,7},{8,9},{9,10},{10,11},{12,13},{... | collective-permute-start | bytes 1769480 | tf_op jit(solution)/shard_map/ppermute | solution.py:27
  47.2 21.6 %collective-permute-start.1 = (bf16[32,96,96]{2,1,0:T(8,128)(2,1)}, bf16[32,96,96]{2,1,0:T(8,128)(2,1)}, u32[]{:S(2)}, u32[]{:S(2)}) collective-permute-start(bf16[32,96,96]{2,1,0:T(8,128)(2,1)} %convolution_convert_fusion), channel_id=1, source_target_pairs={{0,3},{4,7},{8,11},{12,15},{16,19},{20,23},{24,27},{28,31},{32,35}... | collective-permute-start | bytes 1769480 | tf_op jit(solution)/shard_map/ppermute | solution.py:28
  63.7 15.1 %collective-permute-start.2 = (bf16[32,96,96]{2,1,0:T(8,128)(2,1)S(1)}, bf16[32,96,96]{2,1,0:T(8,128)(2,1)}, u32[]{:S(2)}, u32[]{:S(2)}) collective-permute-start(bf16[32,96,96]{2,1,0:T(8,128)(2,1)S(1)} %collective-permute-done), channel_id=1, source_target_pairs={{1,2},{2,3},{5,6},{6,7},{9,10},{10,11},{13,14},{14,15},{17,18},{18... | collective-permute-start | bytes 1769480 | tf_op jit(solution)/shard_map/ppermute | solution.py:29
  81.4 0.7 copy-start.2
  82.3 13.5 %collective-permute-start.3 = (bf16[104,3072]{1,0:T(8,128)(2,1)S(1)}, bf16[104,3072]{1,0:T(8,128)(2,1)S(1)}, u32[]{:S(2)}, u32[]{:S(2)}) collective-permute-start(bf16[104,3072]{1,0:T(8,128)(2,1)S(1)} %multiply_convert_fusion.1), channel_id=1, source_target_pairs={{0,3},{1,0},{2,1},{3,2},{4,7},{5,4},{6,5},{7,6},{8,11},{9,8},{10,9... | collective-permute-start | bytes 1916936 | tf_op jit(solution)/shard_map/ppermute | solution.py:48
  85.0 12.3 %collective-permute-start.4 = (bf16[104,3072]{1,0:T(8,128)(2,1)S(1)}, bf16[104,3072]{1,0:T(8,128)(2,1)S(1)}, u32[]{:S(2)}, u32[]{:S(2)}) collective-permute-start(bf16[104,3072]{1,0:T(8,128)(2,1)S(1)} %multiply_convert_fusion.1), channel_id=1, source_target_pairs={{0,1},{1,2},{2,3},{3,0},{4,5},{5,6},{6,7},{7,4},{8,9},{9,10},{10,1... | collective-permute-start | bytes 1916936 | tf_op jit(solution)/shard_map/ppermute | solution.py:48
  97.3 10.1 %collective-permute-start.5 = (bf16[1536,768]{1,0:T(8,128)(2,1)}, bf16[1536,768]{1,0:T(8,128)(2,1)}, u32[]{:S(2)}, u32[]{:S(2)}) collective-permute-start(bf16[1536,768]{1,0:T(8,128)(2,1)} %all-gather.2.cloned.1.call-done), channel_id=1, source_target_pairs={{0,4},{4,0},{1,5},{5,1},{2,6},{6,2},{3,7},{7,3},{8,12},{12,8},{9,1... | collective-permute-start | bytes 7077896 | tf_op jit(solution)/shard_map/ppermute | solution.py:63
  99.3 8.1 %copy-start = (bf16[1536,768]{1,0:T(8,128)(2,1)S(1)}, bf16[1536,768]{1,0:T(8,128)(2,1)}, u32[]{:S(2)}) copy-start(bf16[1536,768]{1,0:T(8,128)(2,1)} %all-gather.2.cloned.1.call-done) | copy-start | bytes 7077892
  99.8 13.1 %collective-permute-start.7 = (bf16[104,1536]{1,0:T(8,128)(2,1)S(1)}, bf16[104,1536]{1,0:T(8,128)(2,1)S(1)}, u32[]{:S(2)}, u32[]{:S(2)}) collective-permute-start(bf16[104,1536]{1,0:T(8,128)(2,1)S(1)} %slice.27), channel_id=1, source_target_pairs={{0,1},{1,2},{2,3},{3,0},{4,5},{5,6},{6,7},{7,4},{8,9},{9,10},{10,1... | collective-permute-start | bytes 958472 | tf_op jit(solution)/shard_map/ppermute | solution.py:48
  105.5 12.8 %collective-permute-start.6 = (bf16[104,1536]{1,0:T(8,128)(2,1)S(1)}, bf16[104,1536]{1,0:T(8,128)(2,1)S(1)}, u32[]{:S(2)}, u32[]{:S(2)}) collective-permute-start(bf16[104,1536]{1,0:T(8,128)(2,1)S(1)} %slice.24), channel_id=1, source_target_pairs={{0,3},{1,0},{2,1},{3,2},{4,7},{5,4},{6,5},{7,6},{8,11},{9,8},{10,9... | collective-permute-start | bytes 958472 | tf_op jit(solution)/shard_map/ppermute | solution.py:48
Sparse Core Ops, SparseCore 0:
  42.6 41.6 all-gather.1

commit v8 on v3

--- a/solution.py
+++ b/solution.py
@@ -12,7 +12,7 @@
 def make_on_device(n_ctx, n_core):
     def on_device(queries, keys, values, norm_gain, out_weight):
         weight_block = out_weight
-        for axis in ("core", "z", "y"):
+        for axis in (("z", "core"), "y"):
             weight_block = lax.all_gather(weight_block, axis, axis=0, tiled=True)
 
         tok_rows = queries.shape[0]

time: 123 us -> 133 us (1.081)
  waiting for transfers between devices: 35.9 us -> 49 us
  blocking collectives: 39.5 us -> 37.1 us
    ppermute x1, waiting for transfers between devices: 10.7 us -> 15.9 us  [on_device(): forwarded = lax.ppermute(from_prev, 'ctx', [(1, 2), (2, 3)])]
    ppermute x1, waiting for transfers between devices: 15.2 us -> 19.3 us  [on_device(): from_prev = lax.ppermute(state_bf, 'ctx', [(0, 1), (1, 2), (2, 3)])]
    ppermute x4, waiting for transfers between devices: 9.89 us -> 13.7 us  [shift_by(): return lax.ppermute(x, 'ctx', [(i, (i - s) % n_ctx) for i in range(n_ctx)])]
    all_gather x2 -> x1, blocking collectives: 39.5 us -> 37.1 us  [on_device(): weight_block = lax.all_gather(weight_block, axis, axis=0, tiled=True)]
  transfers between devices with their start and end apart: 8 -> 8, of which waited for: 4 -> 4; matrix products, arithmetic and copies ran while one was open for 12% -> 11% of each run, Pallas kernels for 0% -> 0%
where the time goes in v8:
time: 133 us; the launch traced here: 132 us
  waiting for transfers between devices  49 us (37%)
  blocking collectives  37.1 us (28%)
  starting transfers between devices  15.5 us (12%)
  between operations  13.6 us (10%)
  matrix products  12.6 us (9%)
  local copies, waits for them, and re-layouts  4.29 us (3%)
    all_gather x1, blocking collectives, on_device(): weight_block = lax.all_gather(weight_block, axis, axis=0, tiled=True)  37.1 us
    ppermute x1, waiting for transfers between devices, on_device(): from_prev = lax.ppermute(state_bf, 'ctx', [(0, 1), (1, 2), (2, 3)])  19.3 us
    ppermute x1, waiting for transfers between devices, on_device(): forwarded = lax.ppermute(from_prev, 'ctx', [(1, 2), (2, 3)])  15.9 us
    ppermute x4, waiting for transfers between devices, shift_by(): return lax.ppermute(x, 'ctx', [(i, (i - s) % n_ctx) for i in range(n_ctx)])  13.7 us
    ppermute x4, starting transfers between devices, shift_by(): return lax.ppermute(x, 'ctx', [(i, (i - s) % n_ctx) for i in range(n_ctx)])  11.7 us
    dot_general x1, matrix products, on_device(): outs[0] = jnp.dot(normed, weight_block, preferred_element_type=jnp.float32)  3.33 us
  transfers between devices with their start and end apart: 8, of which 4 were waited for; matrix products, arithmetic and copies ran while one was open for 11% of the time, Pallas kernels for 0%

profile of v8, /device:TPU:6, one launch (start us, length us, event | category | flops | bytes accessed | tf_op | source)
XLA Modules:
  0.0 132.4 jit_solution(7204968895410042447)
XLA Ops:
  6.5 37.1 %all_gather.6 = bf16[384,768]{1,0:T(8,128)(2,1)} all-gather(bf16[16,768]{1,0:T(8,128)(2,1)} %param.9), channel_id=1, replica_groups=mesh['y'=8,'z'=12,'core'=2,'ctx'=4] {'z','core'}, dimensions={0}, use_global_device_ids=true | all-gather | bytes 614400 | tf_op jit(solution)/shard_map/all_gather | solution.py:16
  43.6 0.0 all-gather.2.cloned.1.call-update
  43.7 0.4 copy.26
  44.1 0.4 copy.27
  44.4 1.6 %convolution_convert_fusion = bf16[32,96,96]{2,1,0:T(8,128)(2,1)} fusion(bf16[104,32,96]{0,2,1:T(8,128)(2,1)S(1)} %bitcast.24, bf16[104,32,96]{0,2,1:T(8,128)(2,1)S(1)} %bitcast.26), kind=kOutput, calls=%fused_computation.8 | convolution fusion | flops 61636608 | bytes 1867776 | tf_op jit(solution)/shard_map/shd,she->hde/dot_general | solution.py:22
  46.0 1.3 collective-permute-start
  47.3 1.3 collective-permute-start.1
  48.6 19.3 %collective-permute-done = bf16[32,96,96]{2,1,0:T(8,128)(2,1)S(1)} collective-permute-done((bf16[32,96,96]{2,1,0:T(8,128)(2,1)}, bf16[32,96,96]{2,1,0:T(8,128)(2,1)S(1)}, u32[]{:S(2)}, u32[]{:S(2)}) %collective-permute-start) | collective-permute-done | bytes 589856 | tf_op jit(solution)/shard_map/ppermute | solution.py:26
  67.9 1.3 collective-permute-start.2
  69.2 1.5 %copy.25 = bf16[104,3072]{0,1:T(8,128)(2,1)S(1)} copy(bf16[104,3072]{1,0:T(8,128)(2,1)} %param.5) | data formatting | bytes 1277952 | tf_op jit(solution)/shard_map/reshape | solution.py:19
  70.7 2.4 %fusion.4 = f32[32,104,96]{1,2,0:T(8,128)} fusion(bf16[104,32,96]{0,2,1:T(8,128)(2,1)S(1)} %bitcast.27, bf16[104,32,96]{0,2,1:T(8,128)(2,1)S(1)} %bitcast.22, bf16[104,32,96]{0,2,1:T(8,128)(2,1)S(1)} %bitcast.25, pred[104,104]{1,0:T(8,128)(4,1)S(1)} %iota_compare_fusion), kind=kOutput, calls=%fused_computation.9 | convolution fusion | flops 133599232 | bytes 3205696 | tf_op jit(solution)/shard_map/hts,shd->thd/dot_general | solution.py:40
  73.1 0.0 collective-permute-done.1
  73.1 15.9 %collective-permute-done.2 = bf16[32,96,96]{2,1,0:T(8,128)(2,1)} collective-permute-done((bf16[32,96,96]{2,1,0:T(8,128)(2,1)S(1)}, bf16[32,96,96]{2,1,0:T(8,128)(2,1)}, u32[]{:S(2)}, u32[]{:S(2)}) %collective-permute-start.2) | collective-permute-done | bytes 589856 | tf_op jit(solution)/shard_map/ppermute | solution.py:28
  89.0 2.6 %multiply_reduce_fusion = (f32[104]{0:T(128)S(1)}, f32[104,32,96]{0,2,1:T(8,128)S(1)}) fusion(bf16[104,32,96]{0,2,1:T(8,128)(2,1)S(1)} %bitcast.23, bf16[32,96,96]{2,1,0:T(8,128)(2,1)} %collective-permute-done.2, bf16[32,96,96]{2,1,0:T(8,128)(2,1)} %collective-permute-done.1, bf16[32,96,96]{2,1,0:T(8,128)(2,1)S(1)} %collective-permute-done, ...), kind=kOutput, calls=%fused_computation.6 | convolution fusion | flops 64069528 | bytes 4964768 | tf_op jit(solution)/shard_map/thd,hde->the/dot_general | solution.py:41
  91.6 0.5 copy.23
  92.0 0.2 copy-done.3
  92.3 0.2 multiply_convert_fusion
  92.4 1.9 %collective-permute-start.5 = (bf16[104,3072]{1,0:T(8,128)(2,1)S(1)}, bf16[104,3072]{1,0:T(8,128)(2,1)S(1)}, u32[]{:S(2)}, u32[]{:S(2)}) collective-permute-start(bf16[104,3072]{1,0:T(8,128)(2,1)S(1)} %multiply_convert_fusion), channel_id=1, source_target_pairs={{0,1},{1,2},{2,3},{3,0},{4,5},{5,6},{6,7},{7,4},{8,9},{9,10},{10,1... | collective-permute-start | bytes 1916936 | tf_op jit(solution)/shard_map/ppermute | solution.py:47
  94.4 3.9 %collective-permute-start.3 = (bf16[104,3072]{1,0:T(8,128)(2,1)S(1)}, bf16[104,3072]{1,0:T(8,128)(2,1)S(1)}, u32[]{:S(2)}, u32[]{:S(2)}) collective-permute-start(bf16[104,3072]{1,0:T(8,128)(2,1)S(1)} %multiply_convert_fusion), channel_id=1, source_target_pairs={{0,3},{1,0},{2,1},{3,2},{4,7},{5,4},{6,5},{7,6},{8,11},{9,8},{10,9... | collective-permute-start | bytes 1916936 | tf_op jit(solution)/shard_map/ppermute | solution.py:47
  98.3 11.0 %collective-permute-done.5 = bf16[104,3072]{1,0:T(8,128)(2,1)S(1)} collective-permute-done((bf16[104,3072]{1,0:T(8,128)(2,1)S(1)}, bf16[104,3072]{1,0:T(8,128)(2,1)S(1)}, u32[]{:S(2)}, u32[]{:S(2)}) %collective-permute-start.5) | collective-permute-done | bytes 639008 | tf_op jit(solution)/shard_map/ppermute | solution.py:47
  109.4 3.4 %collective-permute-start.6 = (bf16[104,1536]{1,0:T(8,128)(2,1)S(1)}, bf16[104,1536]{1,0:T(8,128)(2,1)S(1)}, u32[]{:S(2)}, u32[]{:S(2)}) collective-permute-start(bf16[104,1536]{1,0:T(8,128)(2,1)S(1)} %slice.18), channel_id=1, source_target_pairs={{0,1},{1,2},{2,3},{3,0},{4,5},{5,6},{6,7},{7,4},{8,9},{9,10},{10,1... | collective-permute-start | bytes 958472 | tf_op jit(solution)/shard_map/ppermute | solution.py:47
  112.8 0.0 collective-permute-done.3
  112.8 2.4 %collective-permute-start.4 = (bf16[104,1536]{1,0:T(8,128)(2,1)S(1)}, bf16[104,1536]{1,0:T(8,128)(2,1)S(1)}, u32[]{:S(2)}, u32[]{:S(2)}) collective-permute-start(bf16[104,1536]{1,0:T(8,128)(2,1)S(1)} %slice.16), channel_id=1, source_target_pairs={{0,3},{1,0},{2,1},{3,2},{4,7},{5,4},{6,5},{7,6},{8,11},{9,8},{10,9... | collective-permute-start | bytes 958472 | tf_op jit(solution)/shard_map/ppermute | solution.py:47
  115.3 0.0 all-gather.2.cloned.1.call-done
  115.3 3.3 %constant_dynamic-update-slice_fusion.7 = (bf16[832,768]{1,0:T(8,128)(2,1)S(1)}, bf16[104,768]{1,0:T(8,128)(2,1)S(1)}) fusion(bf16[104,3072]{1,0:T(8,128)(2,1)S(1)} %multiply_convert_fusion, bf16[3072,768]{1,0:T(8,128)(2,1)} %all-gather.2.cloned.1.call-done), kind=kOutput, calls=%fused_computation.26 | convolution fusion | flops 490813440 | bytes 5677056 | tf_op jit(solution)/shard_map/dot_general | solution.py:51
  118.6 0.4 copy-done
  119.1 0.9 constant_dynamic-update-slice_fusion.6
  119.9 0.5 fusion
  120.5 2.7 %collective-permute-done.4 = bf16[104,1536]{1,0:T(8,128)(2,1)S(1)} collective-permute-done((bf16[104,1536]{1,0:T(8,128)(2,1)S(1)}, bf16[104,1536]{1,0:T(8,128)(2,1)S(1)}, u32[]{:S(2)}, u32[]{:S(2)}) %collective-permute-start.4) | collective-permute-done | bytes 319520 | tf_op jit(solution)/shard_map/ppermute | solution.py:47
  123.2 0.5 constant_dynamic-update-slice_fusion.5
  123.7 0.9 constant_dynamic-update-slice_fusion.4
  124.6 0.9 constant_dynamic-slice_fusion
  (16 shorter events, 0.1 us)
Async XLA Ops:
  6.5 37.1 %copy-start.1 = (bf16[104,3072]{1,0:T(8,128)(2,1)S(1)}, bf16[104,3072]{1,0:T(8,128)(2,1)}, u32[]{:S(2)}) copy-start(bf16[104,3072]{1,0:T(8,128)(2,1)} %param.6) | copy-start | bytes 1916932
  6.5 37.5 %copy-start.2 = (bf16[104,3072]{1,0:T(8,128)(2,1)S(1)}, bf16[104,3072]{1,0:T(8,128)(2,1)}, u32[]{:S(2)}) copy-start(bf16[104,3072]{1,0:T(8,128)(2,1)} %param.7) | copy-start | bytes 1916932
  6.5 108.7 %all-gather.2.cloned.1.call-start = ((), (), s32[]{:S(2)}) async-start(), calls=%async_computation | async-start | bytes 5308416 | tf_op jit(solution)/shard_map/all_gather | solution.py:16
  46.0 21.9 %collective-permute-start = (bf16[32,96,96]{2,1,0:T(8,128)(2,1)}, bf16[32,96,96]{2,1,0:T(8,128)(2,1)S(1)}, u32[]{:S(2)}, u32[]{:S(2)}) collective-permute-start(bf16[32,96,96]{2,1,0:T(8,128)(2,1)} %convolution_convert_fusion), channel_id=1, source_target_pairs={{0,1},{1,2},{2,3},{4,5},{5,6},{6,7},{8,9},{9,10},{10,11},{12,13},{... | collective-permute-start | bytes 1769480 | tf_op jit(solution)/shard_map/ppermute | solution.py:26
  47.3 25.8 %collective-permute-start.1 = (bf16[32,96,96]{2,1,0:T(8,128)(2,1)}, bf16[32,96,96]{2,1,0:T(8,128)(2,1)}, u32[]{:S(2)}, u32[]{:S(2)}) collective-permute-start(bf16[32,96,96]{2,1,0:T(8,128)(2,1)} %convolution_convert_fusion), channel_id=1, source_target_pairs={{0,3},{4,7},{8,11},{12,15},{16,19},{20,23},{24,27},{28,31},{32,35}... | collective-permute-start | bytes 1769480 | tf_op jit(solution)/shard_map/ppermute | solution.py:27
  67.9 21.1 %collective-permute-start.2 = (bf16[32,96,96]{2,1,0:T(8,128)(2,1)S(1)}, bf16[32,96,96]{2,1,0:T(8,128)(2,1)}, u32[]{:S(2)}, u32[]{:S(2)}) collective-permute-start(bf16[32,96,96]{2,1,0:T(8,128)(2,1)S(1)} %collective-permute-done), channel_id=1, source_target_pairs={{1,2},{2,3},{5,6},{6,7},{9,10},{10,11},{13,14},{14,15},{17,18},{18... | collective-permute-start | bytes 1769480 | tf_op jit(solution)/shard_map/ppermute | solution.py:28
  91.5 0.7 copy-start.3
  92.4 16.9 %collective-permute-start.5 = (bf16[104,3072]{1,0:T(8,128)(2,1)S(1)}, bf16[104,3072]{1,0:T(8,128)(2,1)S(1)}, u32[]{:S(2)}, u32[]{:S(2)}) collective-permute-start(bf16[104,3072]{1,0:T(8,128)(2,1)S(1)} %multiply_convert_fusion), channel_id=1, source_target_pairs={{0,1},{1,2},{2,3},{3,0},{4,5},{5,6},{6,7},{7,4},{8,9},{9,10},{10,1... | collective-permute-start | bytes 1916936 | tf_op jit(solution)/shard_map/ppermute | solution.py:47
  94.4 18.4 %collective-permute-start.3 = (bf16[104,3072]{1,0:T(8,128)(2,1)S(1)}, bf16[104,3072]{1,0:T(8,128)(2,1)S(1)}, u32[]{:S(2)}, u32[]{:S(2)}) collective-permute-start(bf16[104,3072]{1,0:T(8,128)(2,1)S(1)} %multiply_convert_fusion), channel_id=1, source_target_pairs={{0,3},{1,0},{2,1},{3,2},{4,7},{5,4},{6,5},{7,6},{8,11},{9,8},{10,9... | collective-permute-start | bytes 1916936 | tf_op jit(solution)/shard_map/ppermute | solution.py:47
  109.4 10.6 %collective-permute-start.6 = (bf16[104,1536]{1,0:T(8,128)(2,1)S(1)}, bf16[104,1536]{1,0:T(8,128)(2,1)S(1)}, u32[]{:S(2)}, u32[]{:S(2)}) collective-permute-start(bf16[104,1536]{1,0:T(8,128)(2,1)S(1)} %slice.18), channel_id=1, source_target_pairs={{0,1},{1,2},{2,3},{3,0},{4,5},{5,6},{6,7},{7,4},{8,9},{9,10},{10,1... | collective-permute-start | bytes 958472 | tf_op jit(solution)/shard_map/ppermute | solution.py:47
  112.8 10.3 %collective-permute-start.4 = (bf16[104,1536]{1,0:T(8,128)(2,1)S(1)}, bf16[104,1536]{1,0:T(8,128)(2,1)S(1)}, u32[]{:S(2)}, u32[]{:S(2)}) collective-permute-start(bf16[104,1536]{1,0:T(8,128)(2,1)S(1)} %slice.16), channel_id=1, source_target_pairs={{0,3},{1,0},{2,1},{3,2},{4,7},{5,4},{6,5},{7,6},{8,11},{9,8},{10,9... | collective-permute-start | bytes 958472 | tf_op jit(solution)/shard_map/ppermute | solution.py:47
  115.3 3.8 %copy-start = (bf16[3072,768]{1,0:T(8,128)(2,1)S(1)}, bf16[3072,768]{1,0:T(8,128)(2,1)}, u32[]{:S(2)}) copy-start(bf16[3072,768]{1,0:T(8,128)(2,1)} %all-gather.2.cloned.1.call-done) | copy-start | bytes 14155780
Sparse Core Ops, SparseCore 0:
  43.8 59.3 all-gather.1

commit v9 on v3

--- a/solution.py
+++ b/solution.py
@@ -47,24 +47,30 @@
             return lax.ppermute(x, "ctx", [(i, (i - s) % n_ctx) for i in range(n_ctx)])
 
         half = HEADS * HEAD_DIM // 2
-        outs = [None] * n_ctx
-        outs[0] = jnp.dot(normed, weight_block, preferred_element_type=jnp.float32)
+        position = lax.axis_index("ctx")
+        cols = weight_block.shape[1]
+        result = jnp.zeros((n_ctx * tok_rows, cols), jnp.bfloat16)
+
+        def put(result, product, s):
+            row = ((position + s) % n_ctx) * tok_rows
+            return lax.dynamic_update_slice_in_dim(result, product.astype(jnp.bfloat16), row, axis=0)
+
+        result = put(result, jnp.dot(normed, weight_block, preferred_element_type=jnp.float32), 0)
         ahead, behind = normed, normed
         for s in range(1, n_ctx // 2 + 1):
             if 2 * s < n_ctx:
                 ahead = shift_by(ahead, 1)
                 behind = shift_by(behind, -1)
-                outs[s] = jnp.dot(ahead, weight_block, preferred_element_type=jnp.float32)
-                outs[n_ctx - s] = jnp.dot(behind, weight_block, preferred_element_type=jnp.float32)
+                result = put(result, jnp.dot(ahead, weight_block, preferred_element_type=jnp.float32), s)
+                result = put(result, jnp.dot(behind, weight_block, preferred_element_type=jnp.float32), n_ctx - s)
             else:
                 left = shift_by(ahead[:, :half], 1)
                 right = shift_by(behind[:, half:], -1)
-                outs[s] = jnp.dot(left, weight_block[:half], preferred_element_type=jnp.float32) + jnp.dot(
+                both = jnp.dot(left, weight_block[:half], preferred_element_type=jnp.float32) + jnp.dot(
                     right, weight_block[half:], preferred_element_type=jnp.float32
                 )
-        stacked = jnp.concatenate(outs + outs, axis=0).astype(jnp.bfloat16)
-        position = lax.axis_index("ctx")
-        return lax.dynamic_slice_in_dim(stacked, (n_ctx - position) * tok_rows, n_ctx * tok_rows, axis=0)
+                result = put(result, both, s)
+        return result
 
     return on_device
 

time: 123 us -> 122 us (level)
  transfers between devices with their start and end apart: 8 -> 8, of which waited for: 4 -> 3; matrix products, arithmetic and copies ran while one was open for 12% -> 12% of each run, Pallas kernels for 0% -> 0%
where the time goes in v9:
time: 122 us; the launch traced here: 121 us
  blocking collectives  39.5 us (32%)
  waiting for transfers between devices  35.1 us (29%)
  starting transfers between devices  15.7 us (13%)
  between operations  13.7 us (11%)
  matrix products  13.2 us (11%)
  local copies, waits for them, and re-layouts  3.69 us (3%)
    all_gather x2, blocking collectives, on_device(): weight_block = lax.all_gather(weight_block, axis, axis=0, tiled=True)  39.5 us
    ppermute x1, waiting for transfers between devices, on_device(): from_prev = lax.ppermute(state_bf, 'ctx', [(0, 1), (1, 2), (2, 3)])  15.2 us
    ppermute x4, starting transfers between devices, shift_by(): return lax.ppermute(x, 'ctx', [(i, (i - s) % n_ctx) for i in range(n_ctx)])  11.9 us
    ppermute x1, waiting for transfers between devices, on_device(): forwarded = lax.ppermute(from_prev, 'ctx', [(1, 2), (2, 3)])  10.7 us
    ppermute x4, waiting for transfers between devices, shift_by(): return lax.ppermute(x, 'ctx', [(i, (i - s) % n_ctx) for i in range(n_ctx)])  9.07 us
    dot_general x1, matrix products, on_device(): jnp.dot(normed, weight_block, preferred_element_type=jnp.float32)  3.33 us
    dot_general x1, matrix products, on_device(): jnp.einsum('thd,hde->the', q_heads, prefix_state, preferred_element_type=...  2.54 us
  transfers between devices with their start and end apart: 8, of which 3 were waited for; matrix products, arithmetic and copies ran while one was open for 12% of the time, Pallas kernels for 0%

profile of v9, /device:TPU:6, one launch (start us, length us, event | category | flops | bytes accessed | tf_op | source)
XLA Modules:
  0.0 121.1 jit_solution(1883770103205295658)
XLA Ops:
  6.5 2.2 %all_gather.9 = bf16[32,768]{1,0:T(8,128)(2,1)S(1)} all-gather(bf16[16,768]{1,0:T(8,128)(2,1)} %param.9), channel_id=1, replica_groups=mesh['y'=8,'z'=12,'core'=2,'ctx'=4] {'core'}, dimensions={0}, use_global_device_ids=true | all-gather | bytes 73728 | tf_op jit(solution)/shard_map/all_gather | solution.py:16
  8.7 37.3 %all_gather.10 = bf16[384,768]{1,0:T(8,128)(2,1)} all-gather(bf16[32,768]{1,0:T(8,128)(2,1)S(1)} %all_gather.9), channel_id=1, replica_groups=mesh['y'=8,'z'=12,'core'=2,'ctx'=4] {'z'}, dimensions={0}, use_global_device_ids=true | all-gather | bytes 638976 | tf_op jit(solution)/shard_map/all_gather | solution.py:16
  46.0 0.0 all-gather.2.cloned.1.call-update
  46.1 0.4 copy.26
  46.4 0.4 copy.27
  46.8 1.6 %convolution_convert_fusion = bf16[32,96,96]{2,1,0:T(8,128)(2,1)} fusion(bf16[104,32,96]{0,2,1:T(8,128)(2,1)S(1)} %bitcast.24, bf16[104,32,96]{0,2,1:T(8,128)(2,1)S(1)} %bitcast.26), kind=kOutput, calls=%fused_computation.8 | convolution fusion | flops 61636608 | bytes 1867776 | tf_op jit(solution)/shard_map/shd,she->hde/dot_general | solution.py:22
  48.4 1.3 %collective-permute-start = (bf16[32,96,96]{2,1,0:T(8,128)(2,1)}, bf16[32,96,96]{2,1,0:T(8,128)(2,1)S(1)}, u32[]{:S(2)}, u32[]{:S(2)}) collective-permute-start(bf16[32,96,96]{2,1,0:T(8,128)(2,1)} %convolution_convert_fusion), channel_id=1, source_target_pairs={{0,1},{1,2},{2,3},{4,5},{5,6},{6,7},{8,9},{9,10},{10,11},{12,13},{... | collective-permute-start | bytes 1769480 | tf_op jit(solution)/shard_map/ppermute | solution.py:26
  49.7 1.3 %collective-permute-start.1 = (bf16[32,96,96]{2,1,0:T(8,128)(2,1)}, bf16[32,96,96]{2,1,0:T(8,128)(2,1)}, u32[]{:S(2)}, u32[]{:S(2)}) collective-permute-start(bf16[32,96,96]{2,1,0:T(8,128)(2,1)} %convolution_convert_fusion), channel_id=1, source_target_pairs={{0,3},{4,7},{8,11},{12,15},{16,19},{20,23},{24,27},{28,31},{32,35}... | collective-permute-start | bytes 1769480 | tf_op jit(solution)/shard_map/ppermute | solution.py:27
  51.0 15.2 %collective-permute-done = bf16[32,96,96]{2,1,0:T(8,128)(2,1)S(1)} collective-permute-done((bf16[32,96,96]{2,1,0:T(8,128)(2,1)}, bf16[32,96,96]{2,1,0:T(8,128)(2,1)S(1)}, u32[]{:S(2)}, u32[]{:S(2)}) %collective-permute-start) | collective-permute-done | bytes 589856 | tf_op jit(solution)/shard_map/ppermute | solution.py:26
  66.2 1.3 %collective-permute-start.2 = (bf16[32,96,96]{2,1,0:T(8,128)(2,1)S(1)}, bf16[32,96,96]{2,1,0:T(8,128)(2,1)}, u32[]{:S(2)}, u32[]{:S(2)}) collective-permute-start(bf16[32,96,96]{2,1,0:T(8,128)(2,1)S(1)} %collective-permute-done), channel_id=1, source_target_pairs={{1,2},{2,3},{5,6},{6,7},{9,10},{10,11},{13,14},{14,15},{17,18},{18... | collective-permute-start | bytes 1769480 | tf_op jit(solution)/shard_map/ppermute | solution.py:28
  67.5 1.5 %copy.25 = bf16[104,3072]{0,1:T(8,128)(2,1)S(1)} copy(bf16[104,3072]{1,0:T(8,128)(2,1)} %param.5) | data formatting | bytes 1277952 | tf_op jit(solution)/shard_map/reshape | solution.py:19
  69.0 2.4 %fusion.4 = f32[32,104,96]{1,2,0:T(8,128)} fusion(bf16[104,32,96]{0,2,1:T(8,128)(2,1)S(1)} %bitcast.27, bf16[104,32,96]{0,2,1:T(8,128)(2,1)S(1)} %bitcast.22, bf16[104,32,96]{0,2,1:T(8,128)(2,1)S(1)} %bitcast.25, pred[104,104]{1,0:T(8,128)(4,1)S(1)} %iota_compare_fusion), kind=kOutput, calls=%fused_computation.9 | convolution fusion | flops 133599232 | bytes 3205696 | tf_op jit(solution)/shard_map/hts,shd->thd/dot_general | solution.py:40
  71.3 0.0 collective-permute-done.1
  71.3 10.7 %collective-permute-done.2 = bf16[32,96,96]{2,1,0:T(8,128)(2,1)} collective-permute-done((bf16[32,96,96]{2,1,0:T(8,128)(2,1)S(1)}, bf16[32,96,96]{2,1,0:T(8,128)(2,1)}, u32[]{:S(2)}, u32[]{:S(2)}) %collective-permute-start.2) | collective-permute-done | bytes 589856 | tf_op jit(solution)/shard_map/ppermute | solution.py:28
  82.1 2.5 %multiply_reduce_fusion = (f32[104]{0:T(128)S(1)}, f32[104,32,96]{0,2,1:T(8,128)S(1)}) fusion(bf16[104,32,96]{0,2,1:T(8,128)(2,1)S(1)} %bitcast.23, bf16[32,96,96]{2,1,0:T(8,128)(2,1)} %collective-permute-done.2, bf16[32,96,96]{2,1,0:T(8,128)(2,1)} %collective-permute-done.1, bf16[32,96,96]{2,1,0:T(8,128)(2,1)S(1)} %collective-permute-done, ...), kind=kOutput, calls=%fused_computation.6 | convolution fusion | flops 64069528 | bytes 4964768 | tf_op jit(solution)/shard_map/thd,hde->the/dot_general | solution.py:41
  84.6 0.5 copy.23
  85.1 0.2 copy-done.4
  85.3 0.2 multiply_convert_fusion
  85.5 1.9 %collective-permute-start.4 = (bf16[104,3072]{1,0:T(8,128)(2,1)S(1)}, bf16[104,3072]{1,0:T(8,128)(2,1)S(1)}, u32[]{:S(2)}, u32[]{:S(2)}) collective-permute-start(bf16[104,3072]{1,0:T(8,128)(2,1)S(1)} %multiply_convert_fusion), channel_id=1, source_target_pairs={{0,1},{1,2},{2,3},{3,0},{4,5},{5,6},{6,7},{7,4},{8,9},{9,10},{10,1... | collective-permute-start | bytes 1916936 | tf_op jit(solution)/shard_map/ppermute | solution.py:47
  87.4 3.9 %collective-permute-start.3 = (bf16[104,3072]{1,0:T(8,128)(2,1)S(1)}, bf16[104,3072]{1,0:T(8,128)(2,1)S(1)}, u32[]{:S(2)}, u32[]{:S(2)}) collective-permute-start(bf16[104,3072]{1,0:T(8,128)(2,1)S(1)} %multiply_convert_fusion), channel_id=1, source_target_pairs={{0,3},{1,0},{2,1},{3,2},{4,7},{5,4},{6,5},{7,6},{8,11},{9,8},{10,9... | collective-permute-start | bytes 1916936 | tf_op jit(solution)/shard_map/ppermute | solution.py:47
  91.4 9.1 %collective-permute-done.4 = bf16[104,3072]{1,0:T(8,128)(2,1)S(1)} collective-permute-done((bf16[104,3072]{1,0:T(8,128)(2,1)S(1)}, bf16[104,3072]{1,0:T(8,128)(2,1)S(1)}, u32[]{:S(2)}, u32[]{:S(2)}) %collective-permute-start.4) | collective-permute-done | bytes 639008 | tf_op jit(solution)/shard_map/ppermute | solution.py:47
  100.5 1.9 %collective-permute-start.6 = (bf16[104,1536]{1,0:T(8,128)(2,1)S(1)}, bf16[104,1536]{1,0:T(8,128)(2,1)S(1)}, u32[]{:S(2)}, u32[]{:S(2)}) collective-permute-start(bf16[104,1536]{1,0:T(8,128)(2,1)S(1)} %slice.18), channel_id=1, source_target_pairs={{0,1},{1,2},{2,3},{3,0},{4,5},{5,6},{6,7},{7,4},{8,9},{9,10},{10,1... | collective-permute-start | bytes 958472 | tf_op jit(solution)/shard_map/ppermute | solution.py:47
  102.5 4.1 %collective-permute-start.5 = (bf16[104,1536]{1,0:T(8,128)(2,1)S(1)}, bf16[104,1536]{1,0:T(8,128)(2,1)S(1)}, u32[]{:S(2)}, u32[]{:S(2)}) collective-permute-start(bf16[104,1536]{1,0:T(8,128)(2,1)S(1)} %slice.16), channel_id=1, source_target_pairs={{0,3},{1,0},{2,1},{3,2},{4,7},{5,4},{6,5},{7,6},{8,11},{9,8},{10,9... | collective-permute-start | bytes 958472 | tf_op jit(solution)/shard_map/ppermute | solution.py:47
  106.6 0.0 all-gather.2.cloned.1.call-done
  106.7 3.3 %fusion.16 = bf16[416,768]{1,0:T(8,128)(2,1)S(1)} fusion(bf16[416,768]{1,0:T(8,128)(2,1)S(1)} %broadcast_in_dim.15, s32[]{:T(128)S(6)} %select_n.37, bf16[104,3072]{1,0:T(8,128)(2,1)S(1)} %multiply_convert_fusion, bf16[3072,768]{1,0:T(8,128)(2,1)} %all-gather.2.cloned.1.call-done), kind=kOutput, calls=%fused_computation.19 | convolution fusion | flops 490813440 | bytes 5517316 | tf_op jit(solution)/shard_map/dot_general | solution.py:58
  110.0 0.4 copy-done
  110.4 0.9 fusion.15
  111.3 0.9 fusion.14
  112.2 0.0 copy-start.1
  112.2 0.5 fusion
  112.7 0.3 copy-done.1
  113.0 1.2 fusion.11
  (15 shorter events, 0.1 us)
Async XLA Ops:
  6.5 39.5 %copy-start.2 = (bf16[104,3072]{1,0:T(8,128)(2,1)S(1)}, bf16[104,3072]{1,0:T(8,128)(2,1)}, u32[]{:S(2)}) copy-start(bf16[104,3072]{1,0:T(8,128)(2,1)} %param.6) | copy-start | bytes 1916932
  6.5 39.9 %copy-start.3 = (bf16[104,3072]{1,0:T(8,128)(2,1)S(1)}, bf16[104,3072]{1,0:T(8,128)(2,1)}, u32[]{:S(2)}) copy-start(bf16[104,3072]{1,0:T(8,128)(2,1)} %param.7) | copy-start | bytes 1916932
  6.5 100.1 %all-gather.2.cloned.1.call-start = ((), (), s32[]{:S(2)}) async-start(), calls=%async_computation | async-start | bytes 5308416 | tf_op jit(solution)/shard_map/all_gather | solution.py:16
  48.4 17.8 %collective-permute-start = (bf16[32,96,96]{2,1,0:T(8,128)(2,1)}, bf16[32,96,96]{2,1,0:T(8,128)(2,1)S(1)}, u32[]{:S(2)}, u32[]{:S(2)}) collective-permute-start(bf16[32,96,96]{2,1,0:T(8,128)(2,1)} %convolution_convert_fusion), channel_id=1, source_target_pairs={{0,1},{1,2},{2,3},{4,5},{5,6},{6,7},{8,9},{9,10},{10,11},{12,13},{... | collective-permute-start | bytes 1769480 | tf_op jit(solution)/shard_map/ppermute | solution.py:26
  49.7 21.7 %collective-permute-start.1 = (bf16[32,96,96]{2,1,0:T(8,128)(2,1)}, bf16[32,96,96]{2,1,0:T(8,128)(2,1)}, u32[]{:S(2)}, u32[]{:S(2)}) collective-permute-start(bf16[32,96,96]{2,1,0:T(8,128)(2,1)} %convolution_convert_fusion), channel_id=1, source_target_pairs={{0,3},{4,7},{8,11},{12,15},{16,19},{20,23},{24,27},{28,31},{32,35}... | collective-permute-start | bytes 1769480 | tf_op jit(solution)/shard_map/ppermute | solution.py:27
  66.2 15.9 %collective-permute-start.2 = (bf16[32,96,96]{2,1,0:T(8,128)(2,1)S(1)}, bf16[32,96,96]{2,1,0:T(8,128)(2,1)}, u32[]{:S(2)}, u32[]{:S(2)}) collective-permute-start(bf16[32,96,96]{2,1,0:T(8,128)(2,1)S(1)} %collective-permute-done), channel_id=1, source_target_pairs={{1,2},{2,3},{5,6},{6,7},{9,10},{10,11},{13,14},{14,15},{17,18},{18... | collective-permute-start | bytes 1769480 | tf_op jit(solution)/shard_map/ppermute | solution.py:28
  84.6 0.7 copy-start.4
  85.5 15.0 %collective-permute-start.4 = (bf16[104,3072]{1,0:T(8,128)(2,1)S(1)}, bf16[104,3072]{1,0:T(8,128)(2,1)S(1)}, u32[]{:S(2)}, u32[]{:S(2)}) collective-permute-start(bf16[104,3072]{1,0:T(8,128)(2,1)S(1)} %multiply_convert_fusion), channel_id=1, source_target_pairs={{0,1},{1,2},{2,3},{3,0},{4,5},{5,6},{6,7},{7,4},{8,9},{9,10},{10,1... | collective-permute-start | bytes 1916936 | tf_op jit(solution)/shard_map/ppermute | solution.py:47
  87.4 15.0 %collective-permute-start.3 = (bf16[104,3072]{1,0:T(8,128)(2,1)S(1)}, bf16[104,3072]{1,0:T(8,128)(2,1)S(1)}, u32[]{:S(2)}, u32[]{:S(2)}) collective-permute-start(bf16[104,3072]{1,0:T(8,128)(2,1)S(1)} %multiply_convert_fusion), channel_id=1, source_target_pairs={{0,3},{1,0},{2,1},{3,2},{4,7},{5,4},{6,5},{7,6},{8,11},{9,8},{10,9... | collective-permute-start | bytes 1916936 | tf_op jit(solution)/shard_map/ppermute | solution.py:47
  100.5 11.7 %collective-permute-start.6 = (bf16[104,1536]{1,0:T(8,128)(2,1)S(1)}, bf16[104,1536]{1,0:T(8,128)(2,1)S(1)}, u32[]{:S(2)}, u32[]{:S(2)}) collective-permute-start(bf16[104,1536]{1,0:T(8,128)(2,1)S(1)} %slice.18), channel_id=1, source_target_pairs={{0,1},{1,2},{2,3},{3,0},{4,5},{5,6},{6,7},{7,4},{8,9},{9,10},{10,1... | collective-permute-start | bytes 958472 | tf_op jit(solution)/shard_map/ppermute | solution.py:47
  102.5 10.3 %collective-permute-start.5 = (bf16[104,1536]{1,0:T(8,128)(2,1)S(1)}, bf16[104,1536]{1,0:T(8,128)(2,1)S(1)}, u32[]{:S(2)}, u32[]{:S(2)}) collective-permute-start(bf16[104,1536]{1,0:T(8,128)(2,1)S(1)} %slice.16), channel_id=1, source_target_pairs={{0,3},{1,0},{2,1},{3,2},{4,7},{5,4},{6,5},{7,6},{8,11},{9,8},{10,9... | collective-permute-start | bytes 958472 | tf_op jit(solution)/shard_map/ppermute | solution.py:47
  106.7 3.8 %copy-start = (bf16[3072,768]{1,0:T(8,128)(2,1)S(1)}, bf16[3072,768]{1,0:T(8,128)(2,1)}, u32[]{:S(2)}) copy-start(bf16[3072,768]{1,0:T(8,128)(2,1)} %all-gather.2.cloned.1.call-done) | copy-start | bytes 14155780
  112.2 0.8 copy-start.1
Sparse Core Ops, SparseCore 0:
  46.2 59.2 all-gather.1

commit v10 on v9

--- a/solution.py
+++ b/solution.py
@@ -55,14 +55,13 @@
             row = ((position + s) % n_ctx) * tok_rows
             return lax.dynamic_update_slice_in_dim(result, product.astype(jnp.bfloat16), row, axis=0)
 
-        result = put(result, jnp.dot(normed, weight_block, preferred_element_type=jnp.float32), 0)
+        full = [(0, normed)]
         ahead, behind = normed, normed
         for s in range(1, n_ctx // 2 + 1):
             if 2 * s < n_ctx:
                 ahead = shift_by(ahead, 1)
                 behind = shift_by(behind, -1)
-                result = put(result, jnp.dot(ahead, weight_block, preferred_element_type=jnp.float32), s)
-                result = put(result, jnp.dot(behind, weight_block, preferred_element_type=jnp.float32), n_ctx - s)
+                full += [(s, ahead), (n_ctx - s, behind)]
             else:
                 left = shift_by(ahead[:, :half], 1)
                 right = shift_by(behind[:, half:], -1)
@@ -70,6 +69,11 @@
                     right, weight_block[half:], preferred_element_type=jnp.float32
                 )
                 result = put(result, both, s)
+        products = jnp.dot(
+            jnp.concatenate([block for _, block in full], axis=0), weight_block, preferred_element_type=jnp.float32
+        )
+        for i, (s, _) in enumerate(full):
+            result = put(result, products[i * tok_rows:(i + 1) * tok_rows], s)
         return result
 
     return on_device

time: 122 us -> 124 us (1.016)
  local copies, waits for them, and re-layouts: 3.69 us -> 5.61 us
  matrix products: 13.2 us -> 11.6 us
    dot_general x3 -> x1, matrix products: 5.07 us -> 4.14 us  [on_device(): jnp.dot(jnp.concatenate([block for _, block in full], axis=0), weight_blo...]
  transfers between devices with their start and end apart: 8 -> 8, of which waited for: 3 -> 4; matrix products, arithmetic and copies ran while one was open for 12% -> 12% of each run, Pallas kernels for 0% -> 0%
where the time goes in v10:
time: 124 us; the launch traced here: 123 us
  blocking collectives  39.5 us (32%)
  waiting for transfers between devices  36.3 us (29%)
  starting transfers between devices  15.7 us (13%)
  between operations  13.7 us (11%)
  matrix products  11.6 us (9%)
  local copies, waits for them, and re-layouts  5.61 us (5%)
    all_gather x2, blocking collectives, on_device(): weight_block = lax.all_gather(weight_block, axis, axis=0, tiled=True)  39.5 us
    ppermute x1, waiting for transfers between devices, on_device(): from_prev = lax.ppermute(state_bf, 'ctx', [(0, 1), (1, 2), (2, 3)])  15.2 us
    ppermute x4, starting transfers between devices, shift_by(): return lax.ppermute(x, 'ctx', [(i, (i - s) % n_ctx) for i in range(n_ctx)])  11.9 us
    ppermute x1, waiting for transfers between devices, on_device(): forwarded = lax.ppermute(from_prev, 'ctx', [(1, 2), (2, 3)])  10.7 us
    ppermute x4, waiting for transfers between devices, shift_by(): return lax.ppermute(x, 'ctx', [(i, (i - s) % n_ctx) for i in range(n_ctx)])  10.3 us
    dot_general x1, matrix products, on_device(): jnp.dot(jnp.concatenate([block for _, block in full], axis=0), weight_blo...  4.14 us
    dot_general x1, matrix products, on_device(): jnp.einsum('thd,hde->the', q_heads, prefix_state, preferred_element_type=...  2.56 us
  transfers between devices with their start and end apart: 8, of which 4 were waited for; matrix products, arithmetic and copies ran while one was open for 12% of the time, Pallas kernels for 0%

profile of v10, /device:TPU:6, one launch (start us, length us, event | category | flops | bytes accessed | tf_op | source)
XLA Modules:
  0.0 122.6 jit_solution(9606719909532325937)
XLA Ops:
  6.5 2.2 %all_gather.9 = bf16[32,768]{1,0:T(8,128)(2,1)S(1)} all-gather(bf16[16,768]{1,0:T(8,128)(2,1)} %param.9), channel_id=1, replica_groups=mesh['y'=8,'z'=12,'core'=2,'ctx'=4] {'core'}, dimensions={0}, use_global_device_ids=true | all-gather | bytes 73728 | tf_op jit(solution)/shard_map/all_gather | solution.py:16
  8.7 37.3 %all_gather.10 = bf16[384,768]{1,0:T(8,128)(2,1)} all-gather(bf16[32,768]{1,0:T(8,128)(2,1)S(1)} %all_gather.9), channel_id=1, replica_groups=mesh['y'=8,'z'=12,'core'=2,'ctx'=4] {'z'}, dimensions={0}, use_global_device_ids=true | all-gather | bytes 638976 | tf_op jit(solution)/shard_map/all_gather | solution.py:16
  46.0 0.0 all-gather.2.cloned.1.call-update
  46.0 1.5 %copy.26 = bf16[104,3072]{0,1:T(8,128)(2,1)S(1)} copy(bf16[104,3072]{1,0:T(8,128)(2,1)} %param.6) | data formatting | bytes 1277952 | tf_op jit(solution)/shard_map/reshape | solution.py:20
  47.5 0.4 copy.27
  47.9 1.6 %convolution_convert_fusion = bf16[32,96,96]{2,1,0:T(8,128)(2,1)} fusion(bf16[104,32,96]{0,2,1:T(8,128)(2,1)S(1)} %bitcast.19, bf16[104,32,96]{0,2,1:T(8,128)(2,1)S(1)} %bitcast.21), kind=kOutput, calls=%fused_computation.14 | convolution fusion | flops 61636608 | bytes 1867776 | tf_op jit(solution)/shard_map/shd,she->hde/dot_general | solution.py:22
  49.5 1.3 %collective-permute-start = (bf16[32,96,96]{2,1,0:T(8,128)(2,1)}, bf16[32,96,96]{2,1,0:T(8,128)(2,1)S(1)}, u32[]{:S(2)}, u32[]{:S(2)}) collective-permute-start(bf16[32,96,96]{2,1,0:T(8,128)(2,1)} %convolution_convert_fusion), channel_id=1, source_target_pairs={{0,1},{1,2},{2,3},{4,5},{5,6},{6,7},{8,9},{9,10},{10,11},{12,13},{... | collective-permute-start | bytes 1769480 | tf_op jit(solution)/shard_map/ppermute | solution.py:26
  50.8 1.3 %collective-permute-start.1 = (bf16[32,96,96]{2,1,0:T(8,128)(2,1)}, bf16[32,96,96]{2,1,0:T(8,128)(2,1)}, u32[]{:S(2)}, u32[]{:S(2)}) collective-permute-start(bf16[32,96,96]{2,1,0:T(8,128)(2,1)} %convolution_convert_fusion), channel_id=1, source_target_pairs={{0,3},{4,7},{8,11},{12,15},{16,19},{20,23},{24,27},{28,31},{32,35}... | collective-permute-start | bytes 1769480 | tf_op jit(solution)/shard_map/ppermute | solution.py:27
  52.1 15.2 %collective-permute-done = bf16[32,96,96]{2,1,0:T(8,128)(2,1)S(1)} collective-permute-done((bf16[32,96,96]{2,1,0:T(8,128)(2,1)}, bf16[32,96,96]{2,1,0:T(8,128)(2,1)S(1)}, u32[]{:S(2)}, u32[]{:S(2)}) %collective-permute-start) | collective-permute-done | bytes 589856 | tf_op jit(solution)/shard_map/ppermute | solution.py:26
  67.3 1.3 %collective-permute-start.2 = (bf16[32,96,96]{2,1,0:T(8,128)(2,1)S(1)}, bf16[32,96,96]{2,1,0:T(8,128)(2,1)}, u32[]{:S(2)}, u32[]{:S(2)}) collective-permute-start(bf16[32,96,96]{2,1,0:T(8,128)(2,1)S(1)} %collective-permute-done), channel_id=1, source_target_pairs={{1,2},{2,3},{5,6},{6,7},{9,10},{10,11},{13,14},{14,15},{17,18},{18... | collective-permute-start | bytes 1769480 | tf_op jit(solution)/shard_map/ppermute | solution.py:28
  68.6 1.5 %copy.25 = bf16[104,3072]{0,1:T(8,128)(2,1)S(1)} copy(bf16[104,3072]{1,0:T(8,128)(2,1)} %param.5) | data formatting | bytes 1277952 | tf_op jit(solution)/shard_map/reshape | solution.py:19
  70.1 2.3 %fusion.10 = f32[32,104,96]{1,2,0:T(8,128)} fusion(bf16[104,32,96]{0,2,1:T(8,128)(2,1)S(1)} %bitcast.22, bf16[104,32,96]{0,2,1:T(8,128)(2,1)S(1)} %bitcast.17, bf16[104,32,96]{0,2,1:T(8,128)(2,1)S(1)} %bitcast.20, pred[104,104]{1,0:T(8,128)(4,1)S(1)} %iota_compare_fusion), kind=kOutput, calls=%fused_computation.15 | convolution fusion | flops 133599232 | bytes 3205696 | tf_op jit(solution)/shard_map/hts,shd->thd/dot_general | solution.py:40
  72.4 10.7 %collective-permute-done.2 = bf16[32,96,96]{2,1,0:T(8,128)(2,1)} collective-permute-done((bf16[32,96,96]{2,1,0:T(8,128)(2,1)S(1)}, bf16[32,96,96]{2,1,0:T(8,128)(2,1)}, u32[]{:S(2)}, u32[]{:S(2)}) %collective-permute-start.2) | collective-permute-done | bytes 589856 | tf_op jit(solution)/shard_map/ppermute | solution.py:28
  83.1 2.6 %multiply_reduce_fusion = (f32[104]{0:T(128)S(1)}, f32[104,32,96]{0,2,1:T(8,128)S(1)}) fusion(bf16[104,32,96]{0,2,1:T(8,128)(2,1)S(1)} %bitcast.18, bf16[32,96,96]{2,1,0:T(8,128)(2,1)} %collective-permute-done.2, bf16[32,96,96]{2,1,0:T(8,128)(2,1)} %collective-permute-done.1, bf16[32,96,96]{2,1,0:T(8,128)(2,1)S(1)} %collective-permute-done, ...), kind=kOutput, calls=%fused_computation.12 | convolution fusion | flops 64069528 | bytes 4964768 | tf_op jit(solution)/shard_map/thd,hde->the/dot_general | solution.py:41
  85.7 0.5 copy.23
  86.2 0.2 copy-done.2
  86.4 0.2 multiply_convert_fusion
  86.6 1.9 %collective-permute-start.5 = (bf16[104,3072]{1,0:T(8,128)(2,1)S(1)}, bf16[104,3072]{1,0:T(8,128)(2,1)S(1)}, u32[]{:S(2)}, u32[]{:S(2)}) collective-permute-start(bf16[104,3072]{1,0:T(8,128)(2,1)S(1)} %multiply_convert_fusion), channel_id=1, source_target_pairs={{0,1},{1,2},{2,3},{3,0},{4,5},{5,6},{6,7},{7,4},{8,9},{9,10},{10,1... | collective-permute-start | bytes 1916936 | tf_op jit(solution)/shard_map/ppermute | solution.py:47
  88.5 3.9 %collective-permute-start.3 = (bf16[104,3072]{1,0:T(8,128)(2,1)S(1)}, bf16[104,3072]{1,0:T(8,128)(2,1)S(1)}, u32[]{:S(2)}, u32[]{:S(2)}) collective-permute-start(bf16[104,3072]{1,0:T(8,128)(2,1)S(1)} %multiply_convert_fusion), channel_id=1, source_target_pairs={{0,3},{1,0},{2,1},{3,2},{4,7},{5,4},{6,5},{7,6},{8,11},{9,8},{10,9... | collective-permute-start | bytes 1916936 | tf_op jit(solution)/shard_map/ppermute | solution.py:47
  92.5 9.0 %collective-permute-done.5 = bf16[104,3072]{1,0:T(8,128)(2,1)S(1)} collective-permute-done((bf16[104,3072]{1,0:T(8,128)(2,1)S(1)}, bf16[104,3072]{1,0:T(8,128)(2,1)S(1)}, u32[]{:S(2)}, u32[]{:S(2)}) %collective-permute-start.5) | collective-permute-done | bytes 639008 | tf_op jit(solution)/shard_map/ppermute | solution.py:47
  101.6 1.9 %collective-permute-start.6 = (bf16[104,1536]{1,0:T(8,128)(2,1)S(1)}, bf16[104,1536]{1,0:T(8,128)(2,1)S(1)}, u32[]{:S(2)}, u32[]{:S(2)}) collective-permute-start(bf16[104,1536]{1,0:T(8,128)(2,1)S(1)} %slice.33), channel_id=1, source_target_pairs={{0,1},{1,2},{2,3},{3,0},{4,5},{5,6},{6,7},{7,4},{8,9},{9,10},{10,1... | collective-permute-start | bytes 958472 | tf_op jit(solution)/shard_map/ppermute | solution.py:47
  103.5 0.0 collective-permute-done.3
  103.6 4.1 %collective-permute-start.4 = (bf16[104,1536]{1,0:T(8,128)(2,1)S(1)}, bf16[104,1536]{1,0:T(8,128)(2,1)S(1)}, u32[]{:S(2)}, u32[]{:S(2)}) collective-permute-start(bf16[104,1536]{1,0:T(8,128)(2,1)S(1)} %slice.31), channel_id=1, source_target_pairs={{0,3},{1,0},{2,1},{3,2},{4,7},{5,4},{6,5},{7,6},{8,11},{9,8},{10,9... | collective-permute-start | bytes 958472 | tf_op jit(solution)/shard_map/ppermute | solution.py:47
  107.7 0.0 all-gather.2.cloned.1.call-done
  107.7 4.1 %fusion.11 = bf16[312,768]{1,0:T(8,128)(2,1)S(1)} fusion(bf16[3072,768]{1,0:T(8,128)(2,1)} %all-gather.2.cloned.1.call-done, bf16[104,3072]{1,0:T(8,128)(2,1)S(1)} %collective-permute-done.5, bf16[104,3072]{1,0:T(8,128)(2,1)S(1)} %collective-permute-done.3, bf16[104,3072]{1,0:T(8,128)(2,1)S(1)} %multiply_convert_fusion), kind=kOutput, calls=%fused_computation.16 | convolution fusion | flops 1478191104 | bytes 7114752 | tf_op jit(solution)/shard_map/dot_general | solution.py:72
  111.9 0.0 collective-permute-done.6
  111.9 0.5 fusion
  112.4 1.2 %collective-permute-done.4 = bf16[104,1536]{1,0:T(8,128)(2,1)S(1)} collective-permute-done((bf16[104,1536]{1,0:T(8,128)(2,1)S(1)}, bf16[104,1536]{1,0:T(8,128)(2,1)S(1)}, u32[]{:S(2)}, u32[]{:S(2)}) %collective-permute-start.4) | collective-permute-done | bytes 319520 | tf_op jit(solution)/shard_map/ppermute | solution.py:47
  113.7 0.5 fusion.20
  114.3 0.0 copy-start
  114.3 0.8 copy-done
  115.1 0.7 slice_dynamic-update-slice_fusion
  (14 shorter events, 0.2 us)
Async XLA Ops:
  6.5 41.0 %copy-start.1 = (bf16[104,3072]{1,0:T(8,128)(2,1)S(1)}, bf16[104,3072]{1,0:T(8,128)(2,1)}, u32[]{:S(2)}) copy-start(bf16[104,3072]{1,0:T(8,128)(2,1)} %param.7) | copy-start | bytes 1916932
  6.5 101.2 %all-gather.2.cloned.1.call-start = ((), (), s32[]{:S(2)}) async-start(), calls=%async_computation | async-start | bytes 5308416 | tf_op jit(solution)/shard_map/all_gather | solution.py:16
  49.5 17.8 %collective-permute-start = (bf16[32,96,96]{2,1,0:T(8,128)(2,1)}, bf16[32,96,96]{2,1,0:T(8,128)(2,1)S(1)}, u32[]{:S(2)}, u32[]{:S(2)}) collective-permute-start(bf16[32,96,96]{2,1,0:T(8,128)(2,1)} %convolution_convert_fusion), channel_id=1, source_target_pairs={{0,1},{1,2},{2,3},{4,5},{5,6},{6,7},{8,9},{9,10},{10,11},{12,13},{... | collective-permute-start | bytes 1769480 | tf_op jit(solution)/shard_map/ppermute | solution.py:26
  50.8 21.6 %collective-permute-start.1 = (bf16[32,96,96]{2,1,0:T(8,128)(2,1)}, bf16[32,96,96]{2,1,0:T(8,128)(2,1)}, u32[]{:S(2)}, u32[]{:S(2)}) collective-permute-start(bf16[32,96,96]{2,1,0:T(8,128)(2,1)} %convolution_convert_fusion), channel_id=1, source_target_pairs={{0,3},{4,7},{8,11},{12,15},{16,19},{20,23},{24,27},{28,31},{32,35}... | collective-permute-start | bytes 1769480 | tf_op jit(solution)/shard_map/ppermute | solution.py:27
  67.3 15.9 %collective-permute-start.2 = (bf16[32,96,96]{2,1,0:T(8,128)(2,1)S(1)}, bf16[32,96,96]{2,1,0:T(8,128)(2,1)}, u32[]{:S(2)}, u32[]{:S(2)}) collective-permute-start(bf16[32,96,96]{2,1,0:T(8,128)(2,1)S(1)} %collective-permute-done), channel_id=1, source_target_pairs={{1,2},{2,3},{5,6},{6,7},{9,10},{10,11},{13,14},{14,15},{17,18},{18... | collective-permute-start | bytes 1769480 | tf_op jit(solution)/shard_map/ppermute | solution.py:28
  85.7 0.7 copy-start.2
  86.6 15.0 %collective-permute-start.5 = (bf16[104,3072]{1,0:T(8,128)(2,1)S(1)}, bf16[104,3072]{1,0:T(8,128)(2,1)S(1)}, u32[]{:S(2)}, u32[]{:S(2)}) collective-permute-start(bf16[104,3072]{1,0:T(8,128)(2,1)S(1)} %multiply_convert_fusion), channel_id=1, source_target_pairs={{0,1},{1,2},{2,3},{3,0},{4,5},{5,6},{6,7},{7,4},{8,9},{9,10},{10,1... | collective-permute-start | bytes 1916936 | tf_op jit(solution)/shard_map/ppermute | solution.py:47
  88.5 15.0 %collective-permute-start.3 = (bf16[104,3072]{1,0:T(8,128)(2,1)S(1)}, bf16[104,3072]{1,0:T(8,128)(2,1)S(1)}, u32[]{:S(2)}, u32[]{:S(2)}) collective-permute-start(bf16[104,3072]{1,0:T(8,128)(2,1)S(1)} %multiply_convert_fusion), channel_id=1, source_target_pairs={{0,3},{1,0},{2,1},{3,2},{4,7},{5,4},{6,5},{7,6},{8,11},{9,8},{10,9... | collective-permute-start | bytes 1916936 | tf_op jit(solution)/shard_map/ppermute | solution.py:47
  101.6 10.3 %collective-permute-start.6 = (bf16[104,1536]{1,0:T(8,128)(2,1)S(1)}, bf16[104,1536]{1,0:T(8,128)(2,1)S(1)}, u32[]{:S(2)}, u32[]{:S(2)}) collective-permute-start(bf16[104,1536]{1,0:T(8,128)(2,1)S(1)} %slice.33), channel_id=1, source_target_pairs={{0,1},{1,2},{2,3},{3,0},{4,5},{5,6},{6,7},{7,4},{8,9},{9,10},{10,1... | collective-permute-start | bytes 958472 | tf_op jit(solution)/shard_map/ppermute | solution.py:47
  103.6 10.1 %collective-permute-start.4 = (bf16[104,1536]{1,0:T(8,128)(2,1)S(1)}, bf16[104,1536]{1,0:T(8,128)(2,1)S(1)}, u32[]{:S(2)}, u32[]{:S(2)}) collective-permute-start(bf16[104,1536]{1,0:T(8,128)(2,1)S(1)} %slice.31), channel_id=1, source_target_pairs={{0,3},{1,0},{2,1},{3,2},{4,7},{5,4},{6,5},{7,6},{8,11},{9,8},{10,9... | collective-permute-start | bytes 958472 | tf_op jit(solution)/shard_map/ppermute | solution.py:47
  107.7 4.2 %copy-start.3 = (bf16[3072,768]{1,0:T(8,128)(2,1)S(1)}, bf16[3072,768]{1,0:T(8,128)(2,1)}, u32[]{:S(2)}) copy-start(bf16[3072,768]{1,0:T(8,128)(2,1)} %all-gather.2.cloned.1.call-done) | copy-start | bytes 14155780
  114.3 0.8 copy-start
Sparse Core Ops, SparseCore 0:
  46.2 59.2 all-gather.1

commit v11 on v9

--- a/solution.py
+++ b/solution.py
@@ -21,10 +21,15 @@
         v_heads = values.reshape(tok_rows, HEADS, HEAD_DIM)
         local_state = jnp.einsum("shd,she->hde", k_heads, v_heads, preferred_element_type=jnp.float32)
         state_bf = local_state.astype(jnp.bfloat16)
+        scores = jnp.einsum("thd,shd->hts", q_heads, k_heads, preferred_element_type=jnp.float32)
+        causal = jnp.arange(tok_rows)[:, None] >= jnp.arange(tok_rows)[None, :]
+        scores = jnp.where(causal, scores, 0.0).astype(jnp.bfloat16)
+        intra = jnp.einsum("hts,shd->thd", scores, v_heads, preferred_element_type=jnp.float32)
         prefix_f32 = jnp.zeros(local_state.shape, jnp.float32)
         if n_ctx == 4:
             from_prev = lax.ppermute(state_bf, "ctx", [(0, 1), (1, 2), (2, 3)])
             from_first = lax.ppermute(state_bf, "ctx", [(0, 3)])
+            from_prev, intra = lax.optimization_barrier((from_prev, intra))
             forwarded = lax.ppermute(from_prev, "ctx", [(1, 2), (2, 3)])
             for got in (from_prev, from_first, forwarded):
                 prefix_f32 = prefix_f32 + got.astype(jnp.float32)
@@ -34,10 +39,6 @@
                 prefix_f32 = prefix_f32 + lax.ppermute(state_bf, "ctx", pairs).astype(jnp.float32)
         prefix_state = prefix_f32.astype(jnp.bfloat16)
 
-        scores = jnp.einsum("thd,shd->hts", q_heads, k_heads, preferred_element_type=jnp.float32)
-        causal = jnp.arange(tok_rows)[:, None] >= jnp.arange(tok_rows)[None, :]
-        scores = jnp.where(causal, scores, 0.0).astype(jnp.bfloat16)
-        intra = jnp.einsum("hts,shd->thd", scores, v_heads, preferred_element_type=jnp.float32)
         inter = jnp.einsum("thd,hde->the", q_heads, prefix_state, preferred_element_type=jnp.float32)
         attn = (intra + inter).reshape(tok_rows, HEADS * HEAD_DIM)
         mean_sq = jnp.mean(attn * attn, axis=-1, keepdims=True)

time: 122 us -> 122 us (level)
    ppermute x1, waiting for transfers between devices: 15.2 us -> 11.4 us  [on_device(): from_prev = lax.ppermute(state_bf, 'ctx', [(0, 1), (1, 2), (2, 3)])]
    ppermute x1, waiting for transfers between devices: 10.7 us -> 14.2 us  [on_device(): forwarded = lax.ppermute(from_prev, 'ctx', [(1, 2), (2, 3)])]
  transfers between devices with their start and end apart: 8 -> 8, of which waited for: 3 -> 4; matrix products, arithmetic and copies ran while one was open for 12% -> 12% of each run, Pallas kernels for 0% -> 0%
where the time goes in v11:
time: 122 us; the launch traced here: 120 us
  blocking collectives  39.5 us (32%)
  waiting for transfers between devices  34.8 us (29%)
  starting transfers between devices  15.7 us (13%)
  between operations  13.7 us (11%)
  matrix products  12.4 us (10%)
  local copies, waits for them, and re-layouts  3.69 us (3%)
    all_gather x2, blocking collectives, on_device(): weight_block = lax.all_gather(weight_block, axis, axis=0, tiled=True)  39.5 us
    ppermute x1, waiting for transfers between devices, on_device(): forwarded = lax.ppermute(from_prev, 'ctx', [(1, 2), (2, 3)])  14.2 us
    ppermute x4, starting transfers between devices, shift_by(): return lax.ppermute(x, 'ctx', [(i, (i - s) % n_ctx) for i in range(n_ctx)])  11.9 us
    ppermute x1, waiting for transfers between devices, on_device(): from_prev = lax.ppermute(state_bf, 'ctx', [(0, 1), (1, 2), (2, 3)])  11.4 us
    ppermute x4, waiting for transfers between devices, shift_by(): return lax.ppermute(x, 'ctx', [(i, (i - s) % n_ctx) for i in range(n_ctx)])  8.95 us
    dot_general x1, matrix products, on_device(): jnp.dot(normed, weight_block, preferred_element_type=jnp.float32)  3.33 us
  transfers between devices with their start and end apart: 8, of which 4 were waited for; matrix products, arithmetic and copies ran while one was open for 12% of the time, Pallas kernels for 0%

profile of v11, /device:TPU:6, one launch (start us, length us, event | category | flops | bytes accessed | tf_op | source)
XLA Modules:
  0.0 120.5 jit_solution(8967969023863157693)
XLA Ops:
  6.5 2.2 %all_gather.9 = bf16[32,768]{1,0:T(8,128)(2,1)S(1)} all-gather(bf16[16,768]{1,0:T(8,128)(2,1)} %param.9), channel_id=1, replica_groups=mesh['y'=8,'z'=12,'core'=2,'ctx'=4] {'core'}, dimensions={0}, use_global_device_ids=true | all-gather | bytes 73728 | tf_op jit(solution)/shard_map/all_gather | solution.py:16
  8.7 37.3 %all_gather.10 = bf16[384,768]{1,0:T(8,128)(2,1)} all-gather(bf16[32,768]{1,0:T(8,128)(2,1)S(1)} %all_gather.9), channel_id=1, replica_groups=mesh['y'=8,'z'=12,'core'=2,'ctx'=4] {'z'}, dimensions={0}, use_global_device_ids=true | all-gather | bytes 638976 | tf_op jit(solution)/shard_map/all_gather | solution.py:16
  46.0 0.0 all-gather.2.cloned.1.call-update
  46.1 0.4 copy.25
  46.4 0.4 copy.26
  46.8 1.6 %convolution_convert_fusion = bf16[32,96,96]{2,1,0:T(8,128)(2,1)} fusion(bf16[104,32,96]{0,2,1:T(8,128)(2,1)S(1)} %bitcast.25, bf16[104,32,96]{0,2,1:T(8,128)(2,1)S(1)} %bitcast.27), kind=kOutput, calls=%fused_computation.9 | convolution fusion | flops 61636608 | bytes 1867776 | tf_op jit(solution)/shard_map/shd,she->hde/dot_general | solution.py:22
  48.4 1.3 %collective-permute-start = (bf16[32,96,96]{2,1,0:T(8,128)(2,1)}, bf16[32,96,96]{2,1,0:T(8,128)(2,1)S(1)}, u32[]{:S(2)}, u32[]{:S(2)}) collective-permute-start(bf16[32,96,96]{2,1,0:T(8,128)(2,1)} %convolution_convert_fusion), channel_id=1, source_target_pairs={{0,1},{1,2},{2,3},{4,5},{5,6},{6,7},{8,9},{9,10},{10,11},{12,13},{... | collective-permute-start | bytes 1769480 | tf_op jit(solution)/shard_map/ppermute | solution.py:30
  49.7 1.3 %collective-permute-start.1 = (bf16[32,96,96]{2,1,0:T(8,128)(2,1)}, bf16[32,96,96]{2,1,0:T(8,128)(2,1)}, u32[]{:S(2)}, u32[]{:S(2)}) collective-permute-start(bf16[32,96,96]{2,1,0:T(8,128)(2,1)} %convolution_convert_fusion), channel_id=1, source_target_pairs={{0,3},{4,7},{8,11},{12,15},{16,19},{20,23},{24,27},{28,31},{32,35}... | collective-permute-start | bytes 1769480 | tf_op jit(solution)/shard_map/ppermute | solution.py:31
  51.0 1.5 %copy.27 = bf16[104,3072]{0,1:T(8,128)(2,1)S(1)} copy(bf16[104,3072]{1,0:T(8,128)(2,1)} %param.5) | data formatting | bytes 1277952 | tf_op jit(solution)/shard_map/reshape | solution.py:19
  52.5 2.4 %convolution_bitcast_fusion = f32[104,32,96]{0,2,1:T(8,128)} fusion(bf16[104,32,96]{0,2,1:T(8,128)(2,1)S(1)} %bitcast.28, bf16[104,32,96]{0,2,1:T(8,128)(2,1)S(1)} %bitcast.23, bf16[104,32,96]{0,2,1:T(8,128)(2,1)S(1)} %bitcast.26, pred[104,104]{1,0:T(8,128)(4,1)S(1)} %iota_compare_fusion), kind=kOutput, calls=%fused_computation.8 | convolution fusion | flops 133599232 | bytes 3205696 | tf_op jit(solution)/shard_map/hts,shd->thd/dot_general | solution.py:27
  54.8 11.4 %collective-permute-done = bf16[32,96,96]{2,1,0:T(8,128)(2,1)S(1)} collective-permute-done((bf16[32,96,96]{2,1,0:T(8,128)(2,1)}, bf16[32,96,96]{2,1,0:T(8,128)(2,1)S(1)}, u32[]{:S(2)}, u32[]{:S(2)}) %collective-permute-start) | collective-permute-done | bytes 589856 | tf_op jit(solution)/shard_map/ppermute | solution.py:30
  66.2 1.3 %collective-permute-start.2 = (bf16[32,96,96]{2,1,0:T(8,128)(2,1)S(1)}, bf16[32,96,96]{2,1,0:T(8,128)(2,1)S(1)}, u32[]{:S(2)}, u32[]{:S(2)}) collective-permute-start(bf16[32,96,96]{2,1,0:T(8,128)(2,1)S(1)} %collective-permute-done), channel_id=1, source_target_pairs={{1,2},{2,3},{5,6},{6,7},{9,10},{10,11},{13,14},{14,15},{17,18},{18... | collective-permute-start | bytes 1769480 | tf_op jit(solution)/shard_map/ppermute | solution.py:33
  67.5 0.2 collective-permute-done.1
  67.7 14.2 %collective-permute-done.2 = bf16[32,96,96]{2,1,0:T(8,128)(2,1)S(1)} collective-permute-done((bf16[32,96,96]{2,1,0:T(8,128)(2,1)S(1)}, bf16[32,96,96]{2,1,0:T(8,128)(2,1)S(1)}, u32[]{:S(2)}, u32[]{:S(2)}) %collective-permute-start.2) | collective-permute-done | bytes 589856 | tf_op jit(solution)/shard_map/ppermute | solution.py:33
  82.0 1.7 %fusion.18 = f32[32,96,104]{2,1,0:T(8,128)S(1)} fusion(bf16[104,32,96]{0,2,1:T(8,128)(2,1)S(1)} %bitcast.24, bf16[32,96,96]{2,1,0:T(8,128)(2,1)S(1)} %collective-permute-done.2, bf16[32,96,96]{2,1,0:T(8,128)(2,1)} %collective-permute-done.1, bf16[32,96,96]{2,1,0:T(8,128)(2,1)S(1)} %collective-permute-done), kind=kOutput, calls=%fused_computation.22 | convolution fusion | flops 63111168 | bytes 3686400 | tf_op jit(solution)/shard_map/thd,hde->the/dot_general | solution.py:42
  83.7 0.5 multiply_reduce_fusion
  84.1 0.5 copy.23
  84.6 0.2 copy-done.5
  84.8 0.2 multiply_convert_fusion
  85.0 1.9 %collective-permute-start.4 = (bf16[104,3072]{1,0:T(8,128)(2,1)S(1)}, bf16[104,3072]{1,0:T(8,128)(2,1)S(1)}, u32[]{:S(2)}, u32[]{:S(2)}) collective-permute-start(bf16[104,3072]{1,0:T(8,128)(2,1)S(1)} %multiply_convert_fusion), channel_id=1, source_target_pairs={{0,1},{1,2},{2,3},{3,0},{4,5},{5,6},{6,7},{7,4},{8,9},{9,10},{10,1... | collective-permute-start | bytes 1916936 | tf_op jit(solution)/shard_map/ppermute | solution.py:48
  87.0 3.9 %collective-permute-start.3 = (bf16[104,3072]{1,0:T(8,128)(2,1)S(1)}, bf16[104,3072]{1,0:T(8,128)(2,1)S(1)}, u32[]{:S(2)}, u32[]{:S(2)}) collective-permute-start(bf16[104,3072]{1,0:T(8,128)(2,1)S(1)} %multiply_convert_fusion), channel_id=1, source_target_pairs={{0,3},{1,0},{2,1},{3,2},{4,7},{5,4},{6,5},{7,6},{8,11},{9,8},{10,9... | collective-permute-start | bytes 1916936 | tf_op jit(solution)/shard_map/ppermute | solution.py:48
  90.9 8.9 %collective-permute-done.4 = bf16[104,3072]{1,0:T(8,128)(2,1)S(1)} collective-permute-done((bf16[104,3072]{1,0:T(8,128)(2,1)S(1)}, bf16[104,3072]{1,0:T(8,128)(2,1)S(1)}, u32[]{:S(2)}, u32[]{:S(2)}) %collective-permute-start.4) | collective-permute-done | bytes 639008 | tf_op jit(solution)/shard_map/ppermute | solution.py:48
  99.9 1.9 %collective-permute-start.6 = (bf16[104,1536]{1,0:T(8,128)(2,1)S(1)}, bf16[104,1536]{1,0:T(8,128)(2,1)S(1)}, u32[]{:S(2)}, u32[]{:S(2)}) collective-permute-start(bf16[104,1536]{1,0:T(8,128)(2,1)S(1)} %slice.18), channel_id=1, source_target_pairs={{0,1},{1,2},{2,3},{3,0},{4,5},{5,6},{6,7},{7,4},{8,9},{9,10},{10,1... | collective-permute-start | bytes 958472 | tf_op jit(solution)/shard_map/ppermute | solution.py:48
  101.9 4.1 %collective-permute-start.5 = (bf16[104,1536]{1,0:T(8,128)(2,1)S(1)}, bf16[104,1536]{1,0:T(8,128)(2,1)S(1)}, u32[]{:S(2)}, u32[]{:S(2)}) collective-permute-start(bf16[104,1536]{1,0:T(8,128)(2,1)S(1)} %slice.16), channel_id=1, source_target_pairs={{0,3},{1,0},{2,1},{3,2},{4,7},{5,4},{6,5},{7,6},{8,11},{9,8},{10,9... | collective-permute-start | bytes 958472 | tf_op jit(solution)/shard_map/ppermute | solution.py:48
  106.0 0.0 all-gather.2.cloned.1.call-done
  106.1 3.3 %fusion.15 = bf16[416,768]{1,0:T(8,128)(2,1)S(1)} fusion(bf16[416,768]{1,0:T(8,128)(2,1)S(1)} %broadcast_in_dim.15, s32[]{:T(128)S(6)} %select_n.37, bf16[104,3072]{1,0:T(8,128)(2,1)S(1)} %multiply_convert_fusion, bf16[3072,768]{1,0:T(8,128)(2,1)} %all-gather.2.cloned.1.call-done), kind=kOutput, calls=%fused_computation.19 | convolution fusion | flops 490813440 | bytes 5517316 | tf_op jit(solution)/shard_map/dot_general | solution.py:59
  109.4 0.4 copy-done
  109.8 0.9 fusion.14
  110.7 0.9 fusion.13
  111.6 0.5 fusion
  112.1 0.3 copy-done.2
  112.4 1.2 fusion.10
  (18 shorter events, 0.1 us)
Async XLA Ops:
  6.5 39.5 %copy-start.3 = (bf16[104,3072]{1,0:T(8,128)(2,1)S(1)}, bf16[104,3072]{1,0:T(8,128)(2,1)}, u32[]{:S(2)}) copy-start(bf16[104,3072]{1,0:T(8,128)(2,1)} %param.6) | copy-start | bytes 1916932
  6.5 39.9 %copy-start.4 = (bf16[104,3072]{1,0:T(8,128)(2,1)S(1)}, bf16[104,3072]{1,0:T(8,128)(2,1)}, u32[]{:S(2)}) copy-start(bf16[104,3072]{1,0:T(8,128)(2,1)} %param.7) | copy-start | bytes 1916932
  6.5 99.5 %all-gather.2.cloned.1.call-start = ((), (), s32[]{:S(2)}) async-start(), calls=%async_computation | async-start | bytes 5308416 | tf_op jit(solution)/shard_map/all_gather | solution.py:16
  48.4 17.8 %collective-permute-start = (bf16[32,96,96]{2,1,0:T(8,128)(2,1)}, bf16[32,96,96]{2,1,0:T(8,128)(2,1)S(1)}, u32[]{:S(2)}, u32[]{:S(2)}) collective-permute-start(bf16[32,96,96]{2,1,0:T(8,128)(2,1)} %convolution_convert_fusion), channel_id=1, source_target_pairs={{0,1},{1,2},{2,3},{4,5},{5,6},{6,7},{8,9},{9,10},{10,11},{12,13},{... | collective-permute-start | bytes 1769480 | tf_op jit(solution)/shard_map/ppermute | solution.py:30
  49.7 18.0 %collective-permute-start.1 = (bf16[32,96,96]{2,1,0:T(8,128)(2,1)}, bf16[32,96,96]{2,1,0:T(8,128)(2,1)}, u32[]{:S(2)}, u32[]{:S(2)}) collective-permute-start(bf16[32,96,96]{2,1,0:T(8,128)(2,1)} %convolution_convert_fusion), channel_id=1, source_target_pairs={{0,3},{4,7},{8,11},{12,15},{16,19},{20,23},{24,27},{28,31},{32,35}... | collective-permute-start | bytes 1769480 | tf_op jit(solution)/shard_map/ppermute | solution.py:31
  54.8 28.8 %copy-start.1 = (f32[104,32,96]{0,2,1:T(8,128)S(1)}, f32[104,32,96]{0,2,1:T(8,128)}, u32[]{:S(2)}) copy-start(f32[104,32,96]{0,2,1:T(8,128)} %convolution_bitcast_fusion) | copy-start | bytes 3833860
  66.2 15.8 %collective-permute-start.2 = (bf16[32,96,96]{2,1,0:T(8,128)(2,1)S(1)}, bf16[32,96,96]{2,1,0:T(8,128)(2,1)S(1)}, u32[]{:S(2)}, u32[]{:S(2)}) collective-permute-start(bf16[32,96,96]{2,1,0:T(8,128)(2,1)S(1)} %collective-permute-done), channel_id=1, source_target_pairs={{1,2},{2,3},{5,6},{6,7},{9,10},{10,11},{13,14},{14,15},{17,18},{18... | collective-permute-start | bytes 1769480 | tf_op jit(solution)/shard_map/ppermute | solution.py:33
  84.1 0.7 copy-start.5
  85.0 14.9 %collective-permute-start.4 = (bf16[104,3072]{1,0:T(8,128)(2,1)S(1)}, bf16[104,3072]{1,0:T(8,128)(2,1)S(1)}, u32[]{:S(2)}, u32[]{:S(2)}) collective-permute-start(bf16[104,3072]{1,0:T(8,128)(2,1)S(1)} %multiply_convert_fusion), channel_id=1, source_target_pairs={{0,1},{1,2},{2,3},{3,0},{4,5},{5,6},{6,7},{7,4},{8,9},{9,10},{10,1... | collective-permute-start | bytes 1916936 | tf_op jit(solution)/shard_map/ppermute | solution.py:48
  87.0 14.9 %collective-permute-start.3 = (bf16[104,3072]{1,0:T(8,128)(2,1)S(1)}, bf16[104,3072]{1,0:T(8,128)(2,1)S(1)}, u32[]{:S(2)}, u32[]{:S(2)}) collective-permute-start(bf16[104,3072]{1,0:T(8,128)(2,1)S(1)} %multiply_convert_fusion), channel_id=1, source_target_pairs={{0,3},{1,0},{2,1},{3,2},{4,7},{5,4},{6,5},{7,6},{8,11},{9,8},{10,9... | collective-permute-start | bytes 1916936 | tf_op jit(solution)/shard_map/ppermute | solution.py:48
  99.9 11.7 %collective-permute-start.6 = (bf16[104,1536]{1,0:T(8,128)(2,1)S(1)}, bf16[104,1536]{1,0:T(8,128)(2,1)S(1)}, u32[]{:S(2)}, u32[]{:S(2)}) collective-permute-start(bf16[104,1536]{1,0:T(8,128)(2,1)S(1)} %slice.18), channel_id=1, source_target_pairs={{0,1},{1,2},{2,3},{3,0},{4,5},{5,6},{6,7},{7,4},{8,9},{9,10},{10,1... | collective-permute-start | bytes 958472 | tf_op jit(solution)/shard_map/ppermute | solution.py:48
  101.9 10.3 %collective-permute-start.5 = (bf16[104,1536]{1,0:T(8,128)(2,1)S(1)}, bf16[104,1536]{1,0:T(8,128)(2,1)S(1)}, u32[]{:S(2)}, u32[]{:S(2)}) collective-permute-start(bf16[104,1536]{1,0:T(8,128)(2,1)S(1)} %slice.16), channel_id=1, source_target_pairs={{0,3},{1,0},{2,1},{3,2},{4,7},{5,4},{6,5},{7,6},{8,11},{9,8},{10,9... | collective-permute-start | bytes 958472 | tf_op jit(solution)/shard_map/ppermute | solution.py:48
  106.1 3.8 %copy-start = (bf16[3072,768]{1,0:T(8,128)(2,1)S(1)}, bf16[3072,768]{1,0:T(8,128)(2,1)}, u32[]{:S(2)}) copy-start(bf16[3072,768]{1,0:T(8,128)(2,1)} %all-gather.2.cloned.1.call-done) | copy-start | bytes 14155780
  111.6 0.8 copy-start.2
Sparse Core Ops, SparseCore 0:
  46.2 59.2 all-gather.1
